TPU v7x, 512 devices: a whole 4x8x8 slice. The times are simulated.
512 devices in a mesh: space: 32 (over x, y_hi, core), tm: 16 (over z, y_lo).
Axes of the slice: x: 4, y: 8 (y_hi: 4, y_lo: 2; y = y_hi * 2 + y_lo), z: 8, core: 2. Of those that a mesh axis runs over, the one named last changes fastest.
Arguments:
- field: float32 [256, 32768], P('tm', 'space'), may hold values from -6 to 6
- momentum: float32 [256, 32768], P('tm', 'space'), may hold values from -6 to 6
- solution: float32 [256, 32768], P('tm', 'space'), may hold values from -6 to 6
- tiles: float32 [256, 6, 128, 128], P('space'), may hold values from -1 to 2
- columns: int32 [256, 6], P('space'), may hold values from 0 to 255, as said below
- neighbours: int32 [3, 32768], P(None, 'space'), may hold values from 0 to 32767, as said below
Outputs:
- field_out: float32 [256, 32768], P('tm', 'space')
- momentum_out: float32 [256, 32768], P('tm', 'space')
- fermion_force: float32 [256, 32768], P('tm', 'space')
Inputs may be any that keep to these rules, and one draw needn't show every extreme that they name: Row r lists 6 different tile columns, the first of them r itself; the others lie outside the run of 8 tile rows that holds r (runs r // 8), and the rows of one run name at most 2 columns of any other run, exactly 2 for some run. The neighbour relation is symmetric, each site has three different neighbours, and each neighbour lies in the site's own run of 128 labels or in the run just before or after it, cyclically over the flake.
All inputs are finite; a program needn't handle non-finite values.
Results may differ from a plain program's by a relative error of at most 0.00014.
Values sent between devices are 32-bit elements; how exact they have to be, the bound alone decides.
No kernel may reach another device: no remote copies, remote signals or barrier semaphores. Data moves between devices by JAX's collectives and lax.ppermute only.
A program may use at most 64 MiB of HBM per device.

v0:
```python
import jax
import jax.numpy as jnp
from jax import lax
from jax.sharding import PartitionSpec as P

TILE = 128


step_size = 0.5
hop_kappa = 0.5
coupling = 0.25


def with_halo(block, sides, width):
    for axis, dim in sides:
        count = lax.axis_size(axis)
        forward = [(i, i + 1) for i in range(count - 1)]
        forward.append((count - 1, 0))
        backward = [(target, source) for source, target in forward]
        low = lax.ppermute(
            lax.slice_in_dim(block, block.shape[dim] - width, None, axis=dim), axis, forward
        )
        high = lax.ppermute(lax.slice_in_dim(block, 0, width, axis=dim), axis, backward)
        block = jnp.concatenate([low, block, high], axis=dim)
    return block


def from_behind(value, axis, steps):
    count = lax.axis_size(axis)
    pairs = [(source, (source + steps) % count) for source in range(count)]
    return lax.ppermute(value, axis, pairs)


def body(field, momentum, solution, tiles, columns, neighbours):
    slices = field.shape[0]
    tile_rows = tiles.shape[0]
    kept = tiles.shape[1]
    site_count = field.shape[1]
    cols_flat = columns.reshape(-1)
    space_count = lax.axis_size("space")

    def coulomb(values):
        gathered = lax.all_gather(values, "space", axis=1, tiled=True)
        blocks = gathered.reshape(slices, -1, TILE)
        picked = jnp.take(blocks, cols_flat, axis=1).reshape(slices, tile_rows, kept, TILE)
        mixed = jnp.einsum("rkij,trkj->tri", tiles, picked, precision=lax.Precision.HIGHEST)
        return mixed.reshape(slices, site_count)

    moment = momentum - 0.5 * step_size * coulomb(field)
    field_one = field + step_size * moment
    moment = moment - step_size * coulomb(field_one)
    field_two = field_one + step_size * moment
    moment = moment - 0.5 * step_size * coulomb(field_two)
    total_sites = site_count * space_count
    first_site = lax.axis_index("space") * site_count
    lookup = (neighbours - first_site + TILE) % total_sites
    parity_sign = jnp.where(lax.axis_index("tm") == 0, -1.0, 1.0).astype(jnp.float32)
    widened = with_halo(solution, (("space", 1),), TILE)
    beside = jnp.take(widened, lookup.reshape(-1), axis=1).reshape(solution.shape[0], 3, site_count)
    hopped = solution + hop_kappa * (beside[:, 0] + beside[:, 1] + beside[:, 2])
    arrived = from_behind(hopped[-1:], "tm", 1)
    earlier = jnp.concatenate([parity_sign * arrived, hopped[:-1]], axis=0)
    link_factor = jnp.exp(coupling * field_two)
    shifted = solution - link_factor * earlier
    force = 2.0 * coupling * shifted * link_factor * earlier
    return (field_two, moment, force)


def solution(mesh):
    in_specs = (
        P("tm", "space"),
        P("tm", "space"),
        P("tm", "space"),
        P("space", None, None, None),
        P("space", None),
        P(None, "space"),
    )
    out_specs = (P("tm", "space"), P("tm", "space"), P("tm", "space"))
    return jax.shard_map(body, mesh=mesh, in_specs=in_specs, out_specs=out_specs, check_vma=False)
```

profile of v0, /device:TPU:1, one launch (start us, length us, event | category | flops | bytes accessed | tf_op | source)
XLA Modules:
  0.0 224.8 jit_solution(11539361856187728963)
XLA Ops:
  7.2 0.0 copy-start
  7.2 0.0 all-gather.4.cloned.1.call-start
  7.2 0.7 all-gather.4.cloned.1.call-update
  7.9 0.0 all-gather.6.cloned.1.call-start
  8.0 0.9 reshape.89
  8.9 67.8 %all-gather.4.cloned.1.call-done = f32[16,32768]{1,0:T(8,128)} async-done(((f32[16,1024]{1,0:T(8,128)}), f32[16,32768]{1,0:T(8,128)}) %all-gather.4.cloned.1.call-update) | async-done | bytes 2097168 | tf_op jit(solution)/shard_map/all_gather | solution.py:43
  76.7 3.1 %copy_bitcast_fusion.2 = f32[16,256,128]{2,0,1:T(8,128)} fusion(f32[16,32768]{1,0:T(8,128)} %all-gather.4.cloned.1.call-done), kind=kLoop, calls=%fused_computation.6 | loop fusion | bytes 4194304 | tf_op jit(solution)/shard_map/reshape | solution.py:44
  79.8 2.2 gather_fusion.1
  82.0 0.0 copy-start.8
  82.0 0.0 copy-start.14
  82.0 0.1 broadcast_select_fusion.2
  82.1 0.0 copy-start.4
  82.1 0.0 copy-start.15
  82.2 0.0 copy-done
  82.2 2.7 %fusion.5 = f32[8,2,8,128]{3,2,1,0:T(8,128)S(1)} fusion(f32[16,8,6,128]{3,0,2,1:T(8,128)S(1)} %bitcast.95, f32[8,6,128,128]{3,2,1,0:T(8,128)S(1)} %copy-done), kind=kOutput, calls=%fused_computation.15 | convolution fusion | flops 151011328 | bytes 3604480 | tf_op jit(solution)/shard_map/rkij,trkj->tri/dot_general | solution.py:46
  84.9 0.6 copy-done.1
  85.5 0.0 copy-done.8
  85.5 0.0 copy-done.14
  85.5 0.6 multiply_add_fusion.1
  86.2 0.0 all-gather.6.cloned.1.call-update
  86.2 0.0 all-gather.8.cloned.1.call-start
  86.3 0.0 copy-done.4
  86.3 3.0 %collective-permute-start = (f32[16,128]{1,0:T(8,128)S(1)}, f32[16,128]{1,0:T(8,128)S(1)}, u32[]{:S(2)}, u32[]{:S(2)}) collective-permute-start(f32[16,128]{1,0:T(8,128)S(1)} %get-tuple-element.8), channel_id=1, source_target_pairs={{0,16},{16,32},{32,48},{48,64},{64,80},{80,96},{96,112},{112,128},... | collective-permute-start | bytes 24584 | tf_op jit(solution)/shard_map/ppermute | solution.py:20
  89.3 1.9 collective-permute-start.1
  91.2 0.0 copy-done.15
  91.3 0.0 collective-permute-done
  91.3 4.0 %collective-permute-done.1 = f32[16,128]{1,0:T(8,128)S(1)} collective-permute-done((f32[16,128]{1,0:T(8,128)S(1)}, f32[16,128]{1,0:T(8,128)S(1)}, u32[]{:S(2)}, u32[]{:S(2)}) %collective-permute-start.1) | collective-permute-done | bytes 8224 | tf_op jit(solution)/shard_map/ppermute | solution.py:23
  95.3 1.1 copy.39
  96.4 12.0 %gather_fusion = f32[3072,16]{1,0:T(8,128)} fusion(f32[16,1280]{0,1:T(8,128)} %copy.39, s32[3072]{0:T(1024)S(1)} %broadcast_clamp_fusion), kind=kCustom, calls=%fused_computation.3 | custom fusion | bytes 405504 | tf_op jit(solution)/shard_map/jit(_take)/gather | solution.py:59
  108.4 1.8 copy.40
  110.3 0.0 copy-start.12
  110.3 0.6 copy-done.12
  110.9 2.7 %collective-permute-start.2 = (f32[1,1024]{1,0:T(1,128)S(1)}, f32[1,1024]{1,0:T(1,128)S(1)}, u32[]{:S(2)}, u32[]{:S(2)}) collective-permute-start(f32[1,1024]{1,0:T(1,128)S(1)} %slice.39), channel_id=1, source_target_pairs={{0,1},{1,2},{2,3},{3,4},{4,5},{5,6},{6,7},{7,8},{8,9},{9,10},{10,1... | collective-permute-start | bytes 12296 | tf_op jit(solution)/shard_map/ppermute | solution.py:31
  113.6 4.4 %collective-permute-done.2 = f32[1,1024]{1,0:T(1,128)S(1)} collective-permute-done((f32[1,1024]{1,0:T(1,128)S(1)}, f32[1,1024]{1,0:T(1,128)S(1)}, u32[]{:S(2)}, u32[]{:S(2)}) %collective-permute-start.2) | collective-permute-done | bytes 4128 | tf_op jit(solution)/shard_map/ppermute | solution.py:31
  118.0 25.4 %all-gather.6.cloned.1.call-done = f32[16,32768]{1,0:T(8,128)} async-done(((f32[16,1024]{1,0:T(8,128)}), f32[16,32768]{1,0:T(8,128)}) %all-gather.6.cloned.1.call-update) | async-done | bytes 2097168 | tf_op jit(solution)/shard_map/all_gather | solution.py:43
  143.4 3.1 %copy_bitcast_fusion.1 = f32[16,256,128]{2,0,1:T(8,128)} fusion(f32[16,32768]{1,0:T(8,128)} %all-gather.6.cloned.1.call-done), kind=kLoop, calls=%fused_computation.5 | loop fusion | bytes 4194304 | tf_op jit(solution)/shard_map/reshape | solution.py:44
  146.5 2.2 gather_fusion.2
  148.6 0.0 copy-start.2
  148.6 0.0 copy-start.5
  148.7 0.0 copy-start.9
  148.7 0.0 copy-start.11
  148.7 0.0 copy-start.13
  148.7 0.1 broadcast_select_fusion.1
  148.8 2.7 %fusion.3 = f32[8,2,8,128]{3,2,1,0:T(8,128)S(1)} fusion(f32[16,8,6,128]{3,0,2,1:T(8,128)S(1)} %bitcast.96, f32[8,6,128,128]{3,2,1,0:T(8,128)S(1)} %copy-done), kind=kOutput, calls=%fused_computation.12 | convolution fusion | flops 151011328 | bytes 3604480 | tf_op jit(solution)/shard_map/rkij,trkj->tri/dot_general | solution.py:46
  151.5 0.0 copy-done.2
  151.6 0.0 copy-done.5
  151.6 0.0 copy-done.9
  151.6 0.0 copy-done.11
  151.6 0.0 copy-done.13
  151.6 0.7 multiply_multiply_fusion
  152.3 0.0 copy-done.6
  152.3 0.0 all-gather.8.cloned.1.call-update
  152.3 57.2 %all-gather.8.cloned.1.call-done = f32[16,32768]{1,0:T(8,128)} async-done(((f32[16,1024]{1,0:T(8,128)}), f32[16,32768]{1,0:T(8,128)}) %all-gather.8.cloned.1.call-update) | async-done | bytes 2097168 | tf_op jit(solution)/shard_map/all_gather | solution.py:43
  209.5 3.1 %copy_bitcast_fusion = f32[16,256,128]{2,0,1:T(8,128)} fusion(f32[16,32768]{1,0:T(8,128)} %all-gather.8.cloned.1.call-done), kind=kLoop, calls=%fused_computation.4 | loop fusion | bytes 4194304 | tf_op jit(solution)/shard_map/reshape | solution.py:44
  212.6 2.2 gather_fusion.3
  214.7 0.0 copy-start.3
  214.8 0.0 copy-start.7
  214.8 0.0 copy-start.10
  214.8 0.1 broadcast_select_fusion
  214.9 2.7 %fusion.1 = f32[8,2,8,128]{3,2,1,0:T(8,128)S(1)} fusion(f32[16,8,6,128]{3,0,2,1:T(8,128)S(1)} %bitcast.94, f32[8,6,128,128]{3,2,1,0:T(8,128)S(1)} %copy-done), kind=kOutput, calls=%fused_computation.9 | convolution fusion | flops 151011328 | bytes 3604480 | tf_op jit(solution)/shard_map/rkij,trkj->tri/dot_general | solution.py:46
  217.6 0.0 copy-done.3
  217.6 0.0 copy-done.7
  217.7 0.0 copy-done.10
  217.7 0.6 bitcast_subtract_fusion
  (15 shorter events, 0.2 us)
Async XLA Ops:
  7.2 75.0 %copy-start = (f32[8,6,128,128]{3,2,1,0:T(8,128)S(1)}, f32[8,6,128,128]{3,2,1,0:T(8,128)}, u32[]{:S(2)}) copy-start(f32[8,6,128,128]{3,2,1,0:T(8,128)} %param.11) | copy-start | bytes 9437188
  7.2 69.6 %all-gather.4.cloned.1.call-start = ((), (), s32[]{:S(2)}) async-start(), calls=%async_computation | async-start | bytes 2162688 | tf_op jit(solution)/shard_map/all_gather | solution.py:43
  7.9 135.5 %all-gather.6.cloned.1.call-start = ((), (), s32[]{:S(2)}) async-start(), calls=%async_computation.1 | async-start | bytes 2162688 | tf_op jit(solution)/shard_map/all_gather | solution.py:43
  82.0 3.6 %copy-start.8 = (f32[16,1024]{1,0:T(8,128)S(1)}, f32[16,1024]{1,0:T(8,128)}, u32[]{:S(2)}) copy-start(f32[16,1024]{1,0:T(8,128)} %param.9) | copy-start | bytes 196612
  82.0 3.6 %copy-start.14 = (f32[16,1024]{1,0:T(8,128)S(1)}, f32[16,1024]{1,0:T(8,128)}, u32[]{:S(2)}) copy-start(f32[16,1024]{1,0:T(8,128)} %param.8) | copy-start | bytes 196612
  82.1 4.1 %copy-start.4 = (f32[16,1024]{1,0:T(8,128)S(1)}, f32[16,1024]{1,0:T(8,128)}, u32[]{:S(2)}) copy-start(f32[16,1024]{1,0:T(8,128)} %param.10) | copy-start | bytes 196612
  82.1 9.1 %copy-start.15 = (s32[3,1024]{1,0:T(4,128)S(1)}, s32[3,1024]{1,0:T(4,128)}, u32[]{:S(2)}) copy-start(s32[3,1024]{1,0:T(4,128)} %param.13) | copy-start | bytes 36868
  84.9 0.6 copy-start.1
  86.2 123.3 %all-gather.8.cloned.1.call-start = ((), (), s32[]{:S(2)}) async-start(), calls=%async_computation.2 | async-start | bytes 2162688 | tf_op jit(solution)/shard_map/all_gather | solution.py:43
  86.3 5.0 %collective-permute-start = (f32[16,128]{1,0:T(8,128)S(1)}, f32[16,128]{1,0:T(8,128)S(1)}, u32[]{:S(2)}, u32[]{:S(2)}) collective-permute-start(f32[16,128]{1,0:T(8,128)S(1)} %get-tuple-element.8), channel_id=1, source_target_pairs={{0,16},{16,32},{32,48},{48,64},{64,80},{80,96},{96,112},{112,128},... | collective-permute-start | bytes 24584 | tf_op jit(solution)/shard_map/ppermute | solution.py:20
  89.3 6.1 %collective-permute-start.1 = (f32[16,128]{1,0:T(8,128)S(1)}, f32[16,128]{1,0:T(8,128)S(1)}, u32[]{:S(2)}, u32[]{:S(2)}) collective-permute-start(f32[16,128]{1,0:T(8,128)S(1)} %get-tuple-element.9), channel_id=1, source_target_pairs={{16,0},{32,16},{48,32},{64,48},{80,64},{96,80},{112,96},{128,112},... | collective-permute-start | bytes 24584 | tf_op jit(solution)/shard_map/ppermute | solution.py:23
  110.3 0.6 copy-start.12
  110.9 7.0 %collective-permute-start.2 = (f32[1,1024]{1,0:T(1,128)S(1)}, f32[1,1024]{1,0:T(1,128)S(1)}, u32[]{:S(2)}, u32[]{:S(2)}) collective-permute-start(f32[1,1024]{1,0:T(1,128)S(1)} %slice.39), channel_id=1, source_target_pairs={{0,1},{1,2},{2,3},{3,4},{4,5},{5,6},{6,7},{7,8},{8,9},{9,10},{10,1... | collective-permute-start | bytes 12296 | tf_op jit(solution)/shard_map/ppermute | solution.py:31
  148.6 2.9 %copy-start.2 = (f32[8,2,8,128]{3,2,1,0:T(8,128)S(1)}, f32[8,2,8,128]{3,2,1,0:T(8,128)}, u32[]{:S(2)}) copy-start(f32[8,2,8,128]{3,2,1,0:T(8,128)} %copy-done.1) | copy-start | bytes 196612
  148.6 2.9 %copy-start.5 = (f32[16,1024]{1,0:T(8,128)S(1)}, f32[16,1024]{1,0:T(8,128)}, u32[]{:S(2)}) copy-start(f32[16,1024]{1,0:T(8,128)} %param.10) | copy-start | bytes 196612
  148.7 2.9 %copy-start.9 = (f32[16,1024]{1,0:T(8,128)S(1)}, f32[16,1024]{1,0:T(8,128)}, u32[]{:S(2)}) copy-start(f32[16,1024]{1,0:T(8,128)} %param.9) | copy-start | bytes 196612
  148.7 2.9 %copy-start.11 = (f32[16,1024]{1,0:T(8,128)S(1)}, f32[16,1024]{1,0:T(8,128)}, u32[]{:S(2)}) copy-start(f32[16,1024]{1,0:T(8,128)} %multiply_add_fusion.1) | copy-start | bytes 196612
  148.7 2.9 %copy-start.13 = (f32[16,1024]{1,0:T(8,128)S(1)}, f32[16,1024]{1,0:T(8,128)}, u32[]{:S(2)}) copy-start(f32[16,1024]{1,0:T(8,128)} %copy-done.12) | copy-start | bytes 196612
  151.5 0.8 copy-start.6
  214.7 2.9 %copy-start.3 = (f32[8,2,8,128]{3,2,1,0:T(8,128)S(1)}, f32[8,2,8,128]{3,2,1,0:T(8,128)}, u32[]{:S(2)}) copy-start(f32[8,2,8,128]{3,2,1,0:T(8,128)} %copy-done.1) | copy-start | bytes 196612
  214.8 2.9 %copy-start.7 = (f32[8,2,8,128]{3,2,1,0:T(8,128)S(1)}, f32[8,2,8,128]{3,2,1,0:T(8,128)}, u32[]{:S(2)}) copy-start(f32[8,2,8,128]{3,2,1,0:T(8,128)} %copy-done.6) | copy-start | bytes 196612
  214.8 2.9 %copy-start.10 = (f32[16,1024]{1,0:T(8,128)S(1)}, f32[16,1024]{1,0:T(8,128)}, u32[]{:S(2)}) copy-start(f32[16,1024]{1,0:T(8,128)} %param.9) | copy-start | bytes 196612
Sparse Core Ops, SparseCore 0:
  11.2 65.4 all-gather.3
  86.3 57.0 all-gather.5
  152.5 57.0 all-gather.7
where the time goes:
time: 225 us
  waiting for transfers between devices  160 us (71%)
  local copies, waits for them, and re-layouts  32.9 us (15%)
  between operations  14.1 us (6%)
  matrix products  8.19 us (4%)
  starting transfers between devices  7.67 us (3%)
  other arithmetic  2.47 us (1%)
    all_gather x3, waiting for transfers between devices, coulomb(): gathered = lax.all_gather(values, 'space', axis=1, tiled=True)  150 us
    gather x2, local copies, waits for them, and re-layouts, body(): jnp.take(widened, lookup.reshape(-1), axis=1)  13.8 us
    reshape x3, local copies, waits for them, and re-layouts, coulomb(): blocks = gathered.reshape(slices, -1, TILE)  9.16 us
    dot_general x3, matrix products, coulomb(): jnp.einsum('rkij,trkj->tri', tiles, picked, precision=lax.Precision.HIGHEST)  8.19 us
    gather x3, local copies, waits for them, and re-layouts, coulomb(): jnp.take(blocks, cols_flat, axis=1).reshape(slices, tile_rows, kept, TILE)  6.51 us
  transfers between devices with their start and end apart: 6, of which 5 were waited for; matrix products, arithmetic and copies ran while one was open for 7% of the time, Pallas kernels for 0%

commit v1 on v0

--- a/solution.py
+++ b/solution.py
@@ -36,14 +36,31 @@
     tile_rows = tiles.shape[0]
     kept = tiles.shape[1]
     site_count = field.shape[1]
-    cols_flat = columns.reshape(-1)
     space_count = lax.axis_size("space")
+    me = lax.axis_index("space")
+
+    run_of = columns // tile_rows
+    local_id = columns % tile_rows
+    remote = run_of != me
+    runs = jnp.arange(space_count, dtype=jnp.int32)
+    hit = remote[:, :, None] & (run_of[:, :, None] == runs[None, None, :])
+    lo = jnp.min(jnp.where(hit, local_id[:, :, None], tile_rows), axis=(0, 1))
+    hi = jnp.max(jnp.where(hit, local_id[:, :, None], -1), axis=(0, 1))
+    lo = jnp.clip(lo, 0, tile_rows - 1)
+    hi = jnp.clip(hi, 0, tile_rows - 1)
+    request = jnp.stack([lo, hi], axis=1)
+    wanted = lax.all_to_all(request, "space", 0, 0, tiled=True)
+    send_ids = wanted.reshape(-1)
+    slot = jnp.where(local_id == lo[run_of], 0, 1)
+    pick = jnp.where(remote, tile_rows + run_of * 2 + slot, local_id).reshape(-1)
 
     def coulomb(values):
-        gathered = lax.all_gather(values, "space", axis=1, tiled=True)
-        blocks = gathered.reshape(slices, -1, TILE)
-        picked = jnp.take(blocks, cols_flat, axis=1).reshape(slices, tile_rows, kept, TILE)
-        mixed = jnp.einsum("rkij,trkj->tri", tiles, picked, precision=lax.Precision.HIGHEST)
+        own = values.reshape(slices, tile_rows, TILE).transpose(1, 0, 2)
+        sent = jnp.take(own, send_ids, axis=0)
+        got = lax.all_to_all(sent, "space", 0, 0, tiled=True)
+        pool = jnp.concatenate([own, got], axis=0)
+        picked = jnp.take(pool, pick, axis=0).reshape(tile_rows, kept, slices, TILE)
+        mixed = jnp.einsum("rkij,rktj->tri", tiles, picked, precision=lax.Precision.HIGHEST)
         return mixed.reshape(slices, site_count)
 
     moment = momentum - 0.5 * step_size * coulomb(field)
@@ -51,13 +68,21 @@
     moment = moment - step_size * coulomb(field_one)
     field_two = field_one + step_size * moment
     moment = moment - 0.5 * step_size * coulomb(field_two)
+
     total_sites = site_count * space_count
-    first_site = lax.axis_index("space") * site_count
+    first_site = me * site_count
     lookup = (neighbours - first_site + TILE) % total_sites
     parity_sign = jnp.where(lax.axis_index("tm") == 0, -1.0, 1.0).astype(jnp.float32)
     widened = with_halo(solution, (("space", 1),), TILE)
-    beside = jnp.take(widened, lookup.reshape(-1), axis=1).reshape(solution.shape[0], 3, site_count)
-    hopped = solution + hop_kappa * (beside[:, 0] + beside[:, 1] + beside[:, 2])
+    blocks = site_count // TILE
+    starts = (jnp.arange(blocks, dtype=jnp.int32) * TILE)[:, None, None]
+    offsets = lookup.reshape(3, blocks, TILE).transpose(1, 0, 2) - starts
+    window = jnp.arange(3 * TILE, dtype=jnp.int32)[None, None, :, None]
+    adjacency = jnp.sum((offsets[:, :, None, :] == window).astype(jnp.float32), axis=1)
+    parts = widened.reshape(slices, blocks + 2, TILE)
+    windows = jnp.concatenate([parts[:, :-2], parts[:, 1:-1], parts[:, 2:]], axis=2)
+    beside = jnp.einsum("tbj,bji->tbi", windows, adjacency, precision=lax.Precision.HIGHEST)
+    hopped = solution + hop_kappa * beside.reshape(slices, site_count)
     arrived = from_behind(hopped[-1:], "tm", 1)
     earlier = jnp.concatenate([parity_sign * arrived, hopped[:-1]], axis=0)
     link_factor = jnp.exp(coupling * field_two)

time: 225 us -> 142 us (0.63)
  waiting for transfers between devices: 160 us -> 35.4 us
  blocking collectives: 0 us -> 28.3 us
  starting transfers between devices: 7.67 us -> 30.5 us
  local copies, waits for them, and re-layouts: 32.9 us -> 16.2 us
  other arithmetic: 2.47 us -> 18.3 us
  between operations: 14.1 us -> 1.17 us
  matrix products: 8.19 us -> 10.7 us
    all_gather x3 -> x0, waiting for transfers between devices: 150 us -> none  [coulomb(): gathered = lax.all_gather(values, 'space', axis=1, tiled=True)]
    all_to_all x0 -> x1, blocking collectives: none -> 28.3 us  [coulomb(): got = lax.all_to_all(sent, 'space', 0, 0, tiled=True)]
    all_to_all x0 -> x3, waiting for transfers between devices: none -> 22.6 us  [the longest x2 15.1 us: coulomb(): got = lax.all_to_all(sent, 'space', 0, 0, tiled=True)]
    all_to_all x0 -> x3, starting transfers between devices: none -> 17.9 us  [the longest x2 10 us: coulomb(): got = lax.all_to_all(sent, 'space', 0, 0, tiled=True)]
    reshape x4 -> x3, local copies, waits for them, and re-layouts: 10.1 us -> 0.2 us  [the longest x1 0.1 us: body(): send_ids = wanted.reshape(-1)]
    gather x5 -> x8, local copies, waits for them, and re-layouts: 20.3 us -> 10.7 us  [the longest x3 5.29 us: coulomb(): picked = jnp.take(pool, pick, axis=0).reshape(tile_rows, kept, slices, TILE)]
    ppermute x1, waiting for transfers between devices: 4.36 us -> 12.8 us  [from_behind(): return lax.ppermute(value, axis, pairs)]
    select_n x6 -> x10, other arithmetic: 0.4 us -> 7.55 us  [the longest x4 5.14 us: coulomb(): sent = jnp.take(own, send_ids, axis=0)]
  transfers between devices with their start and end apart: 6 -> 6, of which waited for: 5 -> 4; matrix products, arithmetic and copies ran while one was open for 7% -> 18% of each run, Pallas kernels for 0% -> 0%
where the time goes in v1:
time: 142 us; the launch traced here: 141 us
  waiting for transfers between devices  35.4 us (25%)
  starting transfers between devices  30.5 us (21%)
  blocking collectives  28.3 us (20%)
  other arithmetic  18.3 us (13%)
  local copies, waits for them, and re-layouts  16.2 us (11%)
  matrix products  10.7 us (8%)
    all_to_all x1, blocking collectives, coulomb(): got = lax.all_to_all(sent, 'space', 0, 0, tiled=True)  28.3 us
    all_to_all x2, waiting for transfers between devices, coulomb(): got = lax.all_to_all(sent, 'space', 0, 0, tiled=True)  15.1 us
    ppermute x1, waiting for transfers between devices, from_behind(): return lax.ppermute(value, axis, pairs)  12.8 us
    all_to_all x2, starting transfers between devices, coulomb(): got = lax.all_to_all(sent, 'space', 0, 0, tiled=True)  10 us
    ppermute x1, starting transfers between devices, with_halo(): lax.ppermute(lax.slice_in_dim(block, 0, width, axis=dim), axis, backward)  8.77 us
    dot_general x3, matrix products, coulomb(): jnp.einsum('rkij,rktj->tri', tiles, picked, precision=lax.Precision.HIGHEST)  8.19 us
    all_to_all x1, starting transfers between devices, body(): wanted = lax.all_to_all(request, 'space', 0, 0, tiled=True)  7.9 us
    all_to_all x1, waiting for transfers between devices, body(): wanted = lax.all_to_all(request, 'space', 0, 0, tiled=True)  7.52 us
  transfers between devices with their start and end apart: 6, of which 4 were waited for; matrix products, arithmetic and copies ran while one was open for 18% of the time, Pallas kernels for 0%

profile of v1, /device:TPU:1, one launch (start us, length us, event | category | flops | bytes accessed | tf_op | source)
XLA Modules:
  0.0 140.6 jit_solution(2999100898475018492)
XLA Ops:
  0.6 0.0 copy-start
  0.6 1.5 %fusion.22 = (f32[16,128]{1,0:T(8,128)}, f32[16,128]{1,0:T(8,128)}) fusion(f32[16,1024]{1,0:T(8,128)} %param.12), kind=kLoop, calls=%fused_computation.84 | loop fusion | bytes 32768 | tf_op jit(solution)/shard_map/slice | solution.py:21
  2.1 8.8 %collective-permute-start.1 = (f32[16,128]{1,0:T(8,128)}, f32[16,128]{1,0:T(8,128)S(1)}, u32[]{:S(2)}, u32[]{:S(2)}) collective-permute-start(f32[16,128]{1,0:T(8,128)} %get-tuple-element.15), channel_id=1, source_target_pairs={{16,0},{32,16},{48,32},{64,48},{80,64},{96,80},{112,96},{128,112},... | collective-permute-start | bytes 24584 | tf_op jit(solution)/shard_map/ppermute | solution.py:23
  10.9 1.9 %collective-permute-start = (f32[16,128]{1,0:T(8,128)}, f32[16,128]{1,0:T(8,128)S(1)}, u32[]{:S(2)}, u32[]{:S(2)}) collective-permute-start(f32[16,128]{1,0:T(8,128)} %get-tuple-element.14), channel_id=1, source_target_pairs={{0,16},{16,32},{32,48},{48,64},{64,80},{80,96},{96,112},{112,128},... | collective-permute-start | bytes 24584 | tf_op jit(solution)/shard_map/ppermute | solution.py:20
  12.8 0.7 compare_select_fusion
  13.5 0.1 copy.49
  13.6 0.1 copy.48
  13.7 0.1 copy.47
  13.8 0.1 select_reduce_fusion.1
  13.9 0.7 copy.51
  14.6 7.9 %all-to-all-start = ((s32[32,1,2]{2,1,0:T(1,128)}), s32[32,1,2]{2,1,0:T(1,128)S(1)}, u32[]{:S(2)}, u32[]{:S(2)}) async-start(s32[32,1,2]{2,1,0:T(1,128)} %copy.51), calls=%async_computation | async-start | bytes 32768 | tf_op jit(solution)/shard_map/all_to_all | solution.py:52
  22.6 0.8 bitcast_bitcast_fusion.2
  23.4 0.7 fusion.15
  24.1 0.1 fusion.16
  24.2 0.1 reshape.149
  24.3 7.5 %all-to-all-done = s32[32,1,2]{2,1,0:T(1,128)S(1)} async-done(((s32[32,1,2]{2,1,0:T(1,128)}), s32[32,1,2]{2,1,0:T(1,128)S(1)}, u32[]{:S(2)}, u32[]{:S(2)}) %all-to-all-start) | async-done | bytes 288 | tf_op jit(solution)/shard_map/all_to_all | solution.py:52
  31.8 0.5 broadcast.150
  32.3 0.7 reduce.3
  33.0 0.1 reshape.90
  33.2 1.4 %gather_fusion.1 = f32[64,16,128]{2,1,0:T(8,128)} fusion(f32[8,16,128]{2,1,0:T(8,128)S(1)} %bitcast_bitcast_fusion.2, s32[1024]{0:T(1024)S(1)} %pad_clamp_fusion.1), kind=kCustom, calls=%fused_computation.clone | custom fusion | bytes 1048832 | tf_op jit(solution)/shard_map/jit(_take)/gather | solution.py:59
  34.6 2.0 %broadcast_select_fusion.2 = f32[64,16,128]{2,1,0:T(8,128)} fusion(f32[64,16,128]{2,1,0:T(8,128)} %gather_fusion.1, pred[64]{0:T(512)(128)(4,1)S(1)} %compare_and_fusion.1), kind=kLoop, calls=%fused_computation.25 | loop fusion | flops 131072 | bytes 1048640 | tf_op jit(solution)/shard_map/jit(_take)/select_n | solution.py:59
  36.6 4.9 %all-to-all-start.1 = ((f32[64,16,128]{2,1,0:T(8,128)}), f32[64,16,128]{2,1,0:T(8,128)}, u32[]{:S(2)}, u32[]{:S(2)}) async-start(f32[64,16,128]{2,1,0:T(8,128)} %broadcast_select_fusion.2), calls=%async_computation.1 | async-start | bytes 1048576 | tf_op jit(solution)/shard_map/all_to_all | solution.py:60
  41.5 0.8 gather_fusion
  42.3 0.1 reshape.148
  42.4 0.1 reshape.91
  42.5 0.6 pad_clamp_fusion
  43.1 1.9 %convert_reduce_fusion = f32[8,384,128]{2,1,0:T(8,128)} fusion(s32[8,3,128]{2,1,0:T(4,128)S(1)} %copy.57), kind=kLoop, calls=%fused_computation.7 | loop fusion | flops 3145728 | bytes 1585152 | tf_op jit(solution)/shard_map/reduce_sum | solution.py:81
  44.9 0.5 compare_and_fusion
  45.5 14.3 %all-to-all-done.1 = f32[64,16,128]{2,1,0:T(8,128)} async-done(((f32[64,16,128]{2,1,0:T(8,128)}), f32[64,16,128]{2,1,0:T(8,128)}, u32[]{:S(2)}, u32[]{:S(2)}) %all-to-all-start.1) | async-done | bytes 524320 | tf_op jit(solution)/shard_map/all_to_all | solution.py:60
  59.8 1.9 %pad_maximum_fusion = f32[72,16,128]{2,1,0:T(8,128)} fusion(f32[64,16,128]{2,1,0:T(8,128)} %all-to-all-done.1, f32[8,16,128]{2,1,0:T(8,128)S(1)} %bitcast_bitcast_fusion.2), kind=kLoop, calls=%fused_computation.20 | loop fusion | flops 147456 | bytes 1179648 | tf_op jit(solution)/shard_map/concatenate | solution.py:61
  61.7 1.8 %gather_fusion.2 = f32[48,16,128]{2,1,0:T(8,128)S(1)} fusion(f32[72,16,128]{2,1,0:T(8,128)} %pad_maximum_fusion, s32[1024]{0:T(1024)} %pad_clamp_fusion), kind=kCustom, calls=%fused_computation.1.clone | custom fusion | bytes 786624 | tf_op jit(solution)/shard_map/jit(_take)/gather | solution.py:62
  63.5 0.0 copy-start.8
  63.5 0.0 copy-start.11
  63.5 0.8 broadcast_select_fusion.5
  64.3 0.0 copy-start.4
  64.3 2.7 %fusion.5 = f32[8,2,8,128]{3,2,1,0:T(8,128)S(1)} fusion(f32[8,6,16,128]{3,2,1,0:T(8,128)S(1)} %bitcast.101, f32[8,6,128,128]{3,2,1,0:T(8,128)S(1)} %copy-done), kind=kOutput, calls=%fused_computation.17 | convolution fusion | flops 151011328 | bytes 3604480 | tf_op jit(solution)/shard_map/rkij,rktj->tri/dot_general | solution.py:63
  67.0 0.6 copy-done.1
  67.7 1.5 %gather_fusion.3 = f32[64,16,128]{2,1,0:T(8,128)} fusion(f32[8,16,128]{2,1,0:T(8,128)S(1)} %bitcast_bitcast_fusion.1, s32[1024]{0:T(1024)} %copy-done.17), kind=kCustom, calls=%fused_computation.2.clone | custom fusion | bytes 1048832 | tf_op jit(solution)/shard_map/jit(_take)/gather | solution.py:59
  69.2 2.0 %broadcast_select_fusion.1 = f32[64,16,128]{2,1,0:T(8,128)} fusion(f32[64,16,128]{2,1,0:T(8,128)} %gather_fusion.3, pred[64]{0:T(512)(128)(4,1)S(1)} %copy-done.19), kind=kLoop, calls=%fused_computation.24 | loop fusion | flops 131072 | bytes 1048640 | tf_op jit(solution)/shard_map/jit(_take)/select_n | solution.py:59
  71.2 5.2 %all-to-all-start.2 = ((f32[64,16,128]{2,1,0:T(8,128)}), f32[64,16,128]{2,1,0:T(8,128)}, u32[]{:S(2)}, u32[]{:S(2)}) async-start(f32[64,16,128]{2,1,0:T(8,128)} %broadcast_select_fusion.1), calls=%async_computation.2 | async-start | bytes 1048576 | tf_op jit(solution)/shard_map/all_to_all | solution.py:60
  76.5 2.5 %fusion.6 = f32[8,2,8,128]{3,2,1,0:T(8,128)S(1)} fusion(f32[8,384,128]{2,1,0:T(8,128)} %convert_reduce_fusion, f32[16,8,128]{2,0,1:T(8,128)S(1)} %copy.67, f32[16,8,128]{2,0,1:T(8,128)S(1)} %copy.66, f32[16,8,128]{2,0,1:T(8,128)S(1)} %copy.65), kind=kOutput, calls=%fused_computation.19 | convolution fusion | flops 75612160 | bytes 1835008 | tf_op jit(solution)/shard_map/tbj,bji->tbi/dot_general | solution.py:84
  79.1 0.0 copy-start.13
  79.1 1.9 %collective-permute-start.2 = (f32[1,1024]{1,0:T(1,128)S(1)}, f32[1,1024]{1,0:T(1,128)S(1)}, u32[]{:S(2)}, u32[]{:S(2)}) collective-permute-start(f32[1,1024]{1,0:T(1,128)S(1)} %slice.45), channel_id=1, source_target_pairs={{0,1},{1,2},{2,3},{3,4},{4,5},{5,6},{6,7},{7,8},{8,9},{9,10},{10,1... | collective-permute-start | bytes 12296 | tf_op jit(solution)/shard_map/ppermute | solution.py:31
  81.0 12.8 %collective-permute-done.2 = f32[1,1024]{1,0:T(1,128)S(1)} collective-permute-done((f32[1,1024]{1,0:T(1,128)S(1)}, f32[1,1024]{1,0:T(1,128)S(1)}, u32[]{:S(2)}, u32[]{:S(2)}) %collective-permute-start.2) | collective-permute-done | bytes 4128 | tf_op jit(solution)/shard_map/ppermute | solution.py:31
  93.8 0.8 all-to-all-done.2
  94.6 1.9 %pad_maximum_fusion.1 = f32[72,16,128]{2,1,0:T(8,128)} fusion(f32[64,16,128]{2,1,0:T(8,128)} %all-to-all-done.2, f32[8,16,128]{2,1,0:T(8,128)S(1)} %bitcast_bitcast_fusion.1), kind=kLoop, calls=%fused_computation.21 | loop fusion | flops 147456 | bytes 1179648 | tf_op jit(solution)/shard_map/concatenate | solution.py:61
  96.5 1.8 %gather_fusion.4 = f32[48,16,128]{2,1,0:T(8,128)S(1)} fusion(f32[72,16,128]{2,1,0:T(8,128)} %pad_maximum_fusion.1, s32[1024]{0:T(1024)} %pad_clamp_fusion), kind=kCustom, calls=%fused_computation.4.clone | custom fusion | bytes 786624 | tf_op jit(solution)/shard_map/jit(_take)/gather | solution.py:62
  98.3 0.0 copy-start.9
  98.3 0.0 copy-start.12
  98.4 0.8 broadcast_select_fusion.4
  99.2 2.7 %fusion.3 = f32[8,2,8,128]{3,2,1,0:T(8,128)S(1)} fusion(f32[8,6,16,128]{3,2,1,0:T(8,128)S(1)} %bitcast.102, f32[8,6,128,128]{3,2,1,0:T(8,128)S(1)} %copy-done), kind=kOutput, calls=%fused_computation.14 | convolution fusion | flops 151011328 | bytes 3604480 | tf_op jit(solution)/shard_map/rkij,rktj->tri/dot_general | solution.py:63
  101.9 0.0 copy-start.21
  102.0 0.7 multiply_multiply_fusion
  102.7 0.6 copy-done.15
  103.3 1.6 %gather_fusion.5 = f32[64,16,128]{2,1,0:T(8,128)} fusion(f32[8,16,128]{2,1,0:T(8,128)S(1)} %bitcast_bitcast_fusion, s32[1024]{0:T(1024)} %copy-done.17), kind=kCustom, calls=%fused_computation.3.clone | custom fusion | bytes 1048832 | tf_op jit(solution)/shard_map/jit(_take)/gather | solution.py:59
  104.9 1.2 broadcast_select_fusion
  106.0 28.3 %all_to_all.24 = f32[64,16,128]{2,1,0:T(8,128)S(1)} all-to-all(f32[64,16,128]{2,1,0:T(8,128)S(1)} %broadcast_select_fusion), channel_id=1, replica_groups=mesh['space'=32,'tm'=16] {'space'}, dimensions={0} | all-to-all | bytes 1048576 | tf_op jit(solution)/shard_map/all_to_all | solution.py:60
  134.4 0.9 pad_maximum_fusion.2
  135.2 1.8 %gather_fusion.6 = f32[48,16,128]{2,1,0:T(8,128)S(1)} fusion(f32[72,16,128]{2,1,0:T(8,128)} %pad_maximum_fusion.2, s32[1024]{0:T(1024)} %pad_clamp_fusion), kind=kCustom, calls=%fused_computation.5.clone | custom fusion | bytes 786624 | tf_op jit(solution)/shard_map/jit(_take)/gather | solution.py:62
  137.0 0.0 copy-start.10
  137.0 0.1 broadcast_select_fusion.3
  137.2 2.7 %fusion.1 = f32[8,2,8,128]{3,2,1,0:T(8,128)S(1)} fusion(f32[8,6,16,128]{3,2,1,0:T(8,128)S(1)} %bitcast.100, f32[8,6,128,128]{3,2,1,0:T(8,128)S(1)} %copy-done), kind=kOutput, calls=%fused_computation.11 | convolution fusion | flops 151011328 | bytes 3604480 | tf_op jit(solution)/shard_map/rkij,rktj->tri/dot_general | solution.py:63
  139.9 0.0 copy-done.7
  139.9 0.6 bitcast_subtract_fusion
  (57 shorter events, 0.3 us)
Async XLA Ops:
  0.6 63.7 %copy-start = (f32[8,6,128,128]{3,2,1,0:T(8,128)S(1)}, f32[8,6,128,128]{3,2,1,0:T(8,128)}, u32[]{:S(2)}) copy-start(f32[8,6,128,128]{3,2,1,0:T(8,128)} %param.13) | copy-start | bytes 9437188
  2.1 74.3 %collective-permute-start.1 = (f32[16,128]{1,0:T(8,128)}, f32[16,128]{1,0:T(8,128)S(1)}, u32[]{:S(2)}, u32[]{:S(2)}) collective-permute-start(f32[16,128]{1,0:T(8,128)} %get-tuple-element.15), channel_id=1, source_target_pairs={{16,0},{32,16},{48,32},{64,48},{80,64},{96,80},{112,96},{128,112},... | collective-permute-start | bytes 24584 | tf_op jit(solution)/shard_map/ppermute | solution.py:23
  10.9 65.5 %collective-permute-start = (f32[16,128]{1,0:T(8,128)}, f32[16,128]{1,0:T(8,128)S(1)}, u32[]{:S(2)}, u32[]{:S(2)}) collective-permute-start(f32[16,128]{1,0:T(8,128)} %get-tuple-element.14), channel_id=1, source_target_pairs={{0,16},{16,32},{32,48},{48,64},{64,80},{80,96},{96,112},{112,128},... | collective-permute-start | bytes 24584 | tf_op jit(solution)/shard_map/ppermute | solution.py:20
  14.6 17.2 %all-to-all-start = ((s32[32,1,2]{2,1,0:T(1,128)}), s32[32,1,2]{2,1,0:T(1,128)S(1)}, u32[]{:S(2)}, u32[]{:S(2)}) async-start(s32[32,1,2]{2,1,0:T(1,128)} %copy.51), calls=%async_computation | async-start | bytes 32768 | tf_op jit(solution)/shard_map/all_to_all | solution.py:52
  33.2 3.5 %copy-start.18 = (pred[64]{0:T(512)(128)(4,1)}, pred[64]{0:T(512)(128)(4,1)S(1)}, u32[]{:S(2)}) copy-start(pred[64]{0:T(512)(128)(4,1)S(1)} %compare_and_fusion.1) | copy-start | bytes 196
  33.2 8.3 %copy-start.17 = (s32[1024]{0:T(1024)}, s32[1024]{0:T(1024)S(1)}, u32[]{:S(2)}) copy-start(s32[1024]{0:T(1024)S(1)} %pad_clamp_fusion.1) | copy-start | bytes 12292
  34.6 7.7 %copy-start.16 = (s32[8,6]{1,0:T(8,128)S(1)}, s32[8,6]{1,0:T(8,128)}, u32[]{:S(2)}) copy-start(s32[8,6]{1,0:T(8,128)} %param.14) | copy-start | bytes 580
  36.6 23.2 %all-to-all-start.1 = ((f32[64,16,128]{2,1,0:T(8,128)}), f32[64,16,128]{2,1,0:T(8,128)}, u32[]{:S(2)}, u32[]{:S(2)}) async-start(f32[64,16,128]{2,1,0:T(8,128)} %broadcast_select_fusion.2), calls=%async_computation.1 | async-start | bytes 1048576 | tf_op jit(solution)/shard_map/all_to_all | solution.py:60
  63.5 4.2 %copy-start.8 = (f32[16,1024]{1,0:T(8,128)S(1)}, f32[16,1024]{1,0:T(8,128)}, u32[]{:S(2)}) copy-start(f32[16,1024]{1,0:T(8,128)} %param.11) | copy-start | bytes 196612
  63.5 4.2 %copy-start.11 = (f32[16,1024]{1,0:T(8,128)S(1)}, f32[16,1024]{1,0:T(8,128)}, u32[]{:S(2)}) copy-start(f32[16,1024]{1,0:T(8,128)} %param.10) | copy-start | bytes 196612
  64.3 5.0 %copy-start.19 = (pred[64]{0:T(512)(128)(4,1)S(1)}, pred[64]{0:T(512)(128)(4,1)}, u32[]{:S(2)}) copy-start(pred[64]{0:T(512)(128)(4,1)} %copy-done.18) | copy-start | bytes 196
  64.3 12.1 %copy-start.4 = (f32[16,1024]{1,0:T(8,128)S(1)}, f32[16,1024]{1,0:T(8,128)}, u32[]{:S(2)}) copy-start(f32[16,1024]{1,0:T(8,128)} %param.12) | copy-start | bytes 196612
  67.0 0.6 copy-start.1
  71.2 23.4 %all-to-all-start.2 = ((f32[64,16,128]{2,1,0:T(8,128)}), f32[64,16,128]{2,1,0:T(8,128)}, u32[]{:S(2)}, u32[]{:S(2)}) async-start(f32[64,16,128]{2,1,0:T(8,128)} %broadcast_select_fusion.1), calls=%async_computation.2 | async-start | bytes 1048576 | tf_op jit(solution)/shard_map/all_to_all | solution.py:60
  79.1 15.5 %copy-start.13 = (f32[16,1024]{1,0:T(8,128)}, f32[16,1024]{1,0:T(8,128)S(1)}, u32[]{:S(2)}) copy-start(f32[16,1024]{1,0:T(8,128)S(1)} %bitcast_add_fusion) | copy-start | bytes 196612
  79.1 14.7 %collective-permute-start.2 = (f32[1,1024]{1,0:T(1,128)S(1)}, f32[1,1024]{1,0:T(1,128)S(1)}, u32[]{:S(2)}, u32[]{:S(2)}) collective-permute-start(f32[1,1024]{1,0:T(1,128)S(1)} %slice.45), channel_id=1, source_target_pairs={{0,1},{1,2},{2,3},{3,4},{4,5},{5,6},{6,7},{7,8},{8,9},{9,10},{10,1... | collective-permute-start | bytes 12296 | tf_op jit(solution)/shard_map/ppermute | solution.py:31
  98.3 3.6 %copy-start.2 = (f32[8,2,8,128]{3,2,1,0:T(8,128)S(1)}, f32[8,2,8,128]{3,2,1,0:T(8,128)}, u32[]{:S(2)}) copy-start(f32[8,2,8,128]{3,2,1,0:T(8,128)} %copy-done.1) | copy-start | bytes 196612
  98.3 3.6 %copy-start.5 = (f32[16,1024]{1,0:T(8,128)S(1)}, f32[16,1024]{1,0:T(8,128)}, u32[]{:S(2)}) copy-start(f32[16,1024]{1,0:T(8,128)} %param.12) | copy-start | bytes 196612
  98.3 3.6 %copy-start.9 = (f32[16,1024]{1,0:T(8,128)S(1)}, f32[16,1024]{1,0:T(8,128)}, u32[]{:S(2)}) copy-start(f32[16,1024]{1,0:T(8,128)} %param.11) | copy-start | bytes 196612
  98.3 3.6 %copy-start.12 = (f32[16,1024]{1,0:T(8,128)S(1)}, f32[16,1024]{1,0:T(8,128)}, u32[]{:S(2)}) copy-start(f32[16,1024]{1,0:T(8,128)} %param.10) | copy-start | bytes 196612
  98.3 3.6 %copy-start.14 = (f32[16,1024]{1,0:T(8,128)S(1)}, f32[16,1024]{1,0:T(8,128)}, u32[]{:S(2)}) copy-start(f32[16,1024]{1,0:T(8,128)} %copy-done.13) | copy-start | bytes 196612
  98.4 6.5 %copy-start.20 = (pred[64]{0:T(512)(128)(4,1)S(1)}, pred[64]{0:T(512)(128)(4,1)}, u32[]{:S(2)}) copy-start(pred[64]{0:T(512)(128)(4,1)} %copy-done.18) | copy-start | bytes 196
  101.9 0.8 copy-start.6
  101.9 35.1 %copy-start.21 = (pred[48]{0:T(512)(128)(4,1)S(1)}, pred[48]{0:T(512)(128)(4,1)}, u32[]{:S(2)}) copy-start(pred[48]{0:T(512)(128)(4,1)} %compare_and_fusion) | copy-start | bytes 148
  102.7 0.6 copy-start.15
  137.0 2.9 %copy-start.3 = (f32[8,2,8,128]{3,2,1,0:T(8,128)S(1)}, f32[8,2,8,128]{3,2,1,0:T(8,128)}, u32[]{:S(2)}) copy-start(f32[8,2,8,128]{3,2,1,0:T(8,128)} %copy-done.1) | copy-start | bytes 196612
  137.0 2.9 %copy-start.7 = (f32[8,2,8,128]{3,2,1,0:T(8,128)S(1)}, f32[8,2,8,128]{3,2,1,0:T(8,128)}, u32[]{:S(2)}) copy-start(f32[8,2,8,128]{3,2,1,0:T(8,128)} %copy-done.6) | copy-start | bytes 196612
  137.0 2.9 %copy-start.10 = (f32[16,1024]{1,0:T(8,128)S(1)}, f32[16,1024]{1,0:T(8,128)}, u32[]{:S(2)}) copy-start(f32[16,1024]{1,0:T(8,128)} %param.11) | copy-start | bytes 196612

commit v2 on v1

--- a/solution.py
+++ b/solution.py
@@ -2,6 +2,8 @@
 import jax.numpy as jnp
 from jax import lax
 from jax.sharding import PartitionSpec as P
+from jax.experimental import pallas as pl
+from jax.experimental.pallas import tpu as pltpu
 
 TILE = 128
 
@@ -31,6 +33,83 @@
     return lax.ppermute(value, axis, pairs)
 
 
+def dot_t(a, b):
+    return lax.dot_general(
+        a, b, (((1,), (1,)), ((), ())),
+        precision=lax.Precision.HIGHEST, preferred_element_type=jnp.float32,
+    )
+
+
+def substep(field, moment, got, tiles, pick, send_ids, scale, advance, send):
+    slices, site_count = field.shape
+    rows, kept = tiles.shape[0], tiles.shape[1]
+    slots = send_ids.shape[0]
+
+    def kernel(pick_ref, sid_ref, f_ref, p_ref, got_ref, tiles_ref, *refs):
+        outs = list(refs)
+        p_out = outs.pop(0)
+        f_out = outs.pop(0) if advance else None
+        send_out = outs.pop(0) if send else None
+        held = outs.pop(0) if send else None
+        for r in range(rows):
+            cols = slice(r * TILE, (r + 1) * TILE)
+            acc = dot_t(f_ref[:, cols], tiles_ref[r, 0])
+            for k in range(1, kept):
+                acc = acc + dot_t(got_ref[pick_ref[r * kept + k]], tiles_ref[r, k])
+            p_new = p_ref[:, cols] - scale * acc
+            p_out[:, cols] = p_new
+            if advance:
+                f_new = f_ref[:, cols] + step_size * p_new
+                f_out[:, cols] = f_new
+                if send:
+                    held[r] = f_new
+        if send:
+            def copy_one(s, carry):
+                send_out[s] = held[sid_ref[s]]
+                return carry
+            lax.fori_loop(0, slots, copy_one, 0)
+
+    vmem = pl.BlockSpec(memory_space=pltpu.VMEM)
+    smem = pl.BlockSpec(memory_space=pltpu.SMEM)
+    out_shape = [jax.ShapeDtypeStruct(field.shape, jnp.float32)]
+    if advance:
+        out_shape.append(jax.ShapeDtypeStruct(field.shape, jnp.float32))
+    scratch = []
+    if send:
+        out_shape.append(jax.ShapeDtypeStruct((slots, slices, TILE), jnp.float32))
+        scratch.append(pltpu.VMEM((rows, slices, TILE), jnp.float32))
+    return pl.pallas_call(
+        kernel,
+        out_shape=tuple(out_shape),
+        in_specs=[smem, smem, vmem, vmem, vmem, vmem],
+        out_specs=tuple([vmem] * len(out_shape)),
+        scratch_shapes=scratch,
+    )(pick, send_ids, field, moment, got, tiles)
+
+
+def gather_tiles(values, send_ids):
+    slices, site_count = values.shape
+    rows = site_count // TILE
+    slots = send_ids.shape[0]
+
+    def kernel(sid_ref, v_ref, send_out, held):
+        for r in range(rows):
+            held[r] = v_ref[:, r * TILE:(r + 1) * TILE]
+
+        def copy_one(s, carry):
+            send_out[s] = held[sid_ref[s]]
+            return carry
+        lax.fori_loop(0, slots, copy_one, 0)
+
+    return pl.pallas_call(
+        kernel,
+        out_shape=jax.ShapeDtypeStruct((slots, slices, TILE), jnp.float32),
+        in_specs=[pl.BlockSpec(memory_space=pltpu.SMEM), pl.BlockSpec(memory_space=pltpu.VMEM)],
+        out_specs=pl.BlockSpec(memory_space=pltpu.VMEM),
+        scratch_shapes=[pltpu.VMEM((rows, slices, TILE), jnp.float32)],
+    )(send_ids, values)
+
+
 def body(field, momentum, solution, tiles, columns, neighbours):
     slices = field.shape[0]
     tile_rows = tiles.shape[0]
@@ -52,22 +131,18 @@
     wanted = lax.all_to_all(request, "space", 0, 0, tiled=True)
     send_ids = wanted.reshape(-1)
     slot = jnp.where(local_id == lo[run_of], 0, 1)
-    pick = jnp.where(remote, tile_rows + run_of * 2 + slot, local_id).reshape(-1)
 
-    def coulomb(values):
-        own = values.reshape(slices, tile_rows, TILE).transpose(1, 0, 2)
-        sent = jnp.take(own, send_ids, axis=0)
-        got = lax.all_to_all(sent, "space", 0, 0, tiled=True)
-        pool = jnp.concatenate([own, got], axis=0)
-        picked = jnp.take(pool, pick, axis=0).reshape(tile_rows, kept, slices, TILE)
-        mixed = jnp.einsum("rkij,rktj->tri", tiles, picked, precision=lax.Precision.HIGHEST)
-        return mixed.reshape(slices, site_count)
+    pick = jnp.where(remote, run_of * 2 + slot, 0).reshape(-1)
 
-    moment = momentum - 0.5 * step_size * coulomb(field)
-    field_one = field + step_size * moment
-    moment = moment - step_size * coulomb(field_one)
-    field_two = field_one + step_size * moment
-    moment = moment - 0.5 * step_size * coulomb(field_two)
+    def exchange(sent):
+        return lax.all_to_all(sent, "space", 0, 0, tiled=True)
+
+    got = exchange(gather_tiles(field, send_ids))
+    moment, field_one, sent = substep(field, momentum, got, tiles, pick, send_ids, 0.5 * step_size, True, True)
+    got = exchange(sent)
+    moment, field_two, sent = substep(field_one, moment, got, tiles, pick, send_ids, step_size, True, True)
+    got = exchange(sent)
+    (moment,) = substep(field_two, moment, got, tiles, pick, send_ids, 0.5 * step_size, False, False)
 
     total_sites = site_count * space_count
     first_site = me * site_count

time: 142 us -> 124 us (0.87)
  the two profiles are of different devices: /device:TPU:1 before, /device:TPU:32 now
where the time goes in v2:
time: 124 us
  waiting for transfers between devices  36.9 us (30%)
  starting transfers between devices  35.5 us (29%)
  Pallas kernels  26.4 us (21%)
  blocking collectives  14.3 us (12%)
  local copies, waits for them, and re-layouts  5.53 us (4%)
  other arithmetic  3.03 us (2%)
    all_to_all x3, starting transfers between devices, exchange(): return lax.all_to_all(sent, 'space', 0, 0, tiled=True)  25.6 us
    pallas_call x3, Pallas kernels, substep(): pl.pallas_call(kernel, out_shape=tuple(out_shape), in_specs=[smem, smem,...  24.4 us
    ppermute x1, waiting for transfers between devices, from_behind(): return lax.ppermute(value, axis, pairs)  17.5 us
    all_to_all x3, waiting for transfers between devices, exchange(): return lax.all_to_all(sent, 'space', 0, 0, tiled=True)  16.3 us
    all_to_all x1, blocking collectives, body(): wanted = lax.all_to_all(request, 'space', 0, 0, tiled=True)  14.3 us
    ppermute x1, starting transfers between devices, with_halo(): lax.ppermute(lax.slice_in_dim(block, 0, width, axis=dim), axis, backward)  5.61 us
    ppermute x1, waiting for transfers between devices, with_halo(): lax.ppermute(lax.slice_in_dim(block, block.shape[dim] - width, None, axis...  2.94 us
  transfers between devices with their start and end apart: 6, of which 5 were waited for; matrix products, arithmetic and copies ran while one was open for 3% of the time, Pallas kernels for 0%

profile of v2, /device:TPU:32, one launch (start us, length us, event | category | flops | bytes accessed | tf_op | source)
XLA Modules:
  0.0 123.7 jit_solution(1383309080763904901)
XLA Ops:
  0.6 0.7 compare_select_fusion
  1.3 0.1 copy.25
  1.4 0.1 copy.24
  1.5 0.1 copy.26
  1.6 0.1 select_reduce_fusion
  1.7 0.1 copy.27
  1.8 14.3 %all_to_all.24 = s32[32,1,2]{2,1,0:T(1,128)S(1)} all-to-all(s32[32,1,2]{2,1,0:T(1,128)S(1)} %copy.27), channel_id=1, replica_groups=mesh['space'=32,'tm'=16] {'space'}, dimensions={0} | all-to-all | bytes 512 | tf_op jit(solution)/shard_map/all_to_all | solution.py:131
  16.2 0.5 broadcast.98
  16.7 0.7 reduce.3
  17.4 0.7 reshape.53.sid_ref
  18.0 2.0 %shard_map.85 = f32[64,16,128]{2,1,0:T(8,128)} custom-call(s32[64]{0:T(128)} %reshape.53.sid_ref, f32[16,1024]{1,0:T(8,128)} %f_ref.1), custom_call_target="tpu_custom_call" | custom-call | tf_op jit(solution)/shard_map/pallas_call | solution.py:104
  20.1 8.9 %all-to-all-start.1 = ((f32[64,16,128]{2,1,0:T(8,128)}), f32[64,16,128]{2,1,0:T(8,128)S(1)}, u32[]{:S(2)}, u32[]{:S(2)}) async-start(f32[64,16,128]{2,1,0:T(8,128)} %shard_map.85), calls=%async_computation.1 | async-start | bytes 1048576 | tf_op jit(solution)/shard_map/all_to_all | solution.py:138
  28.9 0.1 reshape.58
  29.0 0.0 copy-start.6
  29.0 0.8 gather_fusion
  29.8 0.1 reshape.57
  29.9 0.0 copy-done.6
  29.9 0.6 reshape.52.pick_ref
  30.5 0.0 copy-start.3
  30.5 0.0 copy-start.5
  30.5 13.2 %all-to-all-done.1.got_ref = f32[64,16,128]{2,1,0:T(8,128)S(1)} async-done(((f32[64,16,128]{2,1,0:T(8,128)}), f32[64,16,128]{2,1,0:T(8,128)S(1)}, u32[]{:S(2)}, u32[]{:S(2)}) %all-to-all-start.1) | async-done | bytes 524320 | tf_op jit(solution)/shard_map/all_to_all | solution.py:138
  43.7 0.0 copy-start.2
  43.7 0.8 copy-done.2
  44.5 8.3 %shard_map.86 = (f32[16,1024]{1,0:T(8,128)}, f32[16,1024]{1,0:T(8,128)}, f32[64,16,128]{2,1,0:T(8,128)}) custom-call(s32[48]{0:T(128)} %reshape.52.pick_ref, s32[64]{0:T(128)} %reshape.53.sid_ref, f32[16,1024]{1,0:T(8,128)} %f_ref.1, f32[16,1024]{1,0:T(8,128)} %p_ref.1, f32[64,16,128]{2,1,0:T(8,128)} %copy-done.2, f32[8,6,128,128]{3,2,1,0:T(8,128)} %tiles_ref.5), custom_call_target="tpu_custom_call" | custom-call | tf_op jit(solution)/shard_map/pallas_call | solution.py:81
  52.8 8.4 %all-to-all-start.2 = ((f32[64,16,128]{2,1,0:T(8,128)}), f32[64,16,128]{2,1,0:T(8,128)S(1)}, u32[]{:S(2)}, u32[]{:S(2)}) async-start(f32[64,16,128]{2,1,0:T(8,128)} %get-tuple-element.11), calls=%async_computation.2 | async-start | bytes 1048576 | tf_op jit(solution)/shard_map/all_to_all | solution.py:138
  61.3 0.0 copy-done.3
  61.3 2.1 %collective-permute-start = (f32[16,128]{1,0:T(8,128)S(1)}, f32[16,128]{1,0:T(8,128)S(1)}, u32[]{:S(2)}, u32[]{:S(2)}) collective-permute-start(f32[16,128]{1,0:T(8,128)S(1)} %get-tuple-element.22), channel_id=1, source_target_pairs={{0,16},{16,32},{32,48},{48,64},{64,80},{80,96},{96,112},{112,128},... | collective-permute-start | bytes 24584 | tf_op jit(solution)/shard_map/ppermute | solution.py:22
  63.3 5.6 %collective-permute-start.1 = (f32[16,128]{1,0:T(8,128)S(1)}, f32[16,128]{1,0:T(8,128)S(1)}, u32[]{:S(2)}, u32[]{:S(2)}) collective-permute-start(f32[16,128]{1,0:T(8,128)S(1)} %get-tuple-element.23), channel_id=1, source_target_pairs={{16,0},{32,16},{48,32},{64,48},{80,64},{96,80},{112,96},{128,112},... | collective-permute-start | bytes 24584 | tf_op jit(solution)/shard_map/ppermute | solution.py:25
  69.0 0.0 copy-done.5
  69.0 0.1 fusion.9
  69.1 0.7 convert_reduce_fusion
  69.8 2.9 %collective-permute-done = f32[16,128]{1,0:T(8,128)S(1)} collective-permute-done((f32[16,128]{1,0:T(8,128)S(1)}, f32[16,128]{1,0:T(8,128)S(1)}, u32[]{:S(2)}, u32[]{:S(2)}) %collective-permute-start) | collective-permute-done | bytes 8224 | tf_op jit(solution)/shard_map/ppermute | solution.py:22
  72.7 0.1 collective-permute-done.1
  72.9 3.0 %all-to-all-done.2.got_ref = f32[64,16,128]{2,1,0:T(8,128)S(1)} async-done(((f32[64,16,128]{2,1,0:T(8,128)}), f32[64,16,128]{2,1,0:T(8,128)S(1)}, u32[]{:S(2)}, u32[]{:S(2)}) %all-to-all-start.2) | async-done | bytes 524320 | tf_op jit(solution)/shard_map/all_to_all | solution.py:138
  76.0 0.0 copy-start.1
  76.0 0.8 copy-done.1
  76.7 8.3 %shard_map.87 = (f32[16,1024]{1,0:T(8,128)}, f32[16,1024]{1,0:T(8,128)}, f32[64,16,128]{2,1,0:T(8,128)}) custom-call(s32[48]{0:T(128)} %reshape.52.pick_ref, s32[64]{0:T(128)} %reshape.53.sid_ref, f32[16,1024]{1,0:T(8,128)} %get-tuple-element.9.f_ref, f32[16,1024]{1,0:T(8,128)} %get-tuple-element.10.p_ref, f32[64,16,128]{2,1,0:T(8,128)} %copy-done.1, ...), custom_call_target="tpu_custom_call" | custom-call | tf_op jit(solution)/shard_map/pallas_call | solution.py:81
  85.1 8.4 %all-to-all-start.3 = ((f32[64,16,128]{2,1,0:T(8,128)}), f32[64,16,128]{2,1,0:T(8,128)S(1)}, u32[]{:S(2)}, u32[]{:S(2)}) async-start(f32[64,16,128]{2,1,0:T(8,128)} %get-tuple-element.14), calls=%async_computation.3 | async-start | bytes 1048576 | tf_op jit(solution)/shard_map/all_to_all | solution.py:138
  93.4 0.0 copy-start.4
  93.5 1.1 fusion
  94.7 2.2 %collective-permute-start.2 = (f32[1,1024]{1,0:T(1,128)S(1)}, f32[1,1024]{1,0:T(1,128)S(1)}, u32[]{:S(2)}, u32[]{:S(2)}) collective-permute-start(f32[1,1024]{1,0:T(1,128)S(1)} %slice.33), channel_id=1, source_target_pairs={{0,1},{1,2},{2,3},{3,4},{4,5},{5,6},{6,7},{7,8},{8,9},{9,10},{10,1... | collective-permute-start | bytes 12296 | tf_op jit(solution)/shard_map/ppermute | solution.py:33
  96.9 17.5 %collective-permute-done.2 = f32[1,1024]{1,0:T(1,128)S(1)} collective-permute-done((f32[1,1024]{1,0:T(1,128)S(1)}, f32[1,1024]{1,0:T(1,128)S(1)}, u32[]{:S(2)}, u32[]{:S(2)}) %collective-permute-start.2) | collective-permute-done | bytes 4128 | tf_op jit(solution)/shard_map/ppermute | solution.py:33
  114.5 0.0 copy-done.4
  114.5 0.7 multiply_multiply_fusion
  115.1 0.0 all-to-all-done.3.got_ref
  115.1 0.0 copy-start
  115.1 0.8 copy-done
  115.9 7.7 %shard_map.88 = f32[16,1024]{1,0:T(8,128)} custom-call(s32[48]{0:T(128)} %reshape.52.pick_ref, s32[64]{0:T(128)} %reshape.53.sid_ref, f32[16,1024]{1,0:T(8,128)} %get-tuple-element.6.f_ref, f32[16,1024]{1,0:T(8,128)} %get-tuple-element.13.p_ref, f32[64,16,128]{2,1,0:T(8,128)} %copy-done, f32[8,6,128,128]{3,2,1,0:T(8,128)} %tiles_ref.5), custom_call_target="tpu_custom_call" | custom-call | tf_op jit(solution)/shard_map/pallas_call | solution.py:81
  (19 shorter events, 0.2 us)
Async XLA Ops:
  20.1 23.7 %all-to-all-start.1 = ((f32[64,16,128]{2,1,0:T(8,128)}), f32[64,16,128]{2,1,0:T(8,128)S(1)}, u32[]{:S(2)}, u32[]{:S(2)}) async-start(f32[64,16,128]{2,1,0:T(8,128)} %shard_map.85), calls=%async_computation.1 | async-start | bytes 1048576 | tf_op jit(solution)/shard_map/all_to_all | solution.py:138
  29.0 0.9 copy-start.6
  30.5 30.7 %copy-start.3 = (f32[16,1024]{1,0:T(8,128)S(1)}, f32[16,1024]{1,0:T(8,128)}, u32[]{:S(2)}) copy-start(f32[16,1024]{1,0:T(8,128)} %param.8) | copy-start | bytes 196612
  30.5 38.5 %copy-start.5 = (s32[3,1024]{1,0:T(4,128)S(1)}, s32[3,1024]{1,0:T(4,128)}, u32[]{:S(2)}) copy-start(s32[3,1024]{1,0:T(4,128)} %param.11) | copy-start | bytes 36868
  43.7 0.8 copy-start.2
  52.8 23.1 %all-to-all-start.2 = ((f32[64,16,128]{2,1,0:T(8,128)}), f32[64,16,128]{2,1,0:T(8,128)S(1)}, u32[]{:S(2)}, u32[]{:S(2)}) async-start(f32[64,16,128]{2,1,0:T(8,128)} %get-tuple-element.11), calls=%async_computation.2 | async-start | bytes 1048576 | tf_op jit(solution)/shard_map/all_to_all | solution.py:138
  61.3 11.5 %collective-permute-start = (f32[16,128]{1,0:T(8,128)S(1)}, f32[16,128]{1,0:T(8,128)S(1)}, u32[]{:S(2)}, u32[]{:S(2)}) collective-permute-start(f32[16,128]{1,0:T(8,128)S(1)} %get-tuple-element.22), channel_id=1, source_target_pairs={{0,16},{16,32},{32,48},{48,64},{64,80},{80,96},{96,112},{112,128},... | collective-permute-start | bytes 24584 | tf_op jit(solution)/shard_map/ppermute | solution.py:22
  63.3 9.5 %collective-permute-start.1 = (f32[16,128]{1,0:T(8,128)S(1)}, f32[16,128]{1,0:T(8,128)S(1)}, u32[]{:S(2)}, u32[]{:S(2)}) collective-permute-start(f32[16,128]{1,0:T(8,128)S(1)} %get-tuple-element.23), channel_id=1, source_target_pairs={{16,0},{32,16},{48,32},{64,48},{80,64},{96,80},{112,96},{128,112},... | collective-permute-start | bytes 24584 | tf_op jit(solution)/shard_map/ppermute | solution.py:25
  76.0 0.8 copy-start.1
  85.1 30.1 %all-to-all-start.3 = ((f32[64,16,128]{2,1,0:T(8,128)}), f32[64,16,128]{2,1,0:T(8,128)S(1)}, u32[]{:S(2)}, u32[]{:S(2)}) async-start(f32[64,16,128]{2,1,0:T(8,128)} %get-tuple-element.14), calls=%async_computation.3 | async-start | bytes 1048576 | tf_op jit(solution)/shard_map/all_to_all | solution.py:138
  93.4 21.0 %copy-start.4 = (f32[16,1024]{1,0:T(8,128)S(1)}, f32[16,1024]{1,0:T(8,128)}, u32[]{:S(2)}) copy-start(f32[16,1024]{1,0:T(8,128)} %get-tuple-element.6.f_ref) | copy-start | bytes 196612
  94.7 19.8 %collective-permute-start.2 = (f32[1,1024]{1,0:T(1,128)S(1)}, f32[1,1024]{1,0:T(1,128)S(1)}, u32[]{:S(2)}, u32[]{:S(2)}) collective-permute-start(f32[1,1024]{1,0:T(1,128)S(1)} %slice.33), channel_id=1, source_target_pairs={{0,1},{1,2},{2,3},{3,4},{4,5},{5,6},{6,7},{7,8},{8,9},{9,10},{10,1... | collective-permute-start | bytes 12296 | tf_op jit(solution)/shard_map/ppermute | solution.py:33
  115.1 0.8 copy-start

commit v3 on v2

--- a/solution.py
+++ b/solution.py
@@ -33,16 +33,9 @@
     return lax.ppermute(value, axis, pairs)
 
 
-def dot_t(a, b):
-    return lax.dot_general(
-        a, b, (((1,), (1,)), ((), ())),
-        precision=lax.Precision.HIGHEST, preferred_element_type=jnp.float32,
-    )
-
-
 def substep(field, moment, got, tiles, pick, send_ids, scale, advance, send):
     slices, site_count = field.shape
-    rows, kept = tiles.shape[0], tiles.shape[1]
+    rows, kept = tiles.shape[0], tiles.shape[1] // TILE
     slots = send_ids.shape[0]
 
     def kernel(pick_ref, sid_ref, f_ref, p_ref, got_ref, tiles_ref, *refs):
@@ -53,9 +46,11 @@
         held = outs.pop(0) if send else None
         for r in range(rows):
             cols = slice(r * TILE, (r + 1) * TILE)
-            acc = dot_t(f_ref[:, cols], tiles_ref[r, 0])
-            for k in range(1, kept):
-                acc = acc + dot_t(got_ref[pick_ref[r * kept + k]], tiles_ref[r, k])
+            pieces = [f_ref[:, cols]] + [got_ref[pick_ref[r * kept + k]] for k in range(1, kept)]
+            acc = jnp.dot(
+                jnp.concatenate(pieces, axis=1), tiles_ref[r],
+                precision=lax.Precision.HIGHEST, preferred_element_type=jnp.float32,
+            )
             p_new = p_ref[:, cols] - scale * acc
             p_out[:, cols] = p_new
             if advance:
@@ -137,6 +132,7 @@
     def exchange(sent):
         return lax.all_to_all(sent, "space", 0, 0, tiled=True)
 
+    tiles = tiles.transpose(0, 1, 3, 2).reshape(tile_rows, kept * TILE, TILE)
     got = exchange(gather_tiles(field, send_ids))
     moment, field_one, sent = substep(field, momentum, got, tiles, pick, send_ids, 0.5 * step_size, True, True)
     got = exchange(sent)

time: 124 us -> 114 us (0.919)
  the two profiles are of different devices: /device:TPU:32 before, /device:TPU:1 now
where the time goes in v3:
time: 114 us; the launch traced here: 112 us
  waiting for transfers between devices  39.7 us (35%)
  starting transfers between devices  23.5 us (21%)
  blocking collectives  20.4 us (18%)
  Pallas kernels  15.7 us (14%)
  local copies, waits for them, and re-layouts  7.51 us (7%)
  other arithmetic  3.03 us (3%)
    all_to_all x1, blocking collectives, body(): wanted = lax.all_to_all(request, 'space', 0, 0, tiled=True)  20.4 us
    all_to_all x3, waiting for transfers between devices, exchange(): return lax.all_to_all(sent, 'space', 0, 0, tiled=True)  17.4 us
    ppermute x1, waiting for transfers between devices, from_behind(): return lax.ppermute(value, axis, pairs)  14.9 us
    all_to_all x3, starting transfers between devices, exchange(): return lax.all_to_all(sent, 'space', 0, 0, tiled=True)  14.7 us
    pallas_call x3, Pallas kernels, substep(): pl.pallas_call(kernel, out_shape=tuple(out_shape), in_specs=[smem, smem,...  13.7 us
    ppermute x1, waiting for transfers between devices, with_halo(): lax.ppermute(lax.slice_in_dim(block, 0, width, axis=dim), axis, backward)  7.35 us
    ppermute x1, starting transfers between devices, with_halo(): lax.ppermute(lax.slice_in_dim(block, block.shape[dim] - width, None, axis...  4.32 us
    ppermute x1, starting transfers between devices, from_behind(): return lax.ppermute(value, axis, pairs)  2.35 us
  transfers between devices with their start and end apart: 6, of which 4 were waited for; matrix products, arithmetic and copies ran while one was open for 6% of the time, Pallas kernels for 0%

profile of v3, /device:TPU:1, one launch (start us, length us, event | category | flops | bytes accessed | tf_op | source)
XLA Modules:
  0.0 111.8 jit_solution(3195534281632441241)
XLA Ops:
  0.6 0.7 compare_select_fusion
  1.3 0.1 copy.29
  1.4 0.1 copy.28
  1.5 0.1 copy.27
  1.6 0.1 select_reduce_fusion
  1.7 0.1 copy.30
  1.8 20.4 %all_to_all.24 = s32[32,1,2]{2,1,0:T(1,128)S(1)} all-to-all(s32[32,1,2]{2,1,0:T(1,128)S(1)} %copy.30), channel_id=1, replica_groups=mesh['space'=32,'tm'=16] {'space'}, dimensions={0} | all-to-all | bytes 512 | tf_op jit(solution)/shard_map/all_to_all | solution.py:126
  22.2 0.5 broadcast.98
  22.7 0.7 reduce.3
  23.4 0.6 reshape.56.sid_ref
  24.0 2.1 %shard_map.85 = f32[64,16,128]{2,1,0:T(8,128)} custom-call(s32[64]{0:T(128)} %reshape.56.sid_ref, f32[16,1024]{1,0:T(8,128)} %f_ref.1), custom_call_target="tpu_custom_call" | custom-call | tf_op jit(solution)/shard_map/pallas_call | solution.py:99
  26.1 4.8 %all-to-all-start.1 = ((f32[64,16,128]{2,1,0:T(8,128)}), f32[64,16,128]{2,1,0:T(8,128)}, u32[]{:S(2)}, u32[]{:S(2)}) async-start(f32[64,16,128]{2,1,0:T(8,128)} %shard_map.85), calls=%async_computation.1 | async-start | bytes 1048576 | tf_op jit(solution)/shard_map/all_to_all | solution.py:133
  30.9 0.1 reshape.62
  31.0 0.0 copy-start.6
  31.0 0.0 copy-start
  31.0 0.8 gather_fusion
  31.8 0.1 reshape.61
  31.9 0.0 copy-done.6
  31.9 0.7 reshape.55.pick_ref
  32.6 0.3 copy-done
  32.9 2.3 %copy.31 = f32[8,6,128,128]{3,2,1,0:T(8,128)} copy(f32[8,6,128,128]{2,3,1,0:T(8,128)S(1)} %bitcast.26) | data formatting | bytes 6291456 | tf_op jit(solution)/shard_map/transpose | solution.py:135
  35.3 14.0 %all-to-all-done.1.got_ref = f32[64,16,128]{2,1,0:T(8,128)} async-done(((f32[64,16,128]{2,1,0:T(8,128)}), f32[64,16,128]{2,1,0:T(8,128)}, u32[]{:S(2)}, u32[]{:S(2)}) %all-to-all-start.1) | async-done | bytes 524320 | tf_op jit(solution)/shard_map/all_to_all | solution.py:133
  49.3 0.0 copy-start.3
  49.3 0.0 copy-start.5
  49.3 4.8 %shard_map.86 = (f32[16,1024]{1,0:T(8,128)}, f32[16,1024]{1,0:T(8,128)}, f32[64,16,128]{2,1,0:T(8,128)}) custom-call(s32[48]{0:T(128)} %reshape.55.pick_ref, s32[64]{0:T(128)} %reshape.56.sid_ref, f32[16,1024]{1,0:T(8,128)} %f_ref.1, f32[16,1024]{1,0:T(8,128)} %p_ref.1, f32[64,16,128]{2,1,0:T(8,128)} %all-to-all-done.1.got_ref, f32[8,768,128]{2,1,0:T(8,128)} %bitcast.23), custom_call_target="tpu_custom_call" | custom-call | tf_op jit(solution)/shard_map/pallas_call | solution.py:76
  54.0 5.0 %all-to-all-start.2 = ((f32[64,16,128]{2,1,0:T(8,128)}), f32[64,16,128]{2,1,0:T(8,128)S(1)}, u32[]{:S(2)}, u32[]{:S(2)}) async-start(f32[64,16,128]{2,1,0:T(8,128)} %get-tuple-element.11), calls=%async_computation.2 | async-start | bytes 1048576 | tf_op jit(solution)/shard_map/all_to_all | solution.py:133
  59.0 0.0 copy-done.3
  59.0 2.1 %collective-permute-start.1 = (f32[16,128]{1,0:T(8,128)S(1)}, f32[16,128]{1,0:T(8,128)S(1)}, u32[]{:S(2)}, u32[]{:S(2)}) collective-permute-start(f32[16,128]{1,0:T(8,128)S(1)} %get-tuple-element.23), channel_id=1, source_target_pairs={{16,0},{32,16},{48,32},{64,48},{80,64},{96,80},{112,96},{128,112},... | collective-permute-start | bytes 24584 | tf_op jit(solution)/shard_map/ppermute | solution.py:25
  61.2 4.3 %collective-permute-start = (f32[16,128]{1,0:T(8,128)S(1)}, f32[16,128]{1,0:T(8,128)S(1)}, u32[]{:S(2)}, u32[]{:S(2)}) collective-permute-start(f32[16,128]{1,0:T(8,128)S(1)} %get-tuple-element.22), channel_id=1, source_target_pairs={{0,16},{16,32},{32,48},{48,64},{64,80},{80,96},{96,112},{112,128},... | collective-permute-start | bytes 24584 | tf_op jit(solution)/shard_map/ppermute | solution.py:22
  65.5 0.0 copy-done.5
  65.6 0.1 fusion.9
  65.6 0.7 convert_reduce_fusion
  66.4 7.4 %collective-permute-done.1 = f32[16,128]{1,0:T(8,128)S(1)} collective-permute-done((f32[16,128]{1,0:T(8,128)S(1)}, f32[16,128]{1,0:T(8,128)S(1)}, u32[]{:S(2)}, u32[]{:S(2)}) %collective-permute-start.1) | collective-permute-done | bytes 8224 | tf_op jit(solution)/shard_map/ppermute | solution.py:25
  73.7 0.0 collective-permute-done
  73.7 3.4 %all-to-all-done.2.got_ref = f32[64,16,128]{2,1,0:T(8,128)S(1)} async-done(((f32[64,16,128]{2,1,0:T(8,128)}), f32[64,16,128]{2,1,0:T(8,128)S(1)}, u32[]{:S(2)}, u32[]{:S(2)}) %all-to-all-start.2) | async-done | bytes 524320 | tf_op jit(solution)/shard_map/all_to_all | solution.py:133
  77.2 0.0 copy-start.2
  77.2 0.8 copy-done.2
  78.0 4.7 %shard_map.87 = (f32[16,1024]{1,0:T(8,128)}, f32[16,1024]{1,0:T(8,128)}, f32[64,16,128]{2,1,0:T(8,128)}) custom-call(s32[48]{0:T(128)} %reshape.55.pick_ref, s32[64]{0:T(128)} %reshape.56.sid_ref, f32[16,1024]{1,0:T(8,128)} %get-tuple-element.9.f_ref, f32[16,1024]{1,0:T(8,128)} %get-tuple-element.10.p_ref, f32[64,16,128]{2,1,0:T(8,128)} %copy-done.2, ...), custom_call_target="tpu_custom_call" | custom-call | tf_op jit(solution)/shard_map/pallas_call | solution.py:76
  82.7 4.9 %all-to-all-start.3 = ((f32[64,16,128]{2,1,0:T(8,128)}), f32[64,16,128]{2,1,0:T(8,128)S(1)}, u32[]{:S(2)}, u32[]{:S(2)}) async-start(f32[64,16,128]{2,1,0:T(8,128)} %get-tuple-element.14), calls=%async_computation.3 | async-start | bytes 1048576 | tf_op jit(solution)/shard_map/all_to_all | solution.py:133
  87.6 0.0 copy-start.4
  87.7 1.1 fusion
  88.9 2.4 %collective-permute-start.2 = (f32[1,1024]{1,0:T(1,128)S(1)}, f32[1,1024]{1,0:T(1,128)S(1)}, u32[]{:S(2)}, u32[]{:S(2)}) collective-permute-start(f32[1,1024]{1,0:T(1,128)S(1)} %slice.33), channel_id=1, source_target_pairs={{0,1},{1,2},{2,3},{3,4},{4,5},{5,6},{6,7},{7,8},{8,9},{9,10},{10,1... | collective-permute-start | bytes 12296 | tf_op jit(solution)/shard_map/ppermute | solution.py:33
  91.3 14.9 %collective-permute-done.2 = f32[1,1024]{1,0:T(1,128)S(1)} collective-permute-done((f32[1,1024]{1,0:T(1,128)S(1)}, f32[1,1024]{1,0:T(1,128)S(1)}, u32[]{:S(2)}, u32[]{:S(2)}) %collective-permute-start.2) | collective-permute-done | bytes 4128 | tf_op jit(solution)/shard_map/ppermute | solution.py:33
  106.2 0.0 copy-done.4
  106.2 0.7 multiply_multiply_fusion
  106.8 0.0 all-to-all-done.3.got_ref
  106.8 0.0 copy-start.1
  106.8 0.8 copy-done.1
  107.7 4.1 %shard_map.88 = f32[16,1024]{1,0:T(8,128)} custom-call(s32[48]{0:T(128)} %reshape.55.pick_ref, s32[64]{0:T(128)} %reshape.56.sid_ref, f32[16,1024]{1,0:T(8,128)} %get-tuple-element.6.f_ref, f32[16,1024]{1,0:T(8,128)} %get-tuple-element.13.p_ref, f32[64,16,128]{2,1,0:T(8,128)} %copy-done.1, f32[8,768,128]{2,1,0:T(8,128)} %bitcast.25), custom_call_target="tpu_custom_call" | custom-call | tf_op jit(solution)/shard_map/pallas_call | solution.py:76
  (19 shorter events, 0.2 us)
Async XLA Ops:
  26.1 23.2 %all-to-all-start.1 = ((f32[64,16,128]{2,1,0:T(8,128)}), f32[64,16,128]{2,1,0:T(8,128)}, u32[]{:S(2)}, u32[]{:S(2)}) async-start(f32[64,16,128]{2,1,0:T(8,128)} %shard_map.85), calls=%async_computation.1 | async-start | bytes 1048576 | tf_op jit(solution)/shard_map/all_to_all | solution.py:133
  31.0 0.9 copy-start.6
  31.0 1.9 %copy-start = (f32[8,6,128,128]{3,2,1,0:T(8,128)S(1)}, f32[8,6,128,128]{3,2,1,0:T(8,128)}, u32[]{:S(2)}) copy-start(f32[8,6,128,128]{3,2,1,0:T(8,128)} %param.9) | copy-start | bytes 9437188
  49.3 9.8 %copy-start.3 = (f32[16,1024]{1,0:T(8,128)S(1)}, f32[16,1024]{1,0:T(8,128)}, u32[]{:S(2)}) copy-start(f32[16,1024]{1,0:T(8,128)} %param.8) | copy-start | bytes 196612
  49.3 16.3 %copy-start.5 = (s32[3,1024]{1,0:T(4,128)S(1)}, s32[3,1024]{1,0:T(4,128)}, u32[]{:S(2)}) copy-start(s32[3,1024]{1,0:T(4,128)} %param.11) | copy-start | bytes 36868
  54.0 23.1 %all-to-all-start.2 = ((f32[64,16,128]{2,1,0:T(8,128)}), f32[64,16,128]{2,1,0:T(8,128)S(1)}, u32[]{:S(2)}, u32[]{:S(2)}) async-start(f32[64,16,128]{2,1,0:T(8,128)} %get-tuple-element.11), calls=%async_computation.2 | async-start | bytes 1048576 | tf_op jit(solution)/shard_map/all_to_all | solution.py:133
  59.0 14.7 %collective-permute-start.1 = (f32[16,128]{1,0:T(8,128)S(1)}, f32[16,128]{1,0:T(8,128)S(1)}, u32[]{:S(2)}, u32[]{:S(2)}) collective-permute-start(f32[16,128]{1,0:T(8,128)S(1)} %get-tuple-element.23), channel_id=1, source_target_pairs={{16,0},{32,16},{48,32},{64,48},{80,64},{96,80},{112,96},{128,112},... | collective-permute-start | bytes 24584 | tf_op jit(solution)/shard_map/ppermute | solution.py:25
  61.2 12.5 %collective-permute-start = (f32[16,128]{1,0:T(8,128)S(1)}, f32[16,128]{1,0:T(8,128)S(1)}, u32[]{:S(2)}, u32[]{:S(2)}) collective-permute-start(f32[16,128]{1,0:T(8,128)S(1)} %get-tuple-element.22), channel_id=1, source_target_pairs={{0,16},{16,32},{32,48},{48,64},{64,80},{80,96},{96,112},{112,128},... | collective-permute-start | bytes 24584 | tf_op jit(solution)/shard_map/ppermute | solution.py:22
  77.2 0.8 copy-start.2
  82.7 24.1 %all-to-all-start.3 = ((f32[64,16,128]{2,1,0:T(8,128)}), f32[64,16,128]{2,1,0:T(8,128)S(1)}, u32[]{:S(2)}, u32[]{:S(2)}) async-start(f32[64,16,128]{2,1,0:T(8,128)} %get-tuple-element.14), calls=%async_computation.3 | async-start | bytes 1048576 | tf_op jit(solution)/shard_map/all_to_all | solution.py:133
  87.6 18.5 %copy-start.4 = (f32[16,1024]{1,0:T(8,128)S(1)}, f32[16,1024]{1,0:T(8,128)}, u32[]{:S(2)}) copy-start(f32[16,1024]{1,0:T(8,128)} %get-tuple-element.6.f_ref) | copy-start | bytes 196612
  88.9 17.3 %collective-permute-start.2 = (f32[1,1024]{1,0:T(1,128)S(1)}, f32[1,1024]{1,0:T(1,128)S(1)}, u32[]{:S(2)}, u32[]{:S(2)}) collective-permute-start(f32[1,1024]{1,0:T(1,128)S(1)} %slice.33), channel_id=1, source_target_pairs={{0,1},{1,2},{2,3},{3,4},{4,5},{5,6},{6,7},{7,8},{8,9},{9,10},{10,1... | collective-permute-start | bytes 12296 | tf_op jit(solution)/shard_map/ppermute | solution.py:33
  106.8 0.8 copy-start.1

commit v4 on v3

--- a/solution.py
+++ b/solution.py
@@ -33,10 +33,22 @@
     return lax.ppermute(value, axis, pairs)
 
 
+def split_dot(a, b):
+    a_hi = a.astype(jnp.bfloat16)
+    a_lo = (a - a_hi.astype(jnp.float32)).astype(jnp.bfloat16)
+    b_hi = b.astype(jnp.bfloat16)
+    b_lo = (b - b_hi.astype(jnp.float32)).astype(jnp.bfloat16)
+
+    def part(x, y):
+        return jnp.dot(x, y, preferred_element_type=jnp.float32)
+
+    return part(a_hi, b_hi) + (part(a_hi, b_lo) + part(a_lo, b_hi))
+
+
 def substep(field, moment, got, tiles, pick, send_ids, scale, advance, send):
     slices, site_count = field.shape
     rows, kept = tiles.shape[0], tiles.shape[1] // TILE
-    slots = send_ids.shape[0]
+    slots = send_ids.shape[0] * send_ids.shape[1]
 
     def kernel(pick_ref, sid_ref, f_ref, p_ref, got_ref, tiles_ref, *refs):
         outs = list(refs)
@@ -46,11 +58,8 @@
         held = outs.pop(0) if send else None
         for r in range(rows):
             cols = slice(r * TILE, (r + 1) * TILE)
-            pieces = [f_ref[:, cols]] + [got_ref[pick_ref[r * kept + k]] for k in range(1, kept)]
-            acc = jnp.dot(
-                jnp.concatenate(pieces, axis=1), tiles_ref[r],
-                precision=lax.Precision.HIGHEST, preferred_element_type=jnp.float32,
-            )
+            pieces = [f_ref[:, cols]] + [got_ref[pick_ref[r, k]] for k in range(1, kept)]
+            acc = split_dot(jnp.concatenate(pieces, axis=1), tiles_ref[r])
             p_new = p_ref[:, cols] - scale * acc
             p_out[:, cols] = p_new
             if advance:
@@ -60,7 +69,7 @@
                     held[r] = f_new
         if send:
             def copy_one(s, carry):
-                send_out[s] = held[sid_ref[s]]
+                send_out[s] = held[sid_ref[s // 2, s % 2]]
                 return carry
             lax.fori_loop(0, slots, copy_one, 0)
 
@@ -85,14 +94,14 @@
 def gather_tiles(values, send_ids):
     slices, site_count = values.shape
     rows = site_count // TILE
-    slots = send_ids.shape[0]
+    slots = send_ids.shape[0] * send_ids.shape[1]
 
     def kernel(sid_ref, v_ref, send_out, held):
         for r in range(rows):
             held[r] = v_ref[:, r * TILE:(r + 1) * TILE]
 
         def copy_one(s, carry):
-            send_out[s] = held[sid_ref[s]]
+            send_out[s] = held[sid_ref[s // 2, s % 2]]
             return carry
         lax.fori_loop(0, slots, copy_one, 0)
 
@@ -123,11 +132,10 @@
     lo = jnp.clip(lo, 0, tile_rows - 1)
     hi = jnp.clip(hi, 0, tile_rows - 1)
     request = jnp.stack([lo, hi], axis=1)
-    wanted = lax.all_to_all(request, "space", 0, 0, tiled=True)
-    send_ids = wanted.reshape(-1)
+    send_ids = lax.all_to_all(request, "space", 0, 0)
     slot = jnp.where(local_id == lo[run_of], 0, 1)
 
-    pick = jnp.where(remote, run_of * 2 + slot, 0).reshape(-1)
+    pick = jnp.where(remote, run_of * 2 + slot, 0)
 
     def exchange(sent):
         return lax.all_to_all(sent, "space", 0, 0, tiled=True)

time: 114 us -> 113 us (level)
  the two profiles are of different devices: /device:TPU:1 before, /device:TPU:38 now
where the time goes in v4:
time: 113 us; the launch traced here: 112 us
  starting transfers between devices  38.4 us (34%)
  waiting for transfers between devices  33.5 us (30%)
  Pallas kernels  15.3 us (14%)
  blocking collectives  12.7 us (11%)
  local copies, waits for them, and re-layouts  7.13 us (6%)
  other arithmetic  2.92 us (3%)
    all_to_all x3, starting transfers between devices, exchange(): return lax.all_to_all(sent, 'space', 0, 0, tiled=True)  31.3 us
    ppermute x1, waiting for transfers between devices, from_behind(): return lax.ppermute(value, axis, pairs)  17.5 us
    pallas_call x3, Pallas kernels, substep(): pl.pallas_call(kernel, out_shape=tuple(out_shape), in_specs=[smem, smem,...  12.8 us
    all_to_all x1, blocking collectives, body(): send_ids = lax.all_to_all(request, 'space', 0, 0)  12.7 us
    all_to_all x3, waiting for transfers between devices, exchange(): return lax.all_to_all(sent, 'space', 0, 0, tiled=True)  9.52 us
    ppermute x1, waiting for transfers between devices, with_halo(): lax.ppermute(lax.slice_in_dim(block, 0, width, axis=dim), axis, backward)  6.5 us
    ppermute x1, starting transfers between devices, from_behind(): return lax.ppermute(value, axis, pairs)  2.75 us
    unnamed x17, local copies, waits for them, and re-layouts  2.7 us
  transfers between devices with their start and end apart: 6, of which 4 were waited for; matrix products, arithmetic and copies ran while one was open for 6% of the time, Pallas kernels for 0%

profile of v4, /device:TPU:38, one launch (start us, length us, event | category | flops | bytes accessed | tf_op | source)
XLA Modules:
  0.0 111.9 jit_solution(361036595408931648)
XLA Ops:
  0.6 0.7 compare_select_fusion
  1.3 0.1 copy.40
  1.4 0.1 copy.39
  1.5 0.1 copy.38
  1.6 0.1 select_reduce_fusion
  1.7 0.1 copy.41
  1.8 12.7 %all_to_all.26 = s32[32,1,2]{2,1,0:T(1,128)S(1)} all-to-all(s32[32,1,2]{2,1,0:T(1,128)S(1)} %copy.41), channel_id=1, replica_groups=mesh['space'=32,'tm'=16] {'space'}, dimensions={0} | all-to-all | bytes 512 | tf_op jit(solution)/shard_map/all_to_all | solution.py:135
  14.5 0.1 copy.42
  14.6 0.7 copy.46.sid_ref
  15.3 2.6 %shard_map.85 = f32[64,16,128]{2,1,0:T(8,128)} custom-call(s32[32,2]{1,0:T(8,128)} %copy.46.sid_ref, f32[16,1024]{1,0:T(8,128)} %f_ref.1), custom_call_target="tpu_custom_call" | custom-call | tf_op jit(solution)/shard_map/pallas_call | solution.py:108
  17.9 11.2 %all-to-all-start.1 = ((f32[64,16,128]{2,1,0:T(8,128)}), f32[64,16,128]{2,1,0:T(8,128)}, u32[]{:S(2)}, u32[]{:S(2)}) async-start(f32[64,16,128]{2,1,0:T(8,128)} %shard_map.85), calls=%async_computation.1 | async-start | bytes 1048576 | tf_op jit(solution)/shard_map/all_to_all | solution.py:141
  29.1 0.1 reshape.53
  29.2 0.0 copy-start
  29.2 0.8 gather_fusion
  30.0 0.1 reshape.52
  30.1 1.0 copy-done
  31.1 0.0 copy-start.6
  31.1 2.3 %copy.44 = f32[8,6,128,128]{3,2,1,0:T(8,128)} copy(f32[8,6,128,128]{2,3,1,0:T(8,128)S(1)} %bitcast.27) | data formatting | bytes 6291456 | tf_op jit(solution)/shard_map/transpose | solution.py:143
  33.4 0.0 copy-done.6
  33.4 0.6 add_select_fusion.3.pick_ref
  34.0 8.1 %all-to-all-done.1.got_ref = f32[64,16,128]{2,1,0:T(8,128)} async-done(((f32[64,16,128]{2,1,0:T(8,128)}), f32[64,16,128]{2,1,0:T(8,128)}, u32[]{:S(2)}, u32[]{:S(2)}) %all-to-all-start.1) | async-done | bytes 524320 | tf_op jit(solution)/shard_map/all_to_all | solution.py:141
  42.2 0.0 copy-start.3
  42.2 0.0 copy-start.5
  42.2 4.6 %shard_map.86 = (f32[16,1024]{1,0:T(8,128)}, f32[16,1024]{1,0:T(8,128)}, f32[64,16,128]{2,1,0:T(8,128)}) custom-call(s32[8,6]{1,0:T(8,128)} %add_select_fusion.3.pick_ref, s32[32,2]{1,0:T(8,128)} %copy.46.sid_ref, f32[16,1024]{1,0:T(8,128)} %f_ref.1, f32[16,1024]{1,0:T(8,128)} %p_ref.1, f32[64,16,128]{2,1,0:T(8,128)} %all-to-all-done.1.got_ref, ...), custom_call_target="tpu_custom_call" | custom-call | tf_op jit(solution)/shard_map/pallas_call | solution.py:85
  46.8 10.1 %all-to-all-start.2 = ((f32[64,16,128]{2,1,0:T(8,128)}), f32[64,16,128]{2,1,0:T(8,128)S(1)}, u32[]{:S(2)}, u32[]{:S(2)}) async-start(f32[64,16,128]{2,1,0:T(8,128)} %get-tuple-element.11), calls=%async_computation.2 | async-start | bytes 1048576 | tf_op jit(solution)/shard_map/all_to_all | solution.py:141
  56.9 0.0 copy-done.3
  57.0 2.2 %collective-permute-start.1 = (f32[16,128]{1,0:T(8,128)S(1)}, f32[16,128]{1,0:T(8,128)S(1)}, u32[]{:S(2)}, u32[]{:S(2)}) collective-permute-start(f32[16,128]{1,0:T(8,128)S(1)} %get-tuple-element.23), channel_id=1, source_target_pairs={{16,0},{32,16},{48,32},{64,48},{80,64},{96,80},{112,96},{128,112},... | collective-permute-start | bytes 24584 | tf_op jit(solution)/shard_map/ppermute | solution.py:25
  59.2 2.1 %collective-permute-start = (f32[16,128]{1,0:T(8,128)S(1)}, f32[16,128]{1,0:T(8,128)S(1)}, u32[]{:S(2)}, u32[]{:S(2)}) collective-permute-start(f32[16,128]{1,0:T(8,128)S(1)} %get-tuple-element.22), channel_id=1, source_target_pairs={{0,16},{16,32},{32,48},{48,64},{64,80},{80,96},{96,112},{112,128},... | collective-permute-start | bytes 24584 | tf_op jit(solution)/shard_map/ppermute | solution.py:22
  61.3 0.0 copy-done.5
  61.4 0.1 fusion.9
  61.4 0.7 convert_reduce_fusion
  62.1 6.5 %collective-permute-done.1 = f32[16,128]{1,0:T(8,128)S(1)} collective-permute-done((f32[16,128]{1,0:T(8,128)S(1)}, f32[16,128]{1,0:T(8,128)S(1)}, u32[]{:S(2)}, u32[]{:S(2)}) %collective-permute-start.1) | collective-permute-done | bytes 8224 | tf_op jit(solution)/shard_map/ppermute | solution.py:25
  68.7 0.0 collective-permute-done
  68.7 1.4 %all-to-all-done.2.got_ref = f32[64,16,128]{2,1,0:T(8,128)S(1)} async-done(((f32[64,16,128]{2,1,0:T(8,128)}), f32[64,16,128]{2,1,0:T(8,128)S(1)}, u32[]{:S(2)}, u32[]{:S(2)}) %all-to-all-start.2) | async-done | bytes 524320 | tf_op jit(solution)/shard_map/all_to_all | solution.py:141
  70.1 0.0 copy-start.2
  70.1 0.8 copy-done.2
  70.9 4.6 %shard_map.87 = (f32[16,1024]{1,0:T(8,128)}, f32[16,1024]{1,0:T(8,128)}, f32[64,16,128]{2,1,0:T(8,128)}) custom-call(s32[8,6]{1,0:T(8,128)} %add_select_fusion.3.pick_ref, s32[32,2]{1,0:T(8,128)} %copy.46.sid_ref, f32[16,1024]{1,0:T(8,128)} %get-tuple-element.9.f_ref, f32[16,1024]{1,0:T(8,128)} %get-tuple-element.10.p_ref, f32[64,16,128]{2,1,0:T(8,128)} %copy-done.2, ...), custom_call_target="tpu_custom_call" | custom-call | tf_op jit(solution)/shard_map/pallas_call | solution.py:85
  75.5 9.9 %all-to-all-start.3 = ((f32[64,16,128]{2,1,0:T(8,128)}), f32[64,16,128]{2,1,0:T(8,128)S(1)}, u32[]{:S(2)}, u32[]{:S(2)}) async-start(f32[64,16,128]{2,1,0:T(8,128)} %get-tuple-element.14), calls=%async_computation.3 | async-start | bytes 1048576 | tf_op jit(solution)/shard_map/all_to_all | solution.py:141
  85.4 0.0 copy-start.4
  85.5 1.1 fusion
  86.7 2.7 %collective-permute-start.2 = (f32[1,1024]{1,0:T(1,128)S(1)}, f32[1,1024]{1,0:T(1,128)S(1)}, u32[]{:S(2)}, u32[]{:S(2)}) collective-permute-start(f32[1,1024]{1,0:T(1,128)S(1)} %slice.33), channel_id=1, source_target_pairs={{0,1},{1,2},{2,3},{3,4},{4,5},{5,6},{6,7},{7,8},{8,9},{9,10},{10,1... | collective-permute-start | bytes 12296 | tf_op jit(solution)/shard_map/ppermute | solution.py:33
  89.4 17.5 %collective-permute-done.2 = f32[1,1024]{1,0:T(1,128)S(1)} collective-permute-done((f32[1,1024]{1,0:T(1,128)S(1)}, f32[1,1024]{1,0:T(1,128)S(1)}, u32[]{:S(2)}, u32[]{:S(2)}) %collective-permute-start.2) | collective-permute-done | bytes 4128 | tf_op jit(solution)/shard_map/ppermute | solution.py:33
  106.9 0.0 copy-done.4
  106.9 0.7 multiply_multiply_fusion
  107.5 0.0 all-to-all-done.3.got_ref
  107.6 0.0 copy-start.1
  107.6 0.8 copy-done.1
  108.4 3.5 %shard_map.88 = f32[16,1024]{1,0:T(8,128)} custom-call(s32[8,6]{1,0:T(8,128)} %add_select_fusion.3.pick_ref, s32[32,2]{1,0:T(8,128)} %copy.46.sid_ref, f32[16,1024]{1,0:T(8,128)} %get-tuple-element.6.f_ref, f32[16,1024]{1,0:T(8,128)} %get-tuple-element.13.p_ref, f32[64,16,128]{2,1,0:T(8,128)} %copy-done.1, f32[8,768,128]{2,1,0:T(8,128)} %bitcast.26), custom_call_target="tpu_custom_call" | custom-call | tf_op jit(solution)/shard_map/pallas_call | solution.py:85
  (18 shorter events, 0.2 us)
Async XLA Ops:
  17.9 24.3 %all-to-all-start.1 = ((f32[64,16,128]{2,1,0:T(8,128)}), f32[64,16,128]{2,1,0:T(8,128)}, u32[]{:S(2)}, u32[]{:S(2)}) async-start(f32[64,16,128]{2,1,0:T(8,128)} %shard_map.85), calls=%async_computation.1 | async-start | bytes 1048576 | tf_op jit(solution)/shard_map/all_to_all | solution.py:141
  29.2 1.9 %copy-start = (f32[8,6,128,128]{3,2,1,0:T(8,128)S(1)}, f32[8,6,128,128]{3,2,1,0:T(8,128)}, u32[]{:S(2)}) copy-start(f32[8,6,128,128]{3,2,1,0:T(8,128)} %param.9) | copy-start | bytes 9437188
  31.1 2.3 %copy-start.6 = (s32[8,6]{1,0:T(8,128)S(1)}, s32[8,6]{1,0:T(8,128)}, u32[]{:S(2)}) copy-start(s32[8,6]{1,0:T(8,128)} %param.10) | copy-start | bytes 580
  42.2 14.8 %copy-start.3 = (f32[16,1024]{1,0:T(8,128)S(1)}, f32[16,1024]{1,0:T(8,128)}, u32[]{:S(2)}) copy-start(f32[16,1024]{1,0:T(8,128)} %param.8) | copy-start | bytes 196612
  42.2 19.1 %copy-start.5 = (s32[3,1024]{1,0:T(4,128)S(1)}, s32[3,1024]{1,0:T(4,128)}, u32[]{:S(2)}) copy-start(s32[3,1024]{1,0:T(4,128)} %param.11) | copy-start | bytes 36868
  46.8 23.3 %all-to-all-start.2 = ((f32[64,16,128]{2,1,0:T(8,128)}), f32[64,16,128]{2,1,0:T(8,128)S(1)}, u32[]{:S(2)}, u32[]{:S(2)}) async-start(f32[64,16,128]{2,1,0:T(8,128)} %get-tuple-element.11), calls=%async_computation.2 | async-start | bytes 1048576 | tf_op jit(solution)/shard_map/all_to_all | solution.py:141
  57.0 11.7 %collective-permute-start.1 = (f32[16,128]{1,0:T(8,128)S(1)}, f32[16,128]{1,0:T(8,128)S(1)}, u32[]{:S(2)}, u32[]{:S(2)}) collective-permute-start(f32[16,128]{1,0:T(8,128)S(1)} %get-tuple-element.23), channel_id=1, source_target_pairs={{16,0},{32,16},{48,32},{64,48},{80,64},{96,80},{112,96},{128,112},... | collective-permute-start | bytes 24584 | tf_op jit(solution)/shard_map/ppermute | solution.py:25
  59.2 9.5 %collective-permute-start = (f32[16,128]{1,0:T(8,128)S(1)}, f32[16,128]{1,0:T(8,128)S(1)}, u32[]{:S(2)}, u32[]{:S(2)}) collective-permute-start(f32[16,128]{1,0:T(8,128)S(1)} %get-tuple-element.22), channel_id=1, source_target_pairs={{0,16},{16,32},{32,48},{48,64},{64,80},{80,96},{96,112},{112,128},... | collective-permute-start | bytes 24584 | tf_op jit(solution)/shard_map/ppermute | solution.py:22
  70.1 0.8 copy-start.2
  75.5 32.1 %all-to-all-start.3 = ((f32[64,16,128]{2,1,0:T(8,128)}), f32[64,16,128]{2,1,0:T(8,128)S(1)}, u32[]{:S(2)}, u32[]{:S(2)}) async-start(f32[64,16,128]{2,1,0:T(8,128)} %get-tuple-element.14), calls=%async_computation.3 | async-start | bytes 1048576 | tf_op jit(solution)/shard_map/all_to_all | solution.py:141
  85.4 21.5 %copy-start.4 = (f32[16,1024]{1,0:T(8,128)S(1)}, f32[16,1024]{1,0:T(8,128)}, u32[]{:S(2)}) copy-start(f32[16,1024]{1,0:T(8,128)} %get-tuple-element.6.f_ref) | copy-start | bytes 196612
  86.7 20.2 %collective-permute-start.2 = (f32[1,1024]{1,0:T(1,128)S(1)}, f32[1,1024]{1,0:T(1,128)S(1)}, u32[]{:S(2)}, u32[]{:S(2)}) collective-permute-start(f32[1,1024]{1,0:T(1,128)S(1)} %slice.33), channel_id=1, source_target_pairs={{0,1},{1,2},{2,3},{3,4},{4,5},{5,6},{6,7},{7,8},{8,9},{9,10},{10,1... | collective-permute-start | bytes 12296 | tf_op jit(solution)/shard_map/ppermute | solution.py:33
  107.6 0.8 copy-start.1

commit v5 on v4

--- a/solution.py
+++ b/solution.py
@@ -50,16 +50,28 @@
     rows, kept = tiles.shape[0], tiles.shape[1] // TILE
     slots = send_ids.shape[0] * send_ids.shape[1]
 
-    def kernel(pick_ref, sid_ref, f_ref, p_ref, got_ref, tiles_ref, *refs):
+    def kernel(pick_ref, sid_ref, f_ref, p_ref, got_ref, tiles_hbm, *refs):
         outs = list(refs)
         p_out = outs.pop(0)
         f_out = outs.pop(0) if advance else None
         send_out = outs.pop(0) if send else None
         held = outs.pop(0) if send else None
+        row_buf, row_sem = outs
+
+        def fetch(r):
+            return pltpu.make_async_copy(tiles_hbm.at[r], row_buf.at[r % 2], row_sem.at[r % 2])
+
+        pending = fetch(0)
+        pending.start()
         for r in range(rows):
+            current = pending
+            if r + 1 < rows:
+                pending = fetch(r + 1)
+                pending.start()
+            current.wait()
             cols = slice(r * TILE, (r + 1) * TILE)
             pieces = [f_ref[:, cols]] + [got_ref[pick_ref[r, k]] for k in range(1, kept)]
-            acc = split_dot(jnp.concatenate(pieces, axis=1), tiles_ref[r])
+            acc = split_dot(jnp.concatenate(pieces, axis=1), row_buf[r % 2])
             p_new = p_ref[:, cols] - scale * acc
             p_out[:, cols] = p_new
             if advance:
@@ -82,10 +94,12 @@
     if send:
         out_shape.append(jax.ShapeDtypeStruct((slots, slices, TILE), jnp.float32))
         scratch.append(pltpu.VMEM((rows, slices, TILE), jnp.float32))
+    scratch.append(pltpu.VMEM((2, kept * TILE, TILE), jnp.float32))
+    scratch.append(pltpu.SemaphoreType.DMA((2,)))
     return pl.pallas_call(
         kernel,
         out_shape=tuple(out_shape),
-        in_specs=[smem, smem, vmem, vmem, vmem, vmem],
+        in_specs=[smem, smem, vmem, vmem, vmem, pl.BlockSpec(memory_space=pl.ANY)],
         out_specs=tuple([vmem] * len(out_shape)),
         scratch_shapes=scratch,
     )(pick, send_ids, field, moment, got, tiles)

time: 113 us -> 121 us (1.071)
  Pallas kernels: 15.3 us -> 23.9 us
    pallas_call x3, Pallas kernels: 12.8 us -> 21.3 us  [substep(): pl.pallas_call(kernel, out_shape=tuple(out_shape), in_specs=[smem, smem,...]
  transfers between devices with their start and end apart: 6 -> 6, of which waited for: 4 -> 4; matrix products, arithmetic and copies ran while one was open for 6% -> 5% of each run, Pallas kernels for 0% -> 0%
where the time goes in v5:
time: 121 us
  starting transfers between devices  38.4 us (32%)
  waiting for transfers between devices  33.5 us (28%)
  Pallas kernels  23.9 us (20%)
  blocking collectives  12.7 us (10%)
  local copies, waits for them, and re-layouts  7.13 us (6%)
  other arithmetic  2.92 us (2%)
    all_to_all x3, starting transfers between devices, exchange(): return lax.all_to_all(sent, 'space', 0, 0, tiled=True)  31.3 us
    pallas_call x3, Pallas kernels, substep(): pl.pallas_call(kernel, out_shape=tuple(out_shape), in_specs=[smem, smem,...  21.3 us
    ppermute x1, waiting for transfers between devices, from_behind(): return lax.ppermute(value, axis, pairs)  17.5 us
    all_to_all x1, blocking collectives, body(): send_ids = lax.all_to_all(request, 'space', 0, 0)  12.7 us
    all_to_all x3, waiting for transfers between devices, exchange(): return lax.all_to_all(sent, 'space', 0, 0, tiled=True)  9.52 us
    ppermute x1, waiting for transfers between devices, with_halo(): lax.ppermute(lax.slice_in_dim(block, 0, width, axis=dim), axis, backward)  6.5 us
    ppermute x1, starting transfers between devices, from_behind(): return lax.ppermute(value, axis, pairs)  2.75 us
    unnamed x17, local copies, waits for them, and re-layouts  2.7 us
  transfers between devices with their start and end apart: 6, of which 4 were waited for; matrix products, arithmetic and copies ran while one was open for 5% of the time, Pallas kernels for 0%

profile of v5, /device:TPU:38, one launch (start us, length us, event | category | flops | bytes accessed | tf_op | source)
XLA Modules:
  0.0 120.5 jit_solution(9366366543245155218)
XLA Ops:
  0.6 0.7 compare_select_fusion
  1.3 0.1 copy.40
  1.4 0.1 copy.39
  1.5 0.1 copy.38
  1.6 0.1 select_reduce_fusion
  1.7 0.1 copy.41
  1.8 12.7 %all_to_all.26 = s32[32,1,2]{2,1,0:T(1,128)S(1)} all-to-all(s32[32,1,2]{2,1,0:T(1,128)S(1)} %copy.41), channel_id=1, replica_groups=mesh['space'=32,'tm'=16] {'space'}, dimensions={0} | all-to-all | bytes 512 | tf_op jit(solution)/shard_map/all_to_all | solution.py:149
  14.5 0.1 copy.42
  14.6 0.7 copy.46.sid_ref
  15.3 2.6 %shard_map.85 = f32[64,16,128]{2,1,0:T(8,128)} custom-call(s32[32,2]{1,0:T(8,128)} %copy.46.sid_ref, f32[16,1024]{1,0:T(8,128)} %f_ref.1), custom_call_target="tpu_custom_call" | custom-call | tf_op jit(solution)/shard_map/pallas_call | solution.py:122
  17.9 11.2 %all-to-all-start.1 = ((f32[64,16,128]{2,1,0:T(8,128)}), f32[64,16,128]{2,1,0:T(8,128)}, u32[]{:S(2)}, u32[]{:S(2)}) async-start(f32[64,16,128]{2,1,0:T(8,128)} %shard_map.85), calls=%async_computation.1 | async-start | bytes 1048576 | tf_op jit(solution)/shard_map/all_to_all | solution.py:155
  29.1 0.1 reshape.53
  29.2 0.0 copy-start
  29.2 0.8 gather_fusion
  30.0 0.1 reshape.52
  30.1 1.0 copy-done
  31.1 0.0 copy-start.6
  31.1 2.3 %copy.44 = f32[8,6,128,128]{3,2,1,0:T(8,128)} copy(f32[8,6,128,128]{2,3,1,0:T(8,128)S(1)} %bitcast.27) | data formatting | bytes 6291456 | tf_op jit(solution)/shard_map/transpose | solution.py:157
  33.4 0.0 copy-done.6
  33.4 0.6 add_select_fusion.3.pick_ref
  34.0 8.1 %all-to-all-done.1.got_ref = f32[64,16,128]{2,1,0:T(8,128)} async-done(((f32[64,16,128]{2,1,0:T(8,128)}), f32[64,16,128]{2,1,0:T(8,128)}, u32[]{:S(2)}, u32[]{:S(2)}) %all-to-all-start.1) | async-done | bytes 524320 | tf_op jit(solution)/shard_map/all_to_all | solution.py:155
  42.2 0.0 copy-start.3
  42.2 0.0 copy-start.5
  42.2 7.5 %shard_map.86 = (f32[16,1024]{1,0:T(8,128)}, f32[16,1024]{1,0:T(8,128)}, f32[64,16,128]{2,1,0:T(8,128)}) custom-call(s32[8,6]{1,0:T(8,128)} %add_select_fusion.3.pick_ref, s32[32,2]{1,0:T(8,128)} %copy.46.sid_ref, f32[16,1024]{1,0:T(8,128)} %f_ref.1, f32[16,1024]{1,0:T(8,128)} %p_ref.1, f32[64,16,128]{2,1,0:T(8,128)} %all-to-all-done.1.got_ref, ...), custom_call_target="tpu_custom_call" | custom-call | tf_op jit(solution)/shard_map/pallas_call | solution.py:99
  49.7 10.1 %all-to-all-start.2 = ((f32[64,16,128]{2,1,0:T(8,128)}), f32[64,16,128]{2,1,0:T(8,128)S(1)}, u32[]{:S(2)}, u32[]{:S(2)}) async-start(f32[64,16,128]{2,1,0:T(8,128)} %get-tuple-element.11), calls=%async_computation.2 | async-start | bytes 1048576 | tf_op jit(solution)/shard_map/all_to_all | solution.py:155
  59.8 0.0 copy-done.3
  59.8 2.2 %collective-permute-start.1 = (f32[16,128]{1,0:T(8,128)S(1)}, f32[16,128]{1,0:T(8,128)S(1)}, u32[]{:S(2)}, u32[]{:S(2)}) collective-permute-start(f32[16,128]{1,0:T(8,128)S(1)} %get-tuple-element.23), channel_id=1, source_target_pairs={{16,0},{32,16},{48,32},{64,48},{80,64},{96,80},{112,96},{128,112},... | collective-permute-start | bytes 24584 | tf_op jit(solution)/shard_map/ppermute | solution.py:25
  62.1 2.1 %collective-permute-start = (f32[16,128]{1,0:T(8,128)S(1)}, f32[16,128]{1,0:T(8,128)S(1)}, u32[]{:S(2)}, u32[]{:S(2)}) collective-permute-start(f32[16,128]{1,0:T(8,128)S(1)} %get-tuple-element.22), channel_id=1, source_target_pairs={{0,16},{16,32},{32,48},{48,64},{64,80},{80,96},{96,112},{112,128},... | collective-permute-start | bytes 24584 | tf_op jit(solution)/shard_map/ppermute | solution.py:22
  64.2 0.0 copy-done.5
  64.2 0.1 fusion.9
  64.3 0.7 convert_reduce_fusion
  65.0 6.5 %collective-permute-done.1 = f32[16,128]{1,0:T(8,128)S(1)} collective-permute-done((f32[16,128]{1,0:T(8,128)S(1)}, f32[16,128]{1,0:T(8,128)S(1)}, u32[]{:S(2)}, u32[]{:S(2)}) %collective-permute-start.1) | collective-permute-done | bytes 8224 | tf_op jit(solution)/shard_map/ppermute | solution.py:25
  71.5 0.0 collective-permute-done
  71.6 1.4 %all-to-all-done.2.got_ref = f32[64,16,128]{2,1,0:T(8,128)S(1)} async-done(((f32[64,16,128]{2,1,0:T(8,128)}), f32[64,16,128]{2,1,0:T(8,128)S(1)}, u32[]{:S(2)}, u32[]{:S(2)}) %all-to-all-start.2) | async-done | bytes 524320 | tf_op jit(solution)/shard_map/all_to_all | solution.py:155
  72.9 0.0 copy-start.2
  72.9 0.8 copy-done.2
  73.7 7.5 %shard_map.87 = (f32[16,1024]{1,0:T(8,128)}, f32[16,1024]{1,0:T(8,128)}, f32[64,16,128]{2,1,0:T(8,128)}) custom-call(s32[8,6]{1,0:T(8,128)} %add_select_fusion.3.pick_ref, s32[32,2]{1,0:T(8,128)} %copy.46.sid_ref, f32[16,1024]{1,0:T(8,128)} %get-tuple-element.9.f_ref, f32[16,1024]{1,0:T(8,128)} %get-tuple-element.10.p_ref, f32[64,16,128]{2,1,0:T(8,128)} %copy-done.2, ...), custom_call_target="tpu_custom_call" | custom-call | tf_op jit(solution)/shard_map/pallas_call | solution.py:99
  81.2 10.0 %all-to-all-start.3 = ((f32[64,16,128]{2,1,0:T(8,128)}), f32[64,16,128]{2,1,0:T(8,128)S(1)}, u32[]{:S(2)}, u32[]{:S(2)}) async-start(f32[64,16,128]{2,1,0:T(8,128)} %get-tuple-element.14), calls=%async_computation.3 | async-start | bytes 1048576 | tf_op jit(solution)/shard_map/all_to_all | solution.py:155
  91.2 0.0 copy-start.4
  91.3 1.1 fusion
  92.4 2.7 %collective-permute-start.2 = (f32[1,1024]{1,0:T(1,128)S(1)}, f32[1,1024]{1,0:T(1,128)S(1)}, u32[]{:S(2)}, u32[]{:S(2)}) collective-permute-start(f32[1,1024]{1,0:T(1,128)S(1)} %slice.33), channel_id=1, source_target_pairs={{0,1},{1,2},{2,3},{3,4},{4,5},{5,6},{6,7},{7,8},{8,9},{9,10},{10,1... | collective-permute-start | bytes 12296 | tf_op jit(solution)/shard_map/ppermute | solution.py:33
  95.2 17.5 %collective-permute-done.2 = f32[1,1024]{1,0:T(1,128)S(1)} collective-permute-done((f32[1,1024]{1,0:T(1,128)S(1)}, f32[1,1024]{1,0:T(1,128)S(1)}, u32[]{:S(2)}, u32[]{:S(2)}) %collective-permute-start.2) | collective-permute-done | bytes 4128 | tf_op jit(solution)/shard_map/ppermute | solution.py:33
  112.6 0.0 copy-done.4
  112.6 0.7 multiply_multiply_fusion
  113.3 0.0 all-to-all-done.3.got_ref
  113.3 0.0 copy-start.1
  113.3 0.8 copy-done.1
  114.1 6.4 %shard_map.88 = f32[16,1024]{1,0:T(8,128)} custom-call(s32[8,6]{1,0:T(8,128)} %add_select_fusion.3.pick_ref, s32[32,2]{1,0:T(8,128)} %copy.46.sid_ref, f32[16,1024]{1,0:T(8,128)} %get-tuple-element.6.f_ref, f32[16,1024]{1,0:T(8,128)} %get-tuple-element.13.p_ref, f32[64,16,128]{2,1,0:T(8,128)} %copy-done.1, f32[8,768,128]{2,1,0:T(8,128)} %bitcast.26), custom_call_target="tpu_custom_call" | custom-call | tf_op jit(solution)/shard_map/pallas_call | solution.py:99
  (18 shorter events, 0.2 us)
Async XLA Ops:
  17.9 24.3 %all-to-all-start.1 = ((f32[64,16,128]{2,1,0:T(8,128)}), f32[64,16,128]{2,1,0:T(8,128)}, u32[]{:S(2)}, u32[]{:S(2)}) async-start(f32[64,16,128]{2,1,0:T(8,128)} %shard_map.85), calls=%async_computation.1 | async-start | bytes 1048576 | tf_op jit(solution)/shard_map/all_to_all | solution.py:155
  29.2 1.9 %copy-start = (f32[8,6,128,128]{3,2,1,0:T(8,128)S(1)}, f32[8,6,128,128]{3,2,1,0:T(8,128)}, u32[]{:S(2)}) copy-start(f32[8,6,128,128]{3,2,1,0:T(8,128)} %param.9) | copy-start | bytes 9437188
  31.1 2.3 %copy-start.6 = (s32[8,6]{1,0:T(8,128)S(1)}, s32[8,6]{1,0:T(8,128)}, u32[]{:S(2)}) copy-start(s32[8,6]{1,0:T(8,128)} %param.10) | copy-start | bytes 580
  42.2 17.6 %copy-start.3 = (f32[16,1024]{1,0:T(8,128)S(1)}, f32[16,1024]{1,0:T(8,128)}, u32[]{:S(2)}) copy-start(f32[16,1024]{1,0:T(8,128)} %param.8) | copy-start | bytes 196612
  42.2 22.0 %copy-start.5 = (s32[3,1024]{1,0:T(4,128)S(1)}, s32[3,1024]{1,0:T(4,128)}, u32[]{:S(2)}) copy-start(s32[3,1024]{1,0:T(4,128)} %param.11) | copy-start | bytes 36868
  49.7 23.3 %all-to-all-start.2 = ((f32[64,16,128]{2,1,0:T(8,128)}), f32[64,16,128]{2,1,0:T(8,128)S(1)}, u32[]{:S(2)}, u32[]{:S(2)}) async-start(f32[64,16,128]{2,1,0:T(8,128)} %get-tuple-element.11), calls=%async_computation.2 | async-start | bytes 1048576 | tf_op jit(solution)/shard_map/all_to_all | solution.py:155
  59.8 11.7 %collective-permute-start.1 = (f32[16,128]{1,0:T(8,128)S(1)}, f32[16,128]{1,0:T(8,128)S(1)}, u32[]{:S(2)}, u32[]{:S(2)}) collective-permute-start(f32[16,128]{1,0:T(8,128)S(1)} %get-tuple-element.23), channel_id=1, source_target_pairs={{16,0},{32,16},{48,32},{64,48},{80,64},{96,80},{112,96},{128,112},... | collective-permute-start | bytes 24584 | tf_op jit(solution)/shard_map/ppermute | solution.py:25
  62.1 9.5 %collective-permute-start = (f32[16,128]{1,0:T(8,128)S(1)}, f32[16,128]{1,0:T(8,128)S(1)}, u32[]{:S(2)}, u32[]{:S(2)}) collective-permute-start(f32[16,128]{1,0:T(8,128)S(1)} %get-tuple-element.22), channel_id=1, source_target_pairs={{0,16},{16,32},{32,48},{48,64},{64,80},{80,96},{96,112},{112,128},... | collective-permute-start | bytes 24584 | tf_op jit(solution)/shard_map/ppermute | solution.py:22
  72.9 0.8 copy-start.2
  81.2 32.1 %all-to-all-start.3 = ((f32[64,16,128]{2,1,0:T(8,128)}), f32[64,16,128]{2,1,0:T(8,128)S(1)}, u32[]{:S(2)}, u32[]{:S(2)}) async-start(f32[64,16,128]{2,1,0:T(8,128)} %get-tuple-element.14), calls=%async_computation.3 | async-start | bytes 1048576 | tf_op jit(solution)/shard_map/all_to_all | solution.py:155
  91.2 21.5 %copy-start.4 = (f32[16,1024]{1,0:T(8,128)S(1)}, f32[16,1024]{1,0:T(8,128)}, u32[]{:S(2)}) copy-start(f32[16,1024]{1,0:T(8,128)} %get-tuple-element.6.f_ref) | copy-start | bytes 196612
  92.4 20.2 %collective-permute-start.2 = (f32[1,1024]{1,0:T(1,128)S(1)}, f32[1,1024]{1,0:T(1,128)S(1)}, u32[]{:S(2)}, u32[]{:S(2)}) collective-permute-start(f32[1,1024]{1,0:T(1,128)S(1)} %slice.33), channel_id=1, source_target_pairs={{0,1},{1,2},{2,3},{3,4},{4,5},{5,6},{6,7},{7,8},{8,9},{9,10},{10,1... | collective-permute-start | bytes 12296 | tf_op jit(solution)/shard_map/ppermute | solution.py:33
  113.3 0.8 copy-start.1

commit v6 on v4

--- a/solution.py
+++ b/solution.py
@@ -91,29 +91,6 @@
     )(pick, send_ids, field, moment, got, tiles)
 
 
-def gather_tiles(values, send_ids):
-    slices, site_count = values.shape
-    rows = site_count // TILE
-    slots = send_ids.shape[0] * send_ids.shape[1]
-
-    def kernel(sid_ref, v_ref, send_out, held):
-        for r in range(rows):
-            held[r] = v_ref[:, r * TILE:(r + 1) * TILE]
-
-        def copy_one(s, carry):
-            send_out[s] = held[sid_ref[s // 2, s % 2]]
-            return carry
-        lax.fori_loop(0, slots, copy_one, 0)
-
-    return pl.pallas_call(
-        kernel,
-        out_shape=jax.ShapeDtypeStruct((slots, slices, TILE), jnp.float32),
-        in_specs=[pl.BlockSpec(memory_space=pltpu.SMEM), pl.BlockSpec(memory_space=pltpu.VMEM)],
-        out_specs=pl.BlockSpec(memory_space=pltpu.VMEM),
-        scratch_shapes=[pltpu.VMEM((rows, slices, TILE), jnp.float32)],
-    )(send_ids, values)
-
-
 def body(field, momentum, solution, tiles, columns, neighbours):
     slices = field.shape[0]
     tile_rows = tiles.shape[0]
@@ -141,7 +118,9 @@
         return lax.all_to_all(sent, "space", 0, 0, tiled=True)
 
     tiles = tiles.transpose(0, 1, 3, 2).reshape(tile_rows, kept * TILE, TILE)
-    got = exchange(gather_tiles(field, send_ids))
+    own = field.reshape(slices, tile_rows, TILE)
+    first = jnp.take(own, send_ids.reshape(-1), axis=1, mode="clip").transpose(1, 0, 2)
+    got = exchange(first)
     moment, field_one, sent = substep(field, momentum, got, tiles, pick, send_ids, 0.5 * step_size, True, True)
     got = exchange(sent)
     moment, field_two, sent = substep(field_one, moment, got, tiles, pick, send_ids, step_size, True, True)

time: 113 us -> 113 us (level)
  the two profiles are of different devices: /device:TPU:38 before, /device:TPU:1 now
where the time goes in v6:
time: 113 us; the launch traced here: 111 us
  waiting for transfers between devices  46.8 us (41%)
  starting transfers between devices  34.7 us (31%)
  Pallas kernels  12.8 us (11%)
  local copies, waits for them, and re-layouts  10.6 us (9%)
  other arithmetic  3.62 us (3%)
    all_to_all x3, waiting for transfers between devices, exchange(): return lax.all_to_all(sent, 'space', 0, 0, tiled=True)  16.1 us
    ppermute x1, waiting for transfers between devices, from_behind(): return lax.ppermute(value, axis, pairs)  14.9 us
    all_to_all x3, starting transfers between devices, exchange(): return lax.all_to_all(sent, 'space', 0, 0, tiled=True)  14.7 us
    pallas_call x3, Pallas kernels, substep(): pl.pallas_call(kernel, out_shape=tuple(out_shape), in_specs=[smem, smem,...  12.8 us
    all_to_all x1, starting transfers between devices, body(): send_ids = lax.all_to_all(request, 'space', 0, 0)  11.2 us
    all_to_all x1, waiting for transfers between devices, body(): send_ids = lax.all_to_all(request, 'space', 0, 0)  8.43 us
    ppermute x1, waiting for transfers between devices, with_halo(): lax.ppermute(lax.slice_in_dim(block, 0, width, axis=dim), axis, backward)  7.35 us
    ppermute x1, starting transfers between devices, with_halo(): lax.ppermute(lax.slice_in_dim(block, block.shape[dim] - width, None, axis...  4.32 us
  transfers between devices with their start and end apart: 7, of which 5 were waited for; matrix products, arithmetic and copies ran while one was open for 7% of the time, Pallas kernels for 0%

profile of v6, /device:TPU:1, one launch (start us, length us, event | category | flops | bytes accessed | tf_op | source)
XLA Modules:
  0.0 110.5 jit_solution(10218894509489227627)
XLA Ops:
  0.6 0.7 compare_select_fusion
  1.3 0.1 copy.51
  1.4 0.1 copy.50
  1.5 0.1 copy.49
  1.6 0.1 select_reduce_fusion
  1.7 0.7 copy.52
  2.4 11.2 %all-to-all-start = ((s32[32,1,2]{2,1,0:T(1,128)}), s32[32,1,2]{2,1,0:T(1,128)S(1)}, u32[]{:S(2)}, u32[]{:S(2)}) async-start(s32[32,1,2]{2,1,0:T(1,128)} %copy.52), calls=%async_computation | async-start | bytes 32768 | tf_op jit(solution)/shard_map/all_to_all | solution.py:112
  13.7 0.8 copy_bitcast_fusion
  14.5 8.4 %all-to-all-done = s32[32,1,2]{2,1,0:T(1,128)S(1)} async-done(((s32[32,1,2]{2,1,0:T(1,128)}), s32[32,1,2]{2,1,0:T(1,128)S(1)}, u32[]{:S(2)}, u32[]{:S(2)}) %all-to-all-start) | async-done | bytes 288 | tf_op jit(solution)/shard_map/all_to_all | solution.py:112
  22.9 0.5 broadcast.102
  23.5 0.7 reduce.3
  24.2 0.1 reshape.68
  24.3 1.4 %gather_fusion.1 = f32[64,16,128]{2,1,0:T(8,128)} fusion(f32[16,8,128]{2,0,1:T(8,128)S(1)} %copy_bitcast_fusion, s32[1024]{0:T(1024)S(1)} %pad_clamp_fusion), kind=kCustom, calls=%fused_computation.1 | custom fusion | bytes 1048832 | tf_op jit(solution)/shard_map/jit(_take)/gather | solution.py:122
  25.7 4.9 %all-to-all-start.1 = ((f32[64,16,128]{2,1,0:T(8,128)}), f32[64,16,128]{2,1,0:T(8,128)}, u32[]{:S(2)}, u32[]{:S(2)}) async-start(f32[64,16,128]{2,1,0:T(8,128)} %gather_fusion.1), calls=%async_computation.1 | async-start | bytes 1048576 | tf_op jit(solution)/shard_map/all_to_all | solution.py:118
  30.5 0.1 reshape.60
  30.6 0.0 copy-start
  30.6 0.8 gather_fusion
  31.4 0.1 reshape.59
  31.5 1.0 copy-done
  32.5 0.0 copy-start.6
  32.5 2.3 %copy.55 = f32[8,6,128,128]{3,2,1,0:T(8,128)} copy(f32[8,6,128,128]{2,3,1,0:T(8,128)S(1)} %bitcast.32) | data formatting | bytes 6291456 | tf_op jit(solution)/shard_map/transpose | solution.py:120
  34.9 0.0 copy-done.6
  34.9 0.6 add_select_fusion.3.pick_ref
  35.5 0.1 copy.53
  35.5 0.7 copy.57.sid_ref
  36.2 12.7 %all-to-all-done.1.got_ref = f32[64,16,128]{2,1,0:T(8,128)} async-done(((f32[64,16,128]{2,1,0:T(8,128)}), f32[64,16,128]{2,1,0:T(8,128)}, u32[]{:S(2)}, u32[]{:S(2)}) %all-to-all-start.1) | async-done | bytes 524320 | tf_op jit(solution)/shard_map/all_to_all | solution.py:118
  48.9 0.0 copy-start.3
  48.9 0.0 copy-start.5
  48.9 4.6 %shard_map.85 = (f32[16,1024]{1,0:T(8,128)}, f32[16,1024]{1,0:T(8,128)}, f32[64,16,128]{2,1,0:T(8,128)}) custom-call(s32[8,6]{1,0:T(8,128)} %add_select_fusion.3.pick_ref, s32[32,2]{1,0:T(8,128)} %copy.57.sid_ref, f32[16,1024]{1,0:T(8,128)} %f_ref.1, f32[16,1024]{1,0:T(8,128)} %p_ref.1, f32[64,16,128]{2,1,0:T(8,128)} %all-to-all-done.1.got_ref, ...), custom_call_target="tpu_custom_call" | custom-call | tf_op jit(solution)/shard_map/pallas_call | solution.py:85
  53.5 5.0 %all-to-all-start.2 = ((f32[64,16,128]{2,1,0:T(8,128)}), f32[64,16,128]{2,1,0:T(8,128)S(1)}, u32[]{:S(2)}, u32[]{:S(2)}) async-start(f32[64,16,128]{2,1,0:T(8,128)} %get-tuple-element.11), calls=%async_computation.2 | async-start | bytes 1048576 | tf_op jit(solution)/shard_map/all_to_all | solution.py:118
  58.5 0.0 copy-done.3
  58.5 2.1 %collective-permute-start.1 = (f32[16,128]{1,0:T(8,128)S(1)}, f32[16,128]{1,0:T(8,128)S(1)}, u32[]{:S(2)}, u32[]{:S(2)}) collective-permute-start(f32[16,128]{1,0:T(8,128)S(1)} %get-tuple-element.23), channel_id=1, source_target_pairs={{16,0},{32,16},{48,32},{64,48},{80,64},{96,80},{112,96},{128,112},... | collective-permute-start | bytes 24584 | tf_op jit(solution)/shard_map/ppermute | solution.py:25
  60.6 4.3 %collective-permute-start = (f32[16,128]{1,0:T(8,128)S(1)}, f32[16,128]{1,0:T(8,128)S(1)}, u32[]{:S(2)}, u32[]{:S(2)}) collective-permute-start(f32[16,128]{1,0:T(8,128)S(1)} %get-tuple-element.22), channel_id=1, source_target_pairs={{0,16},{16,32},{32,48},{48,64},{64,80},{80,96},{96,112},{112,128},... | collective-permute-start | bytes 24584 | tf_op jit(solution)/shard_map/ppermute | solution.py:22
  65.0 0.0 copy-done.5
  65.0 0.1 fusion.9
  65.1 0.7 convert_reduce_fusion
  65.8 7.4 %collective-permute-done.1 = f32[16,128]{1,0:T(8,128)S(1)} collective-permute-done((f32[16,128]{1,0:T(8,128)S(1)}, f32[16,128]{1,0:T(8,128)S(1)}, u32[]{:S(2)}, u32[]{:S(2)}) %collective-permute-start.1) | collective-permute-done | bytes 8224 | tf_op jit(solution)/shard_map/ppermute | solution.py:25
  73.2 0.0 collective-permute-done
  73.2 3.4 %all-to-all-done.2.got_ref = f32[64,16,128]{2,1,0:T(8,128)S(1)} async-done(((f32[64,16,128]{2,1,0:T(8,128)}), f32[64,16,128]{2,1,0:T(8,128)S(1)}, u32[]{:S(2)}, u32[]{:S(2)}) %all-to-all-start.2) | async-done | bytes 524320 | tf_op jit(solution)/shard_map/all_to_all | solution.py:118
  76.6 0.0 copy-start.2
  76.6 0.8 copy-done.2
  77.4 4.6 %shard_map.86 = (f32[16,1024]{1,0:T(8,128)}, f32[16,1024]{1,0:T(8,128)}, f32[64,16,128]{2,1,0:T(8,128)}) custom-call(s32[8,6]{1,0:T(8,128)} %add_select_fusion.3.pick_ref, s32[32,2]{1,0:T(8,128)} %copy.57.sid_ref, f32[16,1024]{1,0:T(8,128)} %get-tuple-element.9.f_ref, f32[16,1024]{1,0:T(8,128)} %get-tuple-element.10.p_ref, f32[64,16,128]{2,1,0:T(8,128)} %copy-done.2, ...), custom_call_target="tpu_custom_call" | custom-call | tf_op jit(solution)/shard_map/pallas_call | solution.py:85
  82.0 4.9 %all-to-all-start.3 = ((f32[64,16,128]{2,1,0:T(8,128)}), f32[64,16,128]{2,1,0:T(8,128)S(1)}, u32[]{:S(2)}, u32[]{:S(2)}) async-start(f32[64,16,128]{2,1,0:T(8,128)} %get-tuple-element.14), calls=%async_computation.3 | async-start | bytes 1048576 | tf_op jit(solution)/shard_map/all_to_all | solution.py:118
  86.9 0.0 copy-start.4
  87.0 1.1 fusion
  88.2 2.4 %collective-permute-start.2 = (f32[1,1024]{1,0:T(1,128)S(1)}, f32[1,1024]{1,0:T(1,128)S(1)}, u32[]{:S(2)}, u32[]{:S(2)}) collective-permute-start(f32[1,1024]{1,0:T(1,128)S(1)} %slice.35), channel_id=1, source_target_pairs={{0,1},{1,2},{2,3},{3,4},{4,5},{5,6},{6,7},{7,8},{8,9},{9,10},{10,1... | collective-permute-start | bytes 12296 | tf_op jit(solution)/shard_map/ppermute | solution.py:33
  90.6 14.9 %collective-permute-done.2 = f32[1,1024]{1,0:T(1,128)S(1)} collective-permute-done((f32[1,1024]{1,0:T(1,128)S(1)}, f32[1,1024]{1,0:T(1,128)S(1)}, u32[]{:S(2)}, u32[]{:S(2)}) %collective-permute-start.2) | collective-permute-done | bytes 4128 | tf_op jit(solution)/shard_map/ppermute | solution.py:33
  105.5 0.0 copy-done.4
  105.5 0.7 multiply_multiply_fusion
  106.2 0.0 all-to-all-done.3.got_ref
  106.2 0.0 copy-start.1
  106.2 0.8 copy-done.1
  107.0 3.5 %shard_map.87 = f32[16,1024]{1,0:T(8,128)} custom-call(s32[8,6]{1,0:T(8,128)} %add_select_fusion.3.pick_ref, s32[32,2]{1,0:T(8,128)} %copy.57.sid_ref, f32[16,1024]{1,0:T(8,128)} %get-tuple-element.6.f_ref, f32[16,1024]{1,0:T(8,128)} %get-tuple-element.13.p_ref, f32[64,16,128]{2,1,0:T(8,128)} %copy-done.1, f32[8,768,128]{2,1,0:T(8,128)} %bitcast.31), custom_call_target="tpu_custom_call" | custom-call | tf_op jit(solution)/shard_map/pallas_call | solution.py:85
  (19 shorter events, 0.2 us)
Async XLA Ops:
  2.4 20.5 %all-to-all-start = ((s32[32,1,2]{2,1,0:T(1,128)}), s32[32,1,2]{2,1,0:T(1,128)S(1)}, u32[]{:S(2)}, u32[]{:S(2)}) async-start(s32[32,1,2]{2,1,0:T(1,128)} %copy.52), calls=%async_computation | async-start | bytes 32768 | tf_op jit(solution)/shard_map/all_to_all | solution.py:112
  25.7 23.2 %all-to-all-start.1 = ((f32[64,16,128]{2,1,0:T(8,128)}), f32[64,16,128]{2,1,0:T(8,128)}, u32[]{:S(2)}, u32[]{:S(2)}) async-start(f32[64,16,128]{2,1,0:T(8,128)} %gather_fusion.1), calls=%async_computation.1 | async-start | bytes 1048576 | tf_op jit(solution)/shard_map/all_to_all | solution.py:118
  30.6 1.9 %copy-start = (f32[8,6,128,128]{3,2,1,0:T(8,128)S(1)}, f32[8,6,128,128]{3,2,1,0:T(8,128)}, u32[]{:S(2)}) copy-start(f32[8,6,128,128]{3,2,1,0:T(8,128)} %param.9) | copy-start | bytes 9437188
  32.5 2.3 %copy-start.6 = (s32[8,6]{1,0:T(8,128)S(1)}, s32[8,6]{1,0:T(8,128)}, u32[]{:S(2)}) copy-start(s32[8,6]{1,0:T(8,128)} %param.10) | copy-start | bytes 580
  48.9 9.6 %copy-start.3 = (f32[16,1024]{1,0:T(8,128)S(1)}, f32[16,1024]{1,0:T(8,128)}, u32[]{:S(2)}) copy-start(f32[16,1024]{1,0:T(8,128)} %param.8) | copy-start | bytes 196612
  48.9 16.1 %copy-start.5 = (s32[3,1024]{1,0:T(4,128)S(1)}, s32[3,1024]{1,0:T(4,128)}, u32[]{:S(2)}) copy-start(s32[3,1024]{1,0:T(4,128)} %param.11) | copy-start | bytes 36868
  53.5 23.1 %all-to-all-start.2 = ((f32[64,16,128]{2,1,0:T(8,128)}), f32[64,16,128]{2,1,0:T(8,128)S(1)}, u32[]{:S(2)}, u32[]{:S(2)}) async-start(f32[64,16,128]{2,1,0:T(8,128)} %get-tuple-element.11), calls=%async_computation.2 | async-start | bytes 1048576 | tf_op jit(solution)/shard_map/all_to_all | solution.py:118
  58.5 14.7 %collective-permute-start.1 = (f32[16,128]{1,0:T(8,128)S(1)}, f32[16,128]{1,0:T(8,128)S(1)}, u32[]{:S(2)}, u32[]{:S(2)}) collective-permute-start(f32[16,128]{1,0:T(8,128)S(1)} %get-tuple-element.23), channel_id=1, source_target_pairs={{16,0},{32,16},{48,32},{64,48},{80,64},{96,80},{112,96},{128,112},... | collective-permute-start | bytes 24584 | tf_op jit(solution)/shard_map/ppermute | solution.py:25
  60.6 12.5 %collective-permute-start = (f32[16,128]{1,0:T(8,128)S(1)}, f32[16,128]{1,0:T(8,128)S(1)}, u32[]{:S(2)}, u32[]{:S(2)}) collective-permute-start(f32[16,128]{1,0:T(8,128)S(1)} %get-tuple-element.22), channel_id=1, source_target_pairs={{0,16},{16,32},{32,48},{48,64},{64,80},{80,96},{96,112},{112,128},... | collective-permute-start | bytes 24584 | tf_op jit(solution)/shard_map/ppermute | solution.py:22
  76.6 0.8 copy-start.2
  82.0 24.1 %all-to-all-start.3 = ((f32[64,16,128]{2,1,0:T(8,128)}), f32[64,16,128]{2,1,0:T(8,128)S(1)}, u32[]{:S(2)}, u32[]{:S(2)}) async-start(f32[64,16,128]{2,1,0:T(8,128)} %get-tuple-element.14), calls=%async_computation.3 | async-start | bytes 1048576 | tf_op jit(solution)/shard_map/all_to_all | solution.py:118
  86.9 18.5 %copy-start.4 = (f32[16,1024]{1,0:T(8,128)S(1)}, f32[16,1024]{1,0:T(8,128)}, u32[]{:S(2)}) copy-start(f32[16,1024]{1,0:T(8,128)} %get-tuple-element.6.f_ref) | copy-start | bytes 196612
  88.2 17.3 %collective-permute-start.2 = (f32[1,1024]{1,0:T(1,128)S(1)}, f32[1,1024]{1,0:T(1,128)S(1)}, u32[]{:S(2)}, u32[]{:S(2)}) collective-permute-start(f32[1,1024]{1,0:T(1,128)S(1)} %slice.35), channel_id=1, source_target_pairs={{0,1},{1,2},{2,3},{3,4},{4,5},{5,6},{6,7},{7,8},{8,9},{9,10},{10,1... | collective-permute-start | bytes 12296 | tf_op jit(solution)/shard_map/ppermute | solution.py:33
  106.2 0.8 copy-start.1

commit v7 on v6

--- a/solution.py
+++ b/solution.py
@@ -118,15 +118,6 @@
         return lax.all_to_all(sent, "space", 0, 0, tiled=True)
 
     tiles = tiles.transpose(0, 1, 3, 2).reshape(tile_rows, kept * TILE, TILE)
-    own = field.reshape(slices, tile_rows, TILE)
-    first = jnp.take(own, send_ids.reshape(-1), axis=1, mode="clip").transpose(1, 0, 2)
-    got = exchange(first)
-    moment, field_one, sent = substep(field, momentum, got, tiles, pick, send_ids, 0.5 * step_size, True, True)
-    got = exchange(sent)
-    moment, field_two, sent = substep(field_one, moment, got, tiles, pick, send_ids, step_size, True, True)
-    got = exchange(sent)
-    (moment,) = substep(field_two, moment, got, tiles, pick, send_ids, 0.5 * step_size, False, False)
-
     total_sites = site_count * space_count
     first_site = me * site_count
     lookup = (neighbours - first_site + TILE) % total_sites
@@ -141,7 +132,17 @@
     windows = jnp.concatenate([parts[:, :-2], parts[:, 1:-1], parts[:, 2:]], axis=2)
     beside = jnp.einsum("tbj,bji->tbi", windows, adjacency, precision=lax.Precision.HIGHEST)
     hopped = solution + hop_kappa * beside.reshape(slices, site_count)
+    own = field.reshape(slices, tile_rows, TILE)
+    first = jnp.take(own, send_ids.reshape(-1), axis=1, mode="clip").transpose(1, 0, 2)
+    got = exchange(first)
+    moment, field_one, sent = substep(field, momentum, got, tiles, pick, send_ids, 0.5 * step_size, True, True)
     arrived = from_behind(hopped[-1:], "tm", 1)
+    got = exchange(sent)
+    moment, field_two, sent = substep(field_one, moment, got, tiles, pick, send_ids, step_size, True, True)
+    sent, arrived = lax.optimization_barrier((sent, arrived))
+    got = exchange(sent)
+    (moment,) = substep(field_two, moment, got, tiles, pick, send_ids, 0.5 * step_size, False, False)
+
     earlier = jnp.concatenate([parity_sign * arrived, hopped[:-1]], axis=0)
     link_factor = jnp.exp(coupling * field_two)
     shifted = solution - link_factor * earlier

time: 113 us -> 111 us (0.982); the launches traced: 111 us -> 110 us
  waiting for transfers between devices: 46.8 us -> 43.3 us
  starting transfers between devices: 34.7 us -> 37.4 us
    all_to_all x3, waiting for transfers between devices: 16.1 us -> 34.9 us  [exchange(): return lax.all_to_all(sent, 'space', 0, 0, tiled=True)]
    ppermute x1, waiting for transfers between devices: 14.9 us -> 0.01 us  [from_behind(): return lax.ppermute(value, axis, pairs)]
    ppermute x1, waiting for transfers between devices: 7.35 us -> 0.01 us  [with_halo(): lax.ppermute(lax.slice_in_dim(block, 0, width, axis=dim), axis, backward)]
    all_to_all x3, starting transfers between devices: 14.7 us -> 17.6 us  [exchange(): return lax.all_to_all(sent, 'space', 0, 0, tiled=True)]
    unnamed x17 -> x15, local copies, waits for them, and re-layouts: 2.72 us -> 2.6 us
  transfers between devices with their start and end apart: 7 -> 7, of which waited for: 5 -> 4; matrix products, arithmetic and copies ran while one was open for 7% -> 8% of each run, Pallas kernels for 0% -> 8%
where the time goes in v7:
time: 111 us; the launch traced here: 110 us
  waiting for transfers between devices  43.3 us (39%)
  starting transfers between devices  37.4 us (34%)
  Pallas kernels  12.7 us (11%)
  local copies, waits for them, and re-layouts  10.5 us (9%)
  other arithmetic  4.49 us (4%)
    all_to_all x3, waiting for transfers between devices, exchange(): return lax.all_to_all(sent, 'space', 0, 0, tiled=True)  34.9 us
    all_to_all x3, starting transfers between devices, exchange(): return lax.all_to_all(sent, 'space', 0, 0, tiled=True)  17.6 us
    pallas_call x3, Pallas kernels, substep(): pl.pallas_call(kernel, out_shape=tuple(out_shape), in_specs=[smem, smem,...  12.7 us
    all_to_all x1, starting transfers between devices, body(): send_ids = lax.all_to_all(request, 'space', 0, 0)  11.2 us
    all_to_all x1, waiting for transfers between devices, body(): send_ids = lax.all_to_all(request, 'space', 0, 0)  8.43 us
    ppermute x1, starting transfers between devices, with_halo(): lax.ppermute(lax.slice_in_dim(block, block.shape[dim] - width, None, axis...  4.45 us
    unnamed x15, local copies, waits for them, and re-layouts  2.6 us
    transpose x1, local copies, waits for them, and re-layouts, body(): tiles = tiles.transpose(0, 1, 3, 2).reshape(tile_rows, kept * TILE, TILE)  2.32 us
  transfers between devices with their start and end apart: 7, of which 4 were waited for; matrix products, arithmetic and copies ran while one was open for 8% of the time, Pallas kernels for 8%

profile of v7, /device:TPU:1, one launch (start us, length us, event | category | flops | bytes accessed | tf_op | source)
XLA Modules:
  0.0 110.5 jit_solution(2705886471883234958)
XLA Ops:
  0.6 0.0 copy-start.3
  0.6 0.7 compare_select_fusion
  1.4 0.1 copy.50
  1.5 0.1 copy.49
  1.6 0.1 copy.51
  1.6 0.1 select_reduce_fusion
  1.8 0.7 copy.52
  2.5 11.2 %all-to-all-start = ((s32[32,1,2]{2,1,0:T(1,128)}), s32[32,1,2]{2,1,0:T(1,128)S(1)}, u32[]{:S(2)}, u32[]{:S(2)}) async-start(s32[32,1,2]{2,1,0:T(1,128)} %copy.52), calls=%async_computation | async-start | bytes 32768 | tf_op jit(solution)/shard_map/all_to_all | solution.py:112
  13.7 0.8 copy_bitcast_fusion
  14.6 8.4 %all-to-all-done = s32[32,1,2]{2,1,0:T(1,128)S(1)} async-done(((s32[32,1,2]{2,1,0:T(1,128)}), s32[32,1,2]{2,1,0:T(1,128)S(1)}, u32[]{:S(2)}, u32[]{:S(2)}) %all-to-all-start) | async-done | bytes 288 | tf_op jit(solution)/shard_map/all_to_all | solution.py:112
  23.0 0.5 broadcast.102
  23.5 0.7 reduce.3
  24.2 0.1 reshape.68
  24.3 1.4 %gather_fusion.1 = f32[64,16,128]{2,1,0:T(8,128)} fusion(f32[16,8,128]{2,0,1:T(8,128)S(1)} %copy_bitcast_fusion, s32[1024]{0:T(1024)S(1)} %pad_clamp_fusion), kind=kCustom, calls=%fused_computation.1 | custom fusion | bytes 1048832 | tf_op jit(solution)/shard_map/jit(_take)/gather | solution.py:136
  25.7 4.8 %all-to-all-start.1 = ((f32[64,16,128]{2,1,0:T(8,128)}), f32[64,16,128]{2,1,0:T(8,128)}, u32[]{:S(2)}, u32[]{:S(2)}) async-start(f32[64,16,128]{2,1,0:T(8,128)} %gather_fusion.1), calls=%async_computation.1 | async-start | bytes 1048576 | tf_op jit(solution)/shard_map/all_to_all | solution.py:118
  30.6 0.0 copy-done.3
  30.6 4.4 %collective-permute-start = (f32[16,128]{1,0:T(8,128)S(1)}, f32[16,128]{1,0:T(8,128)S(1)}, u32[]{:S(2)}, u32[]{:S(2)}) collective-permute-start(f32[16,128]{1,0:T(8,128)S(1)} %get-tuple-element.26), channel_id=1, source_target_pairs={{0,16},{16,32},{32,48},{48,64},{64,80},{80,96},{96,112},{112,128},... | collective-permute-start | bytes 24584 | tf_op jit(solution)/shard_map/ppermute | solution.py:22
  35.1 1.9 %collective-permute-start.1 = (f32[16,128]{1,0:T(8,128)S(1)}, f32[16,128]{1,0:T(8,128)S(1)}, u32[]{:S(2)}, u32[]{:S(2)}) collective-permute-start(f32[16,128]{1,0:T(8,128)S(1)} %get-tuple-element.27), channel_id=1, source_target_pairs={{16,0},{32,16},{48,32},{64,48},{80,64},{96,80},{112,96},{128,112},... | collective-permute-start | bytes 24584 | tf_op jit(solution)/shard_map/ppermute | solution.py:25
  37.0 0.1 reshape.60
  37.1 0.0 copy-start.4
  37.1 0.0 copy-start
  37.1 0.8 gather_fusion
  37.9 0.1 reshape.59
  38.0 0.0 copy-done.4
  38.0 0.1 fusion.9
  38.1 0.9 copy-done
  39.0 0.0 copy-start.5
  39.0 2.3 %copy.55 = f32[8,6,128,128]{3,2,1,0:T(8,128)} copy(f32[8,6,128,128]{2,3,1,0:T(8,128)S(1)} %bitcast.32) | data formatting | bytes 6291456 | tf_op jit(solution)/shard_map/transpose | solution.py:120
  41.3 0.0 copy-done.5
  41.3 0.6 add_select_fusion.3.pick_ref
  41.9 0.1 copy.53
  42.0 0.7 copy.57.sid_ref
  42.7 6.3 %all-to-all-done.1.got_ref = f32[64,16,128]{2,1,0:T(8,128)} async-done(((f32[64,16,128]{2,1,0:T(8,128)}), f32[64,16,128]{2,1,0:T(8,128)}, u32[]{:S(2)}, u32[]{:S(2)}) %all-to-all-start.1) | async-done | bytes 524320 | tf_op jit(solution)/shard_map/all_to_all | solution.py:118
  49.0 4.6 %shard_map.85 = (f32[16,1024]{1,0:T(8,128)}, f32[16,1024]{1,0:T(8,128)}, f32[64,16,128]{2,1,0:T(8,128)}) custom-call(s32[8,6]{1,0:T(8,128)} %add_select_fusion.3.pick_ref, s32[32,2]{1,0:T(8,128)} %copy.57.sid_ref, f32[16,1024]{1,0:T(8,128)} %f_ref.1, f32[16,1024]{1,0:T(8,128)} %p_ref.1, f32[64,16,128]{2,1,0:T(8,128)} %all-to-all-done.1.got_ref, ...), custom_call_target="tpu_custom_call" | custom-call | tf_op jit(solution)/shard_map/pallas_call | solution.py:85
  53.6 5.0 %all-to-all-start.2 = ((f32[64,16,128]{2,1,0:T(8,128)}), f32[64,16,128]{2,1,0:T(8,128)S(1)}, u32[]{:S(2)}, u32[]{:S(2)}) async-start(f32[64,16,128]{2,1,0:T(8,128)} %get-tuple-element.13), calls=%async_computation.2 | async-start | bytes 1048576 | tf_op jit(solution)/shard_map/all_to_all | solution.py:118
  58.6 0.7 convert_reduce_fusion
  59.3 0.0 collective-permute-done
  59.3 0.0 collective-permute-done.1
  59.5 1.1 fusion
  60.6 2.2 %collective-permute-start.2 = (f32[1,1024]{1,0:T(1,128)S(1)}, f32[1,1024]{1,0:T(1,128)S(1)}, u32[]{:S(2)}, u32[]{:S(2)}) collective-permute-start(f32[1,1024]{1,0:T(1,128)S(1)} %slice.35), channel_id=1, source_target_pairs={{0,1},{1,2},{2,3},{3,4},{4,5},{5,6},{6,7},{7,8},{8,9},{9,10},{10,1... | collective-permute-start | bytes 12296 | tf_op jit(solution)/shard_map/ppermute | solution.py:33
  62.8 13.9 %all-to-all-done.2.got_ref = f32[64,16,128]{2,1,0:T(8,128)S(1)} async-done(((f32[64,16,128]{2,1,0:T(8,128)}), f32[64,16,128]{2,1,0:T(8,128)S(1)}, u32[]{:S(2)}, u32[]{:S(2)}) %all-to-all-start.2) | async-done | bytes 524320 | tf_op jit(solution)/shard_map/all_to_all | solution.py:118
  76.7 0.0 copy-start.2
  76.7 0.8 copy-done.2
  77.5 4.6 %shard_map.86 = (f32[16,1024]{1,0:T(8,128)}, f32[16,1024]{1,0:T(8,128)}, f32[64,16,128]{2,1,0:T(8,128)}) custom-call(s32[8,6]{1,0:T(8,128)} %add_select_fusion.3.pick_ref, s32[32,2]{1,0:T(8,128)} %copy.57.sid_ref, f32[16,1024]{1,0:T(8,128)} %get-tuple-element.11.f_ref, f32[16,1024]{1,0:T(8,128)} %get-tuple-element.12.p_ref, f32[64,16,128]{2,1,0:T(8,128)} %copy-done.2, ...), custom_call_target="tpu_custom_call" | custom-call | tf_op jit(solution)/shard_map/pallas_call | solution.py:85
  82.1 0.0 collective-permute-done.2
  82.1 7.8 %all-to-all-start.3 = ((f32[64,16,128]{2,1,0:T(8,128)}), f32[64,16,128]{2,1,0:T(8,128)S(1)}, u32[]{:S(2)}, u32[]{:S(2)}) async-start(f32[64,16,128]{2,1,0:T(8,128)} %get-tuple-element.17), calls=%async_computation.3 | async-start | bytes 1048576 | tf_op jit(solution)/shard_map/all_to_all | solution.py:118
  89.9 1.5 %multiply_multiply_fusion = f32[16,1024]{1,0:T(8,128)} fusion(f32[16,1024]{1,0:T(8,128)S(1)} %copy-done.3, f32[15,1024]{1,0:T(8,128)S(1)} %bitcast.33, f32[1,1024]{1,0:T(1,128)S(1)} %broadcast_multiply_fusion, f32[16,1024]{1,0:T(8,128)} %get-tuple-element.8.f_ref), kind=kLoop, calls=%fused_computation.15 | loop fusion | flops 114688 | bytes 262144 | tf_op jit(solution)/shard_map/mul | solution.py:149
  91.4 14.7 %all-to-all-done.3.got_ref = f32[64,16,128]{2,1,0:T(8,128)S(1)} async-done(((f32[64,16,128]{2,1,0:T(8,128)}), f32[64,16,128]{2,1,0:T(8,128)S(1)}, u32[]{:S(2)}, u32[]{:S(2)}) %all-to-all-start.3) | async-done | bytes 524320 | tf_op jit(solution)/shard_map/all_to_all | solution.py:118
  106.1 0.0 copy-start.1
  106.1 0.8 copy-done.1
  106.9 3.5 %shard_map.87 = f32[16,1024]{1,0:T(8,128)} custom-call(s32[8,6]{1,0:T(8,128)} %add_select_fusion.3.pick_ref, s32[32,2]{1,0:T(8,128)} %copy.57.sid_ref, f32[16,1024]{1,0:T(8,128)} %get-tuple-element.8.f_ref, f32[16,1024]{1,0:T(8,128)} %get-tuple-element.15.p_ref, f32[64,16,128]{2,1,0:T(8,128)} %copy-done.1, f32[8,768,128]{2,1,0:T(8,128)} %bitcast.31), custom_call_target="tpu_custom_call" | custom-call | tf_op jit(solution)/shard_map/pallas_call | solution.py:85
  (19 shorter events, 0.2 us)
Async XLA Ops:
  0.6 30.0 %copy-start.3 = (f32[16,1024]{1,0:T(8,128)S(1)}, f32[16,1024]{1,0:T(8,128)}, u32[]{:S(2)}) copy-start(f32[16,1024]{1,0:T(8,128)} %param.8) | copy-start | bytes 196612
  2.5 20.5 %all-to-all-start = ((s32[32,1,2]{2,1,0:T(1,128)}), s32[32,1,2]{2,1,0:T(1,128)S(1)}, u32[]{:S(2)}, u32[]{:S(2)}) async-start(s32[32,1,2]{2,1,0:T(1,128)} %copy.52), calls=%async_computation | async-start | bytes 32768 | tf_op jit(solution)/shard_map/all_to_all | solution.py:112
  25.7 23.3 %all-to-all-start.1 = ((f32[64,16,128]{2,1,0:T(8,128)}), f32[64,16,128]{2,1,0:T(8,128)}, u32[]{:S(2)}, u32[]{:S(2)}) async-start(f32[64,16,128]{2,1,0:T(8,128)} %gather_fusion.1), calls=%async_computation.1 | async-start | bytes 1048576 | tf_op jit(solution)/shard_map/all_to_all | solution.py:118
  30.6 28.7 %collective-permute-start = (f32[16,128]{1,0:T(8,128)S(1)}, f32[16,128]{1,0:T(8,128)S(1)}, u32[]{:S(2)}, u32[]{:S(2)}) collective-permute-start(f32[16,128]{1,0:T(8,128)S(1)} %get-tuple-element.26), channel_id=1, source_target_pairs={{0,16},{16,32},{32,48},{48,64},{64,80},{80,96},{96,112},{112,128},... | collective-permute-start | bytes 24584 | tf_op jit(solution)/shard_map/ppermute | solution.py:22
  35.1 24.3 %collective-permute-start.1 = (f32[16,128]{1,0:T(8,128)S(1)}, f32[16,128]{1,0:T(8,128)S(1)}, u32[]{:S(2)}, u32[]{:S(2)}) collective-permute-start(f32[16,128]{1,0:T(8,128)S(1)} %get-tuple-element.27), channel_id=1, source_target_pairs={{16,0},{32,16},{48,32},{64,48},{80,64},{96,80},{112,96},{128,112},... | collective-permute-start | bytes 24584 | tf_op jit(solution)/shard_map/ppermute | solution.py:25
  37.1 0.9 copy-start.4
  37.1 1.9 %copy-start = (f32[8,6,128,128]{3,2,1,0:T(8,128)S(1)}, f32[8,6,128,128]{3,2,1,0:T(8,128)}, u32[]{:S(2)}) copy-start(f32[8,6,128,128]{3,2,1,0:T(8,128)} %param.9) | copy-start | bytes 9437188
  39.0 2.3 %copy-start.5 = (s32[8,6]{1,0:T(8,128)S(1)}, s32[8,6]{1,0:T(8,128)}, u32[]{:S(2)}) copy-start(s32[8,6]{1,0:T(8,128)} %param.10) | copy-start | bytes 580
  53.6 23.1 %all-to-all-start.2 = ((f32[64,16,128]{2,1,0:T(8,128)}), f32[64,16,128]{2,1,0:T(8,128)S(1)}, u32[]{:S(2)}, u32[]{:S(2)}) async-start(f32[64,16,128]{2,1,0:T(8,128)} %get-tuple-element.13), calls=%async_computation.2 | async-start | bytes 1048576 | tf_op jit(solution)/shard_map/all_to_all | solution.py:118
  60.6 21.5 %collective-permute-start.2 = (f32[1,1024]{1,0:T(1,128)S(1)}, f32[1,1024]{1,0:T(1,128)S(1)}, u32[]{:S(2)}, u32[]{:S(2)}) collective-permute-start(f32[1,1024]{1,0:T(1,128)S(1)} %slice.35), channel_id=1, source_target_pairs={{0,1},{1,2},{2,3},{3,4},{4,5},{5,6},{6,7},{7,8},{8,9},{9,10},{10,1... | collective-permute-start | bytes 12296 | tf_op jit(solution)/shard_map/ppermute | solution.py:33
  76.7 0.8 copy-start.2
  82.1 24.0 %all-to-all-start.3 = ((f32[64,16,128]{2,1,0:T(8,128)}), f32[64,16,128]{2,1,0:T(8,128)S(1)}, u32[]{:S(2)}, u32[]{:S(2)}) async-start(f32[64,16,128]{2,1,0:T(8,128)} %get-tuple-element.17), calls=%async_computation.3 | async-start | bytes 1048576 | tf_op jit(solution)/shard_map/all_to_all | solution.py:118
  106.1 0.8 copy-start.1

commit v8 on v7

--- a/solution.py
+++ b/solution.py
@@ -102,14 +102,17 @@
     run_of = columns // tile_rows
     local_id = columns % tile_rows
     remote = run_of != me
-    runs = jnp.arange(space_count, dtype=jnp.int32)
-    hit = remote[:, :, None] & (run_of[:, :, None] == runs[None, None, :])
-    lo = jnp.min(jnp.where(hit, local_id[:, :, None], tile_rows), axis=(0, 1))
-    hi = jnp.max(jnp.where(hit, local_id[:, :, None], -1), axis=(0, 1))
+    runs = lax.broadcasted_iota(jnp.int32, (space_count, tile_rows * kept), 0)
+    flat_run = jnp.where(remote, run_of, -1).reshape(1, -1)
+    flat_id = local_id.reshape(1, -1)
+    hit = flat_run == runs
+    lo = jnp.min(jnp.where(hit, flat_id, tile_rows), axis=1)
+    hi = jnp.max(jnp.where(hit, flat_id, -1), axis=1)
     lo = jnp.clip(lo, 0, tile_rows - 1)
     hi = jnp.clip(hi, 0, tile_rows - 1)
-    request = jnp.stack([lo, hi], axis=1)
-    send_ids = lax.all_to_all(request, "space", 0, 0)
+    lane = lax.broadcasted_iota(jnp.int32, (space_count, TILE), 1)
+    request = jnp.where(lane == 0, lo[:, None], jnp.where(lane == 1, hi[:, None], 0))
+    send_ids = lax.all_to_all(request, "space", 0, 0, tiled=True)[:, :2]
     slot = jnp.where(local_id == lo[run_of], 0, 1)
 
     pick = jnp.where(remote, run_of * 2 + slot, 0)

time: 111 us -> 109 us (0.982)
  local copies, waits for them, and re-layouts: 10.5 us -> 8.43 us
    all_to_all x4 -> x0, local copies, waits for them, and re-layouts: 1.97 us -> none  [body(): send_ids = lax.all_to_all(request, 'space', 0, 0)]
    unnamed x15 -> x17, local copies, waits for them, and re-layouts: 2.6 us -> 2.56 us
  transfers between devices with their start and end apart: 7 -> 7, of which waited for: 4 -> 4; matrix products, arithmetic and copies ran while one was open for 8% -> 8% of each run, Pallas kernels for 8% -> 9%
where the time goes in v8:
time: 109 us; the launch traced here: 108 us
  waiting for transfers between devices  44.4 us (41%)
  starting transfers between devices  36.4 us (33%)
  Pallas kernels  12.8 us (12%)
  local copies, waits for them, and re-layouts  8.43 us (8%)
  other arithmetic  4.53 us (4%)
  matrix products  1.09 us (1%)
    all_to_all x3, waiting for transfers between devices, exchange(): return lax.all_to_all(sent, 'space', 0, 0, tiled=True)  35.9 us
    all_to_all x3, starting transfers between devices, exchange(): return lax.all_to_all(sent, 'space', 0, 0, tiled=True)  16.9 us
    pallas_call x3, Pallas kernels, substep(): pl.pallas_call(kernel, out_shape=tuple(out_shape), in_specs=[smem, smem,...  12.8 us
    all_to_all x1, starting transfers between devices, body(): send_ids = lax.all_to_all(request, 'space', 0, 0, tiled=True)[:, :2]  11.2 us
    all_to_all x1, waiting for transfers between devices, body(): send_ids = lax.all_to_all(request, 'space', 0, 0, tiled=True)[:, :2]  8.43 us
    ppermute x1, starting transfers between devices, with_halo(): lax.ppermute(lax.slice_in_dim(block, block.shape[dim] - width, None, axis...  4.45 us
    unnamed x17, local copies, waits for them, and re-layouts  2.56 us
    transpose x1, local copies, waits for them, and re-layouts, body(): tiles = tiles.transpose(0, 1, 3, 2).reshape(tile_rows, kept * TILE, TILE)  2.34 us
  transfers between devices with their start and end apart: 7, of which 4 were waited for; matrix products, arithmetic and copies ran while one was open for 8% of the time, Pallas kernels for 9%

profile of v8, /device:TPU:1, one launch (start us, length us, event | category | flops | bytes accessed | tf_op | source)
XLA Modules:
  0.0 108.4 jit_solution(15130669245549219255)
XLA Ops:
  0.6 0.0 copy-start.3
  0.7 0.7 compare_select_fusion
  1.4 0.1 eq.49
  1.4 0.1 broadcast_in_dim.57
  1.5 0.1 select_reduce_fusion
  1.7 0.7 broadcast_select_fusion.1
  2.4 11.2 %all-to-all-start = ((s32[32,1,128]{2,1,0:T(1,128)}), s32[32,1,128]{2,1,0:T(1,128)S(1)}, u32[]{:S(2)}, u32[]{:S(2)}) async-start(s32[32,1,128]{2,1,0:T(1,128)} %broadcast_select_fusion.1), calls=%async_computation | async-start | bytes 32768 | tf_op jit(solution)/shard_map/all_to_all | solution.py:115
  13.6 0.8 copy_bitcast_fusion
  14.5 8.4 %all-to-all-done = s32[32,1,128]{2,1,0:T(1,128)S(1)} async-done(((s32[32,1,128]{2,1,0:T(1,128)}), s32[32,1,128]{2,1,0:T(1,128)S(1)}, u32[]{:S(2)}, u32[]{:S(2)}) %all-to-all-start) | async-done | bytes 16416 | tf_op jit(solution)/shard_map/all_to_all | solution.py:115
  22.9 0.0 copy-start.4
  22.9 0.1 reshape.128
  23.0 1.4 %gather_fusion.1 = f32[64,16,128]{2,1,0:T(8,128)} fusion(f32[16,8,128]{2,0,1:T(8,128)S(1)} %copy_bitcast_fusion, s32[1024]{0:T(1024)S(1)} %pad_clamp_fusion), kind=kCustom, calls=%fused_computation.1 | custom fusion | bytes 1048832 | tf_op jit(solution)/shard_map/jit(_take)/gather | solution.py:139
  24.5 4.8 %all-to-all-start.1 = ((f32[64,16,128]{2,1,0:T(8,128)}), f32[64,16,128]{2,1,0:T(8,128)}, u32[]{:S(2)}, u32[]{:S(2)}) async-start(f32[64,16,128]{2,1,0:T(8,128)} %gather_fusion.1), calls=%async_computation.1 | async-start | bytes 1048576 | tf_op jit(solution)/shard_map/all_to_all | solution.py:121
  29.3 0.0 copy-done.3
  29.3 4.4 %collective-permute-start = (f32[16,128]{1,0:T(8,128)S(1)}, f32[16,128]{1,0:T(8,128)S(1)}, u32[]{:S(2)}, u32[]{:S(2)}) collective-permute-start(f32[16,128]{1,0:T(8,128)S(1)} %get-tuple-element.24), channel_id=1, source_target_pairs={{0,16},{16,32},{32,48},{48,64},{64,80},{80,96},{96,112},{112,128},... | collective-permute-start | bytes 24584 | tf_op jit(solution)/shard_map/ppermute | solution.py:22
  33.8 1.9 %collective-permute-start.1 = (f32[16,128]{1,0:T(8,128)S(1)}, f32[16,128]{1,0:T(8,128)S(1)}, u32[]{:S(2)}, u32[]{:S(2)}) collective-permute-start(f32[16,128]{1,0:T(8,128)S(1)} %get-tuple-element.25), channel_id=1, source_target_pairs={{16,0},{32,16},{48,32},{64,48},{80,64},{96,80},{112,96},{128,112},... | collective-permute-start | bytes 24584 | tf_op jit(solution)/shard_map/ppermute | solution.py:25
  35.7 0.1 reshape.120
  35.8 0.0 copy-start.5
  35.8 0.0 copy-start
  35.8 0.8 gather_fusion
  36.6 0.0 copy-done.4
  36.6 0.1 reshape.119
  36.7 0.0 copy-done.5
  36.7 0.1 fusion.8
  36.8 0.9 copy-done
  37.7 0.0 copy-start.6
  37.7 2.3 %copy.33 = f32[8,6,128,128]{3,2,1,0:T(8,128)} copy(f32[8,6,128,128]{2,3,1,0:T(8,128)S(1)} %bitcast.27) | data formatting | bytes 6291456 | tf_op jit(solution)/shard_map/transpose | solution.py:123
  40.1 0.0 copy-done.6
  40.1 0.6 compare_select_fusion.1.pick_ref
  40.7 7.1 %all-to-all-done.1.got_ref = f32[64,16,128]{2,1,0:T(8,128)} async-done(((f32[64,16,128]{2,1,0:T(8,128)}), f32[64,16,128]{2,1,0:T(8,128)}, u32[]{:S(2)}, u32[]{:S(2)}) %all-to-all-start.1) | async-done | bytes 524320 | tf_op jit(solution)/shard_map/all_to_all | solution.py:121
  47.7 4.6 %shard_map.85 = (f32[16,1024]{1,0:T(8,128)}, f32[16,1024]{1,0:T(8,128)}, f32[64,16,128]{2,1,0:T(8,128)}) custom-call(s32[8,6]{1,0:T(8,128)} %compare_select_fusion.1.pick_ref, s32[32,2]{1,0:T(8,128)} %bitcast.29, f32[16,1024]{1,0:T(8,128)} %f_ref.1, f32[16,1024]{1,0:T(8,128)} %p_ref.1, f32[64,16,128]{2,1,0:T(8,128)} %all-to-all-done.1.got_ref, ...), custom_call_target="tpu_custom_call" | custom-call | tf_op jit(solution)/shard_map/pallas_call | solution.py:85
  52.3 5.0 %all-to-all-start.2 = ((f32[64,16,128]{2,1,0:T(8,128)}), f32[64,16,128]{2,1,0:T(8,128)S(1)}, u32[]{:S(2)}, u32[]{:S(2)}) async-start(f32[64,16,128]{2,1,0:T(8,128)} %get-tuple-element.13), calls=%async_computation.2 | async-start | bytes 1048576 | tf_op jit(solution)/shard_map/all_to_all | solution.py:121
  57.3 0.7 convert_reduce_fusion
  58.0 0.0 collective-permute-done
  58.1 0.0 collective-permute-done.1
  58.2 1.1 %fusion = f32[8,2,8,128]{3,2,1,0:T(8,128)S(1)} fusion(f32[8,384,128]{2,1,0:T(8,128)S(1)} %convert_reduce_fusion, f32[16,8,128]{2,0,1:T(8,128)S(1)} %copy.41, f32[16,8,128]{2,0,1:T(8,128)S(1)} %copy.40, f32[16,8,128]{2,0,1:T(8,128)S(1)} %copy.39), kind=kOutput, calls=%fused_computation.5 | convolution fusion | flops 75612160 | bytes 1835008 | tf_op jit(solution)/shard_map/tbj,bji->tbi/dot_general | solution.py:136
  59.3 1.9 %collective-permute-start.2 = (f32[1,1024]{1,0:T(1,128)S(1)}, f32[1,1024]{1,0:T(1,128)S(1)}, u32[]{:S(2)}, u32[]{:S(2)}) collective-permute-start(f32[1,1024]{1,0:T(1,128)S(1)} %slice.40), channel_id=1, source_target_pairs={{0,1},{1,2},{2,3},{3,4},{4,5},{5,6},{6,7},{7,8},{8,9},{9,10},{10,1... | collective-permute-start | bytes 12296 | tf_op jit(solution)/shard_map/ppermute | solution.py:33
  61.3 14.1 %all-to-all-done.2.got_ref = f32[64,16,128]{2,1,0:T(8,128)S(1)} async-done(((f32[64,16,128]{2,1,0:T(8,128)}), f32[64,16,128]{2,1,0:T(8,128)S(1)}, u32[]{:S(2)}, u32[]{:S(2)}) %all-to-all-start.2) | async-done | bytes 524320 | tf_op jit(solution)/shard_map/all_to_all | solution.py:121
  75.4 0.0 copy-start.2
  75.4 0.8 copy-done.2
  76.2 4.6 %shard_map.86 = (f32[16,1024]{1,0:T(8,128)}, f32[16,1024]{1,0:T(8,128)}, f32[64,16,128]{2,1,0:T(8,128)}) custom-call(s32[8,6]{1,0:T(8,128)} %compare_select_fusion.1.pick_ref, s32[32,2]{1,0:T(8,128)} %bitcast.30, f32[16,1024]{1,0:T(8,128)} %get-tuple-element.11.f_ref, f32[16,1024]{1,0:T(8,128)} %get-tuple-element.12.p_ref, f32[64,16,128]{2,1,0:T(8,128)} %copy-done.2, ...), custom_call_target="tpu_custom_call" | custom-call | tf_op jit(solution)/shard_map/pallas_call | solution.py:85
  80.8 0.0 collective-permute-done.2
  80.8 7.0 %all-to-all-start.3 = ((f32[64,16,128]{2,1,0:T(8,128)}), f32[64,16,128]{2,1,0:T(8,128)S(1)}, u32[]{:S(2)}, u32[]{:S(2)}) async-start(f32[64,16,128]{2,1,0:T(8,128)} %get-tuple-element.17), calls=%async_computation.3 | async-start | bytes 1048576 | tf_op jit(solution)/shard_map/all_to_all | solution.py:121
  87.9 1.5 %multiply_multiply_fusion = f32[16,1024]{1,0:T(8,128)} fusion(f32[16,1024]{1,0:T(8,128)S(1)} %copy-done.3, f32[15,1024]{1,0:T(8,128)S(1)} %bitcast.32, f32[1,1024]{1,0:T(1,128)S(1)} %broadcast_multiply_fusion, f32[16,1024]{1,0:T(8,128)} %get-tuple-element.8.f_ref), kind=kLoop, calls=%fused_computation.15 | loop fusion | flops 114688 | bytes 262144 | tf_op jit(solution)/shard_map/mul | solution.py:152
  89.4 14.7 %all-to-all-done.3.got_ref = f32[64,16,128]{2,1,0:T(8,128)S(1)} async-done(((f32[64,16,128]{2,1,0:T(8,128)}), f32[64,16,128]{2,1,0:T(8,128)S(1)}, u32[]{:S(2)}, u32[]{:S(2)}) %all-to-all-start.3) | async-done | bytes 524320 | tf_op jit(solution)/shard_map/all_to_all | solution.py:121
  104.1 0.0 copy-start.1
  104.1 0.8 copy-done.1
  104.9 3.5 %shard_map.87 = f32[16,1024]{1,0:T(8,128)} custom-call(s32[8,6]{1,0:T(8,128)} %compare_select_fusion.1.pick_ref, s32[32,2]{1,0:T(8,128)} %bitcast.31, f32[16,1024]{1,0:T(8,128)} %get-tuple-element.8.f_ref, f32[16,1024]{1,0:T(8,128)} %get-tuple-element.15.p_ref, f32[64,16,128]{2,1,0:T(8,128)} %copy-done.1, f32[8,768,128]{2,1,0:T(8,128)} %bitcast.26), custom_call_target="tpu_custom_call" | custom-call | tf_op jit(solution)/shard_map/pallas_call | solution.py:85
  (17 shorter events, 0.2 us)
Async XLA Ops:
  0.6 28.7 %copy-start.3 = (f32[16,1024]{1,0:T(8,128)S(1)}, f32[16,1024]{1,0:T(8,128)}, u32[]{:S(2)}) copy-start(f32[16,1024]{1,0:T(8,128)} %param.8) | copy-start | bytes 196612
  2.4 20.5 %all-to-all-start = ((s32[32,1,128]{2,1,0:T(1,128)}), s32[32,1,128]{2,1,0:T(1,128)S(1)}, u32[]{:S(2)}, u32[]{:S(2)}) async-start(s32[32,1,128]{2,1,0:T(1,128)} %broadcast_select_fusion.1), calls=%async_computation | async-start | bytes 32768 | tf_op jit(solution)/shard_map/all_to_all | solution.py:115
  22.9 13.7 %copy-start.4 = (s32[32,1,128]{2,1,0:T(1,128)}, s32[32,1,128]{2,1,0:T(1,128)S(1)}, u32[]{:S(2)}) copy-start(s32[32,1,128]{2,1,0:T(1,128)S(1)} %all-to-all-done) | copy-start | bytes 49156
  24.5 23.3 %all-to-all-start.1 = ((f32[64,16,128]{2,1,0:T(8,128)}), f32[64,16,128]{2,1,0:T(8,128)}, u32[]{:S(2)}, u32[]{:S(2)}) async-start(f32[64,16,128]{2,1,0:T(8,128)} %gather_fusion.1), calls=%async_computation.1 | async-start | bytes 1048576 | tf_op jit(solution)/shard_map/all_to_all | solution.py:121
  29.3 28.7 %collective-permute-start = (f32[16,128]{1,0:T(8,128)S(1)}, f32[16,128]{1,0:T(8,128)S(1)}, u32[]{:S(2)}, u32[]{:S(2)}) collective-permute-start(f32[16,128]{1,0:T(8,128)S(1)} %get-tuple-element.24), channel_id=1, source_target_pairs={{0,16},{16,32},{32,48},{48,64},{64,80},{80,96},{96,112},{112,128},... | collective-permute-start | bytes 24584 | tf_op jit(solution)/shard_map/ppermute | solution.py:22
  33.8 24.3 %collective-permute-start.1 = (f32[16,128]{1,0:T(8,128)S(1)}, f32[16,128]{1,0:T(8,128)S(1)}, u32[]{:S(2)}, u32[]{:S(2)}) collective-permute-start(f32[16,128]{1,0:T(8,128)S(1)} %get-tuple-element.25), channel_id=1, source_target_pairs={{16,0},{32,16},{48,32},{64,48},{80,64},{96,80},{112,96},{128,112},... | collective-permute-start | bytes 24584 | tf_op jit(solution)/shard_map/ppermute | solution.py:25
  35.8 0.9 copy-start.5
  35.8 1.9 %copy-start = (f32[8,6,128,128]{3,2,1,0:T(8,128)S(1)}, f32[8,6,128,128]{3,2,1,0:T(8,128)}, u32[]{:S(2)}) copy-start(f32[8,6,128,128]{3,2,1,0:T(8,128)} %param.9) | copy-start | bytes 9437188
  37.7 2.3 %copy-start.6 = (s32[8,6]{1,0:T(8,128)S(1)}, s32[8,6]{1,0:T(8,128)}, u32[]{:S(2)}) copy-start(s32[8,6]{1,0:T(8,128)} %param.10) | copy-start | bytes 580
  52.3 23.1 %all-to-all-start.2 = ((f32[64,16,128]{2,1,0:T(8,128)}), f32[64,16,128]{2,1,0:T(8,128)S(1)}, u32[]{:S(2)}, u32[]{:S(2)}) async-start(f32[64,16,128]{2,1,0:T(8,128)} %get-tuple-element.13), calls=%async_computation.2 | async-start | bytes 1048576 | tf_op jit(solution)/shard_map/all_to_all | solution.py:121
  59.3 21.5 %collective-permute-start.2 = (f32[1,1024]{1,0:T(1,128)S(1)}, f32[1,1024]{1,0:T(1,128)S(1)}, u32[]{:S(2)}, u32[]{:S(2)}) collective-permute-start(f32[1,1024]{1,0:T(1,128)S(1)} %slice.40), channel_id=1, source_target_pairs={{0,1},{1,2},{2,3},{3,4},{4,5},{5,6},{6,7},{7,8},{8,9},{9,10},{10,1... | collective-permute-start | bytes 12296 | tf_op jit(solution)/shard_map/ppermute | solution.py:33
  75.4 0.8 copy-start.2
  80.8 23.3 %all-to-all-start.3 = ((f32[64,16,128]{2,1,0:T(8,128)}), f32[64,16,128]{2,1,0:T(8,128)S(1)}, u32[]{:S(2)}, u32[]{:S(2)}) async-start(f32[64,16,128]{2,1,0:T(8,128)} %get-tuple-element.17), calls=%async_computation.3 | async-start | bytes 1048576 | tf_op jit(solution)/shard_map/all_to_all | solution.py:121
  104.1 0.8 copy-start.1

commit v9 on v8

--- a/solution.py
+++ b/solution.py
@@ -68,10 +68,9 @@
                 if send:
                     held[r] = f_new
         if send:
-            def copy_one(s, carry):
-                send_out[s] = held[sid_ref[s // 2, s % 2]]
-                return carry
-            lax.fori_loop(0, slots, copy_one, 0)
+            pair = sid_ref.shape[1]
+            for s in range(slots):
+                send_out[s] = held[sid_ref[s // pair, s % pair]]
 
     vmem = pl.BlockSpec(memory_space=pltpu.VMEM)
     smem = pl.BlockSpec(memory_space=pltpu.SMEM)
@@ -99,8 +98,8 @@
     space_count = lax.axis_size("space")
     me = lax.axis_index("space")
 
-    run_of = columns // tile_rows
-    local_id = columns % tile_rows
+    run_of = lax.div(columns, tile_rows)
+    local_id = lax.rem(columns, tile_rows)
     remote = run_of != me
     runs = lax.broadcasted_iota(jnp.int32, (space_count, tile_rows * kept), 0)
     flat_run = jnp.where(remote, run_of, -1).reshape(1, -1)

time: 109 us -> 108 us (level)
  Pallas kernels: 12.8 us -> 11.1 us
    pallas_call x3, Pallas kernels: 12.8 us -> 11.1 us  [substep(): pl.pallas_call(kernel, out_shape=tuple(out_shape), in_specs=[smem, smem,...]
  transfers between devices with their start and end apart: 7 -> 7, of which waited for: 4 -> 4; matrix products, arithmetic and copies ran while one was open for 8% -> 8% of each run, Pallas kernels for 9% -> 7%
where the time goes in v9:
time: 108 us; the launch traced here: 107 us
  waiting for transfers between devices  44 us (41%)
  starting transfers between devices  37.2 us (34%)
  Pallas kernels  11.1 us (10%)
  local copies, waits for them, and re-layouts  8.43 us (8%)
  other arithmetic  4.52 us (4%)
  matrix products  1.09 us (1%)
    all_to_all x3, waiting for transfers between devices, exchange(): return lax.all_to_all(sent, 'space', 0, 0, tiled=True)  35.6 us
    all_to_all x3, starting transfers between devices, exchange(): return lax.all_to_all(sent, 'space', 0, 0, tiled=True)  17.7 us
    all_to_all x1, starting transfers between devices, body(): send_ids = lax.all_to_all(request, 'space', 0, 0, tiled=True)[:, :2]  11.2 us
    pallas_call x3, Pallas kernels, substep(): pl.pallas_call(kernel, out_shape=tuple(out_shape), in_specs=[smem, smem,...  11.1 us
    all_to_all x1, waiting for transfers between devices, body(): send_ids = lax.all_to_all(request, 'space', 0, 0, tiled=True)[:, :2]  8.43 us
    ppermute x1, starting transfers between devices, with_halo(): lax.ppermute(lax.slice_in_dim(block, block.shape[dim] - width, None, axis...  4.45 us
    unnamed x17, local copies, waits for them, and re-layouts  2.56 us
    transpose x1, local copies, waits for them, and re-layouts, body(): tiles = tiles.transpose(0, 1, 3, 2).reshape(tile_rows, kept * TILE, TILE)  2.34 us
  transfers between devices with their start and end apart: 7, of which 4 were waited for; matrix products, arithmetic and copies ran while one was open for 8% of the time, Pallas kernels for 7%

profile of v9, /device:TPU:1, one launch (start us, length us, event | category | flops | bytes accessed | tf_op | source)
XLA Modules:
  0.0 107.2 jit_solution(5361408030030117181)
XLA Ops:
  0.6 0.0 copy-start.3
  0.7 0.7 compare_select_fusion
  1.4 0.1 eq.47
  1.4 0.1 broadcast_in_dim.62
  1.5 0.1 select_reduce_fusion
  1.7 0.7 broadcast_select_fusion.1
  2.4 11.2 %all-to-all-start = ((s32[32,1,128]{2,1,0:T(1,128)}), s32[32,1,128]{2,1,0:T(1,128)S(1)}, u32[]{:S(2)}, u32[]{:S(2)}) async-start(s32[32,1,128]{2,1,0:T(1,128)} %broadcast_select_fusion.1), calls=%async_computation | async-start | bytes 32768 | tf_op jit(solution)/shard_map/all_to_all | solution.py:114
  13.6 0.8 copy_bitcast_fusion
  14.5 8.4 %all-to-all-done = s32[32,1,128]{2,1,0:T(1,128)S(1)} async-done(((s32[32,1,128]{2,1,0:T(1,128)}), s32[32,1,128]{2,1,0:T(1,128)S(1)}, u32[]{:S(2)}, u32[]{:S(2)}) %all-to-all-start) | async-done | bytes 16416 | tf_op jit(solution)/shard_map/all_to_all | solution.py:114
  22.9 0.0 copy-start.4
  22.9 0.1 reshape.128
  23.0 1.4 %gather_fusion.1 = f32[64,16,128]{2,1,0:T(8,128)} fusion(f32[16,8,128]{2,0,1:T(8,128)S(1)} %copy_bitcast_fusion, s32[1024]{0:T(1024)S(1)} %pad_clamp_fusion), kind=kCustom, calls=%fused_computation.1 | custom fusion | bytes 1048832 | tf_op jit(solution)/shard_map/jit(_take)/gather | solution.py:138
  24.5 4.8 %all-to-all-start.1 = ((f32[64,16,128]{2,1,0:T(8,128)}), f32[64,16,128]{2,1,0:T(8,128)}, u32[]{:S(2)}, u32[]{:S(2)}) async-start(f32[64,16,128]{2,1,0:T(8,128)} %gather_fusion.1), calls=%async_computation.1 | async-start | bytes 1048576 | tf_op jit(solution)/shard_map/all_to_all | solution.py:120
  29.3 0.0 copy-done.3
  29.3 4.4 %collective-permute-start = (f32[16,128]{1,0:T(8,128)S(1)}, f32[16,128]{1,0:T(8,128)S(1)}, u32[]{:S(2)}, u32[]{:S(2)}) collective-permute-start(f32[16,128]{1,0:T(8,128)S(1)} %get-tuple-element.24), channel_id=1, source_target_pairs={{0,16},{16,32},{32,48},{48,64},{64,80},{80,96},{96,112},{112,128},... | collective-permute-start | bytes 24584 | tf_op jit(solution)/shard_map/ppermute | solution.py:22
  33.8 1.9 %collective-permute-start.1 = (f32[16,128]{1,0:T(8,128)S(1)}, f32[16,128]{1,0:T(8,128)S(1)}, u32[]{:S(2)}, u32[]{:S(2)}) collective-permute-start(f32[16,128]{1,0:T(8,128)S(1)} %get-tuple-element.25), channel_id=1, source_target_pairs={{16,0},{32,16},{48,32},{64,48},{80,64},{96,80},{112,96},{128,112},... | collective-permute-start | bytes 24584 | tf_op jit(solution)/shard_map/ppermute | solution.py:25
  35.7 0.1 reshape.120
  35.8 0.0 copy-start.5
  35.8 0.0 copy-start
  35.8 0.8 gather_fusion
  36.6 0.0 copy-done.4
  36.6 0.1 reshape.119
  36.7 0.0 copy-done.5
  36.7 0.1 fusion.8
  36.8 0.9 copy-done
  37.7 0.0 copy-start.6
  37.7 2.3 %copy.33 = f32[8,6,128,128]{3,2,1,0:T(8,128)} copy(f32[8,6,128,128]{2,3,1,0:T(8,128)S(1)} %bitcast.27) | data formatting | bytes 6291456 | tf_op jit(solution)/shard_map/transpose | solution.py:122
  40.1 0.0 copy-done.6
  40.1 0.6 compare_select_fusion.1.pick_ref
  40.7 7.1 %all-to-all-done.1.got_ref = f32[64,16,128]{2,1,0:T(8,128)} async-done(((f32[64,16,128]{2,1,0:T(8,128)}), f32[64,16,128]{2,1,0:T(8,128)}, u32[]{:S(2)}, u32[]{:S(2)}) %all-to-all-start.1) | async-done | bytes 524320 | tf_op jit(solution)/shard_map/all_to_all | solution.py:120
  47.7 3.8 %shard_map.100 = (f32[16,1024]{1,0:T(8,128)}, f32[16,1024]{1,0:T(8,128)}, f32[64,16,128]{2,1,0:T(8,128)}) custom-call(s32[8,6]{1,0:T(8,128)} %compare_select_fusion.1.pick_ref, s32[32,2]{1,0:T(8,128)} %bitcast.29, f32[16,1024]{1,0:T(8,128)} %f_ref.1, f32[16,1024]{1,0:T(8,128)} %p_ref.1, f32[64,16,128]{2,1,0:T(8,128)} %all-to-all-done.1.got_ref, ...), custom_call_target="tpu_custom_call" | custom-call | tf_op jit(solution)/shard_map/pallas_call | solution.py:84
  51.5 5.0 %all-to-all-start.2 = ((f32[64,16,128]{2,1,0:T(8,128)}), f32[64,16,128]{2,1,0:T(8,128)S(1)}, u32[]{:S(2)}, u32[]{:S(2)}) async-start(f32[64,16,128]{2,1,0:T(8,128)} %get-tuple-element.13), calls=%async_computation.2 | async-start | bytes 1048576 | tf_op jit(solution)/shard_map/all_to_all | solution.py:120
  56.5 0.7 convert_reduce_fusion
  57.2 0.0 collective-permute-done
  57.2 0.0 collective-permute-done.1
  57.3 1.1 %fusion = f32[8,2,8,128]{3,2,1,0:T(8,128)S(1)} fusion(f32[8,384,128]{2,1,0:T(8,128)S(1)} %convert_reduce_fusion, f32[16,8,128]{2,0,1:T(8,128)S(1)} %copy.41, f32[16,8,128]{2,0,1:T(8,128)S(1)} %copy.40, f32[16,8,128]{2,0,1:T(8,128)S(1)} %copy.39), kind=kOutput, calls=%fused_computation.5 | convolution fusion | flops 75612160 | bytes 1835008 | tf_op jit(solution)/shard_map/tbj,bji->tbi/dot_general | solution.py:135
  58.5 1.9 %collective-permute-start.2 = (f32[1,1024]{1,0:T(1,128)S(1)}, f32[1,1024]{1,0:T(1,128)S(1)}, u32[]{:S(2)}, u32[]{:S(2)}) collective-permute-start(f32[1,1024]{1,0:T(1,128)S(1)} %slice.40), channel_id=1, source_target_pairs={{0,1},{1,2},{2,3},{3,4},{4,5},{5,6},{6,7},{7,8},{8,9},{9,10},{10,1... | collective-permute-start | bytes 12296 | tf_op jit(solution)/shard_map/ppermute | solution.py:33
  60.4 14.1 %all-to-all-done.2.got_ref = f32[64,16,128]{2,1,0:T(8,128)S(1)} async-done(((f32[64,16,128]{2,1,0:T(8,128)}), f32[64,16,128]{2,1,0:T(8,128)S(1)}, u32[]{:S(2)}, u32[]{:S(2)}) %all-to-all-start.2) | async-done | bytes 524320 | tf_op jit(solution)/shard_map/all_to_all | solution.py:120
  74.6 0.0 copy-start.2
  74.6 0.8 copy-done.2
  75.4 3.8 %shard_map.101 = (f32[16,1024]{1,0:T(8,128)}, f32[16,1024]{1,0:T(8,128)}, f32[64,16,128]{2,1,0:T(8,128)}) custom-call(s32[8,6]{1,0:T(8,128)} %compare_select_fusion.1.pick_ref, s32[32,2]{1,0:T(8,128)} %bitcast.30, f32[16,1024]{1,0:T(8,128)} %get-tuple-element.11.f_ref, f32[16,1024]{1,0:T(8,128)} %get-tuple-element.12.p_ref, f32[64,16,128]{2,1,0:T(8,128)} %copy-done.2, ...), custom_call_target="tpu_custom_call" | custom-call | tf_op jit(solution)/shard_map/pallas_call | solution.py:84
  79.1 0.0 collective-permute-done.2
  79.1 7.9 %all-to-all-start.3 = ((f32[64,16,128]{2,1,0:T(8,128)}), f32[64,16,128]{2,1,0:T(8,128)S(1)}, u32[]{:S(2)}, u32[]{:S(2)}) async-start(f32[64,16,128]{2,1,0:T(8,128)} %get-tuple-element.17), calls=%async_computation.3 | async-start | bytes 1048576 | tf_op jit(solution)/shard_map/all_to_all | solution.py:120
  87.0 1.5 %multiply_multiply_fusion = f32[16,1024]{1,0:T(8,128)} fusion(f32[16,1024]{1,0:T(8,128)S(1)} %copy-done.3, f32[15,1024]{1,0:T(8,128)S(1)} %bitcast.32, f32[1,1024]{1,0:T(1,128)S(1)} %broadcast_multiply_fusion, f32[16,1024]{1,0:T(8,128)} %get-tuple-element.8.f_ref), kind=kLoop, calls=%fused_computation.15 | loop fusion | flops 114688 | bytes 262144 | tf_op jit(solution)/shard_map/mul | solution.py:151
  88.5 14.4 %all-to-all-done.3.got_ref = f32[64,16,128]{2,1,0:T(8,128)S(1)} async-done(((f32[64,16,128]{2,1,0:T(8,128)}), f32[64,16,128]{2,1,0:T(8,128)S(1)}, u32[]{:S(2)}, u32[]{:S(2)}) %all-to-all-start.3) | async-done | bytes 524320 | tf_op jit(solution)/shard_map/all_to_all | solution.py:120
  102.9 0.0 copy-start.1
  102.9 0.8 copy-done.1
  103.7 3.5 %shard_map.102 = f32[16,1024]{1,0:T(8,128)} custom-call(s32[8,6]{1,0:T(8,128)} %compare_select_fusion.1.pick_ref, s32[32,2]{1,0:T(8,128)} %bitcast.31, f32[16,1024]{1,0:T(8,128)} %get-tuple-element.8.f_ref, f32[16,1024]{1,0:T(8,128)} %get-tuple-element.15.p_ref, f32[64,16,128]{2,1,0:T(8,128)} %copy-done.1, f32[8,768,128]{2,1,0:T(8,128)} %bitcast.26), custom_call_target="tpu_custom_call" | custom-call | tf_op jit(solution)/shard_map/pallas_call | solution.py:84
  (17 shorter events, 0.2 us)
Async XLA Ops:
  0.6 28.7 %copy-start.3 = (f32[16,1024]{1,0:T(8,128)S(1)}, f32[16,1024]{1,0:T(8,128)}, u32[]{:S(2)}) copy-start(f32[16,1024]{1,0:T(8,128)} %param.8) | copy-start | bytes 196612
  2.4 20.5 %all-to-all-start = ((s32[32,1,128]{2,1,0:T(1,128)}), s32[32,1,128]{2,1,0:T(1,128)S(1)}, u32[]{:S(2)}, u32[]{:S(2)}) async-start(s32[32,1,128]{2,1,0:T(1,128)} %broadcast_select_fusion.1), calls=%async_computation | async-start | bytes 32768 | tf_op jit(solution)/shard_map/all_to_all | solution.py:114
  22.9 13.7 %copy-start.4 = (s32[32,1,128]{2,1,0:T(1,128)}, s32[32,1,128]{2,1,0:T(1,128)S(1)}, u32[]{:S(2)}) copy-start(s32[32,1,128]{2,1,0:T(1,128)S(1)} %all-to-all-done) | copy-start | bytes 49156
  24.5 23.3 %all-to-all-start.1 = ((f32[64,16,128]{2,1,0:T(8,128)}), f32[64,16,128]{2,1,0:T(8,128)}, u32[]{:S(2)}, u32[]{:S(2)}) async-start(f32[64,16,128]{2,1,0:T(8,128)} %gather_fusion.1), calls=%async_computation.1 | async-start | bytes 1048576 | tf_op jit(solution)/shard_map/all_to_all | solution.py:120
  29.3 27.9 %collective-permute-start = (f32[16,128]{1,0:T(8,128)S(1)}, f32[16,128]{1,0:T(8,128)S(1)}, u32[]{:S(2)}, u32[]{:S(2)}) collective-permute-start(f32[16,128]{1,0:T(8,128)S(1)} %get-tuple-element.24), channel_id=1, source_target_pairs={{0,16},{16,32},{32,48},{48,64},{64,80},{80,96},{96,112},{112,128},... | collective-permute-start | bytes 24584 | tf_op jit(solution)/shard_map/ppermute | solution.py:22
  33.8 23.4 %collective-permute-start.1 = (f32[16,128]{1,0:T(8,128)S(1)}, f32[16,128]{1,0:T(8,128)S(1)}, u32[]{:S(2)}, u32[]{:S(2)}) collective-permute-start(f32[16,128]{1,0:T(8,128)S(1)} %get-tuple-element.25), channel_id=1, source_target_pairs={{16,0},{32,16},{48,32},{64,48},{80,64},{96,80},{112,96},{128,112},... | collective-permute-start | bytes 24584 | tf_op jit(solution)/shard_map/ppermute | solution.py:25
  35.8 0.9 copy-start.5
  35.8 1.9 %copy-start = (f32[8,6,128,128]{3,2,1,0:T(8,128)S(1)}, f32[8,6,128,128]{3,2,1,0:T(8,128)}, u32[]{:S(2)}) copy-start(f32[8,6,128,128]{3,2,1,0:T(8,128)} %param.9) | copy-start | bytes 9437188
  37.7 2.3 %copy-start.6 = (s32[8,6]{1,0:T(8,128)S(1)}, s32[8,6]{1,0:T(8,128)}, u32[]{:S(2)}) copy-start(s32[8,6]{1,0:T(8,128)} %param.10) | copy-start | bytes 580
  51.5 23.1 %all-to-all-start.2 = ((f32[64,16,128]{2,1,0:T(8,128)}), f32[64,16,128]{2,1,0:T(8,128)S(1)}, u32[]{:S(2)}, u32[]{:S(2)}) async-start(f32[64,16,128]{2,1,0:T(8,128)} %get-tuple-element.13), calls=%async_computation.2 | async-start | bytes 1048576 | tf_op jit(solution)/shard_map/all_to_all | solution.py:120
  58.5 20.6 %collective-permute-start.2 = (f32[1,1024]{1,0:T(1,128)S(1)}, f32[1,1024]{1,0:T(1,128)S(1)}, u32[]{:S(2)}, u32[]{:S(2)}) collective-permute-start(f32[1,1024]{1,0:T(1,128)S(1)} %slice.40), channel_id=1, source_target_pairs={{0,1},{1,2},{2,3},{3,4},{4,5},{5,6},{6,7},{7,8},{8,9},{9,10},{10,1... | collective-permute-start | bytes 12296 | tf_op jit(solution)/shard_map/ppermute | solution.py:33
  74.6 0.8 copy-start.2
  79.1 23.8 %all-to-all-start.3 = ((f32[64,16,128]{2,1,0:T(8,128)}), f32[64,16,128]{2,1,0:T(8,128)S(1)}, u32[]{:S(2)}, u32[]{:S(2)}) async-start(f32[64,16,128]{2,1,0:T(8,128)} %get-tuple-element.17), calls=%async_computation.3 | async-start | bytes 1048576 | tf_op jit(solution)/shard_map/all_to_all | solution.py:120
  102.9 0.8 copy-start.1

commit v10 on v9

--- a/solution.py
+++ b/solution.py
@@ -45,12 +45,12 @@
     return part(a_hi, b_hi) + (part(a_hi, b_lo) + part(a_lo, b_hi))
 
 
-def substep(field, moment, got, tiles, pick, send_ids, scale, advance, send):
+def substep(field, moment, local, got, tiles, pick, send_ids, scale, advance, send):
     slices, site_count = field.shape
-    rows, kept = tiles.shape[0], tiles.shape[1] // TILE
+    rows, kept = tiles.shape[0], tiles.shape[1] // TILE + 1
     slots = send_ids.shape[0] * send_ids.shape[1]
 
-    def kernel(pick_ref, sid_ref, f_ref, p_ref, got_ref, tiles_ref, *refs):
+    def kernel(pick_ref, sid_ref, f_ref, p_ref, local_ref, got_ref, tiles_ref, *refs):
         outs = list(refs)
         p_out = outs.pop(0)
         f_out = outs.pop(0) if advance else None
@@ -58,8 +58,8 @@
         held = outs.pop(0) if send else None
         for r in range(rows):
             cols = slice(r * TILE, (r + 1) * TILE)
-            pieces = [f_ref[:, cols]] + [got_ref[pick_ref[r, k]] for k in range(1, kept)]
-            acc = split_dot(jnp.concatenate(pieces, axis=1), tiles_ref[r])
+            pieces = [got_ref[pick_ref[r, k]] for k in range(1, kept)]
+            acc = local_ref[:, cols] + split_dot(jnp.concatenate(pieces, axis=1), tiles_ref[r])
             p_new = p_ref[:, cols] - scale * acc
             p_out[:, cols] = p_new
             if advance:
@@ -84,10 +84,10 @@
     return pl.pallas_call(
         kernel,
         out_shape=tuple(out_shape),
-        in_specs=[smem, smem, vmem, vmem, vmem, vmem],
+        in_specs=[smem, smem, vmem, vmem, vmem, vmem, vmem],
         out_specs=tuple([vmem] * len(out_shape)),
         scratch_shapes=scratch,
-    )(pick, send_ids, field, moment, got, tiles)
+    )(pick, send_ids, field, moment, local, got, tiles)
 
 
 def body(field, momentum, solution, tiles, columns, neighbours):
@@ -119,7 +119,14 @@
     def exchange(sent):
         return lax.all_to_all(sent, "space", 0, 0, tiled=True)
 
-    tiles = tiles.transpose(0, 1, 3, 2).reshape(tile_rows, kept * TILE, TILE)
+    own_tiles = tiles[:, 0]
+    tiles = tiles[:, 1:].transpose(0, 1, 3, 2).reshape(tile_rows, (kept - 1) * TILE, TILE)
+
+    def local_term(values):
+        blocks = values.reshape(slices, tile_rows, TILE)
+        mixed = jnp.einsum("rij,trj->tri", own_tiles, blocks, precision=lax.Precision.HIGHEST)
+        return mixed.reshape(slices, site_count)
+
     total_sites = site_count * space_count
     first_site = me * site_count
     lookup = (neighbours - first_site + TILE) % total_sites
@@ -137,13 +144,13 @@
     own = field.reshape(slices, tile_rows, TILE)
     first = jnp.take(own, send_ids.reshape(-1), axis=1, mode="clip").transpose(1, 0, 2)
     got = exchange(first)
-    moment, field_one, sent = substep(field, momentum, got, tiles, pick, send_ids, 0.5 * step_size, True, True)
+    moment, field_one, sent = substep(field, momentum, local_term(field), got, tiles, pick, send_ids, 0.5 * step_size, True, True)
     arrived = from_behind(hopped[-1:], "tm", 1)
     got = exchange(sent)
-    moment, field_two, sent = substep(field_one, moment, got, tiles, pick, send_ids, step_size, True, True)
+    moment, field_two, sent = substep(field_one, moment, local_term(field_one), got, tiles, pick, send_ids, step_size, True, True)
     sent, arrived = lax.optimization_barrier((sent, arrived))
     got = exchange(sent)
-    (moment,) = substep(field_two, moment, got, tiles, pick, send_ids, 0.5 * step_size, False, False)
+    (moment,) = substep(field_two, moment, local_term(field_two), got, tiles, pick, send_ids, 0.5 * step_size, False, False)
 
     earlier = jnp.concatenate([parity_sign * arrived, hopped[:-1]], axis=0)
     link_factor = jnp.exp(coupling * field_two)

time: 108 us -> 115 us (1.065)
  waiting for transfers between devices: 44 us -> 35.2 us
  starting transfers between devices: 37.2 us -> 44 us
  matrix products: 1.09 us -> 6.99 us
  local copies, waits for them, and re-layouts: 8.43 us -> 11.8 us
    all_to_all x1, waiting for transfers between devices: 8.43 us -> 0.16 us  [body(): send_ids = lax.all_to_all(request, 'space', 0, 0, tiled=True)[:, :2]]
    all_to_all x3, starting transfers between devices: 17.7 us -> 24.5 us  [exchange(): return lax.all_to_all(sent, 'space', 0, 0, tiled=True)]
    dot_general x0 -> x3, matrix products: none -> 5.9 us  [local_term(): jnp.einsum('rij,trj->tri', own_tiles, blocks, precision=lax.Precision.HIG...]
    transpose x1 -> x2, local copies, waits for them, and re-layouts: 2.34 us -> 4.01 us  [body(): tiles[:, 1:].transpose(0, 1, 3, 2)]
    unnamed x17 -> x21, local copies, waits for them, and re-layouts: 2.56 us -> 2.45 us
  transfers between devices with their start and end apart: 7 -> 7, of which waited for: 4 -> 4; matrix products, arithmetic and copies ran while one was open for 8% -> 17% of each run, Pallas kernels for 7% -> 6%
where the time goes in v10:
time: 115 us; the launch traced here: 114 us
  starting transfers between devices  44 us (38%)
  waiting for transfers between devices  35.2 us (31%)
  local copies, waits for them, and re-layouts  11.8 us (10%)
  Pallas kernels  10.5 us (9%)
  matrix products  6.99 us (6%)
  other arithmetic  4.5 us (4%)
    all_to_all x3, waiting for transfers between devices, exchange(): return lax.all_to_all(sent, 'space', 0, 0, tiled=True)  35.1 us
    all_to_all x3, starting transfers between devices, exchange(): return lax.all_to_all(sent, 'space', 0, 0, tiled=True)  24.5 us
    all_to_all x1, starting transfers between devices, body(): send_ids = lax.all_to_all(request, 'space', 0, 0, tiled=True)[:, :2]  11.2 us
    pallas_call x3, Pallas kernels, substep(): pl.pallas_call(kernel, out_shape=tuple(out_shape), in_specs=[smem, smem,...  10.5 us
    dot_general x3, matrix products, local_term(): jnp.einsum('rij,trj->tri', own_tiles, blocks, precision=lax.Precision.HIG...  5.9 us
    ppermute x1, starting transfers between devices, with_halo(): lax.ppermute(lax.slice_in_dim(block, block.shape[dim] - width, None, axis...  4.43 us
    transpose x2, local copies, waits for them, and re-layouts, body(): tiles[:, 1:].transpose(0, 1, 3, 2)  4.01 us
    unnamed x21, local copies, waits for them, and re-layouts  2.45 us
  transfers between devices with their start and end apart: 7, of which 4 were waited for; matrix products, arithmetic and copies ran while one was open for 17% of the time, Pallas kernels for 6%

profile of v10, /device:TPU:1, one launch (start us, length us, event | category | flops | bytes accessed | tf_op | source)
XLA Modules:
  0.0 114.0 jit_solution(18299041303252121137)
XLA Ops:
  0.6 0.0 copy-start.4
  0.7 0.7 compare_select_fusion
  1.4 0.1 broadcast_in_dim.62
  1.4 0.1 eq.47
  1.5 0.1 select_reduce_fusion
  1.7 0.7 broadcast_select_fusion.1
  2.4 11.2 %all-to-all-start = ((s32[32,1,128]{2,1,0:T(1,128)}), s32[32,1,128]{2,1,0:T(1,128)S(1)}, u32[]{:S(2)}, u32[]{:S(2)}) async-start(s32[32,1,128]{2,1,0:T(1,128)} %broadcast_select_fusion.1), calls=%async_computation | async-start | bytes 32768 | tf_op jit(solution)/shard_map/all_to_all | solution.py:114
  13.6 0.7 fusion.21
  14.3 4.4 %collective-permute-start = (f32[16,128]{1,0:T(8,128)S(1)}, f32[16,128]{1,0:T(8,128)S(1)}, u32[]{:S(2)}, u32[]{:S(2)}) collective-permute-start(f32[16,128]{1,0:T(8,128)S(1)} %get-tuple-element.24), channel_id=1, source_target_pairs={{0,16},{16,32},{32,48},{48,64},{64,80},{80,96},{96,112},{112,128},... | collective-permute-start | bytes 24584 | tf_op jit(solution)/shard_map/ppermute | solution.py:22
  18.8 1.9 %collective-permute-start.1 = (f32[16,128]{1,0:T(8,128)S(1)}, f32[16,128]{1,0:T(8,128)S(1)}, u32[]{:S(2)}, u32[]{:S(2)}) collective-permute-start(f32[16,128]{1,0:T(8,128)S(1)} %get-tuple-element.25), channel_id=1, source_target_pairs={{16,0},{32,16},{48,32},{64,48},{80,64},{96,80},{112,96},{128,112},... | collective-permute-start | bytes 24584 | tf_op jit(solution)/shard_map/ppermute | solution.py:25
  20.7 1.9 %slice_bitcast_fusion = f32[8,5,128,128]{2,3,1,0:T(8,128)S(1)} fusion(f32[8,6,128,128]{3,2,1,0:T(8,128)} %param.9), kind=kLoop, calls=%fused_computation.4 | loop fusion | bytes 5242880 | tf_op jit(solution)/shard_map/transpose | solution.py:123
  22.6 0.0 copy-done.4
  22.7 0.1 reshape.141
  22.7 0.2 all-to-all-done
  22.9 0.0 copy-start.5
  22.9 0.1 reshape.149
  23.0 1.4 %gather_fusion.1 = f32[64,16,128]{2,1,0:T(8,128)} fusion(f32[16,8,128]{2,0,1:T(8,128)S(1)} %copy_bitcast_fusion.3, s32[1024]{0:T(1024)S(1)} %pad_clamp_fusion), kind=kCustom, calls=%fused_computation.1 | custom fusion | bytes 1048832 | tf_op jit(solution)/shard_map/jit(_take)/gather | solution.py:145
  24.4 10.9 %all-to-all-start.1 = ((f32[64,16,128]{2,1,0:T(8,128)}), f32[64,16,128]{2,1,0:T(8,128)S(1)}, u32[]{:S(2)}, u32[]{:S(2)}) async-start(f32[64,16,128]{2,1,0:T(8,128)} %gather_fusion.1), calls=%async_computation.1 | async-start | bytes 1048576 | tf_op jit(solution)/shard_map/all_to_all | solution.py:120
  35.4 0.8 gather_fusion
  36.2 0.0 copy-done.5
  36.2 0.0 copy-start.7
  36.2 0.0 copy-start.8
  36.2 0.1 reshape.140
  36.3 2.1 %copy.63 = f32[8,5,128,128]{3,2,1,0:T(8,128)} copy(f32[8,5,128,128]{2,3,1,0:T(8,128)S(1)} %slice_bitcast_fusion) | data formatting | bytes 5242880 | tf_op jit(solution)/shard_map/transpose | solution.py:123
  38.4 1.9 %convolution_bitcast_fusion.2 = f32[8,2,8,128]{3,2,1,0:T(8,128)S(1)} fusion(f32[8,6,128,128]{3,2,1,0:T(8,128)} %param.9, f32[16,1024]{1,0:T(8,128)S(1)} %copy-done.4), kind=kOutput, calls=%fused_computation.9 | convolution fusion | flops 25165824 | bytes 655360 | tf_op jit(solution)/shard_map/rij,trj->tri/dot_general | solution.py:127
  40.3 0.0 copy-start.3
  40.3 0.7 copy.102
  41.0 0.0 copy-done.7
  41.0 0.1 fusion.18
  41.1 0.0 copy-done.8
  41.1 0.6 compare_select_fusion.1.pick_ref
  41.7 11.9 %all-to-all-done.1.got_ref = f32[64,16,128]{2,1,0:T(8,128)S(1)} async-done(((f32[64,16,128]{2,1,0:T(8,128)}), f32[64,16,128]{2,1,0:T(8,128)S(1)}, u32[]{:S(2)}, u32[]{:S(2)}) %all-to-all-start.1) | async-done | bytes 524320 | tf_op jit(solution)/shard_map/all_to_all | solution.py:120
  53.6 0.0 copy-start.1
  53.6 0.8 copy-done.1
  54.4 3.6 %shard_map.100 = (f32[16,1024]{1,0:T(8,128)}, f32[16,1024]{1,0:T(8,128)}, f32[64,16,128]{2,1,0:T(8,128)}) custom-call(s32[8,6]{1,0:T(8,128)} %compare_select_fusion.1.pick_ref, s32[32,2]{1,0:T(8,128)} %bitcast.74, f32[16,1024]{1,0:T(8,128)} %f_ref.1, f32[16,1024]{1,0:T(8,128)} %p_ref.1, f32[16,1024]{1,0:T(8,128)} %bitcast.78, f32[64,16,128]{2,1,0:T(8,128)} %copy-done.1, ...), custom_call_target="tpu_custom_call" | custom-call | tf_op jit(solution)/shard_map/pallas_call | solution.py:84
  57.9 0.0 copy-start.6
  57.9 5.1 %all-to-all-start.2 = ((f32[64,16,128]{2,1,0:T(8,128)}), f32[64,16,128]{2,1,0:T(8,128)S(1)}, u32[]{:S(2)}, u32[]{:S(2)}) async-start(f32[64,16,128]{2,1,0:T(8,128)} %get-tuple-element.13), calls=%async_computation.2 | async-start | bytes 1048576 | tf_op jit(solution)/shard_map/all_to_all | solution.py:120
  63.0 0.7 convert_reduce_fusion
  63.8 0.0 collective-permute-done
  63.8 0.0 collective-permute-done.1
  63.8 0.0 copy-done.3
  63.9 1.1 fusion
  65.1 1.9 %collective-permute-start.2 = (f32[1,1024]{1,0:T(1,128)S(1)}, f32[1,1024]{1,0:T(1,128)S(1)}, u32[]{:S(2)}, u32[]{:S(2)}) collective-permute-start(f32[1,1024]{1,0:T(1,128)S(1)} %slice.48), channel_id=1, source_target_pairs={{0,1},{1,2},{2,3},{3,4},{4,5},{5,6},{6,7},{7,8},{8,9},{9,10},{10,1... | collective-permute-start | bytes 12296 | tf_op jit(solution)/shard_map/ppermute | solution.py:33
  67.0 0.0 copy-done.6
  67.0 2.0 %convolution_bitcast_fusion.1 = f32[8,2,8,128]{3,2,1,0:T(8,128)S(1)} fusion(f32[8,6,128,128]{3,2,1,0:T(8,128)} %param.9, f32[16,1024]{1,0:T(8,128)S(1)} %copy-done.6), kind=kOutput, calls=%fused_computation.8 | convolution fusion | flops 25165824 | bytes 655360 | tf_op jit(solution)/shard_map/rij,trj->tri/dot_general | solution.py:127
  69.0 0.7 copy.101
  69.6 11.5 %all-to-all-done.2.got_ref = f32[64,16,128]{2,1,0:T(8,128)S(1)} async-done(((f32[64,16,128]{2,1,0:T(8,128)}), f32[64,16,128]{2,1,0:T(8,128)S(1)}, u32[]{:S(2)}, u32[]{:S(2)}) %all-to-all-start.2) | async-done | bytes 524320 | tf_op jit(solution)/shard_map/all_to_all | solution.py:120
  81.1 0.0 copy-start
  81.1 0.8 copy-done
  81.9 3.6 %shard_map.101 = (f32[16,1024]{1,0:T(8,128)}, f32[16,1024]{1,0:T(8,128)}, f32[64,16,128]{2,1,0:T(8,128)}) custom-call(s32[8,6]{1,0:T(8,128)} %compare_select_fusion.1.pick_ref, s32[32,2]{1,0:T(8,128)} %bitcast.75, f32[16,1024]{1,0:T(8,128)} %get-tuple-element.11.f_ref, f32[16,1024]{1,0:T(8,128)} %get-tuple-element.12.p_ref, f32[16,1024]{1,0:T(8,128)} %bitcast.79, ...), custom_call_target="tpu_custom_call" | custom-call | tf_op jit(solution)/shard_map/pallas_call | solution.py:84
  85.5 0.0 collective-permute-done.2
  85.5 8.4 %all-to-all-start.3 = ((f32[64,16,128]{2,1,0:T(8,128)}), f32[64,16,128]{2,1,0:T(8,128)S(1)}, u32[]{:S(2)}, u32[]{:S(2)}) async-start(f32[64,16,128]{2,1,0:T(8,128)} %get-tuple-element.17), calls=%async_computation.3 | async-start | bytes 1048576 | tf_op jit(solution)/shard_map/all_to_all | solution.py:120
  94.0 2.0 %convolution_bitcast_fusion = f32[8,2,8,128]{3,2,1,0:T(8,128)S(1)} fusion(f32[8,6,128,128]{3,2,1,0:T(8,128)} %param.9, f32[16,1024]{1,0:T(8,128)} %get-tuple-element.8.f_ref), kind=kOutput, calls=%fused_computation.7 | convolution fusion | flops 25165824 | bytes 655360 | tf_op jit(solution)/shard_map/rij,trj->tri/dot_general | solution.py:127
  96.0 0.6 copy.100
  96.6 1.5 %multiply_multiply_fusion = f32[16,1024]{1,0:T(8,128)} fusion(f32[16,1024]{1,0:T(8,128)S(1)} %copy-done.3, f32[15,1024]{1,0:T(8,128)S(1)} %bitcast.77, f32[1,1024]{1,0:T(1,128)S(1)} %broadcast_multiply_fusion, f32[16,1024]{1,0:T(8,128)} %get-tuple-element.8.f_ref), kind=kLoop, calls=%fused_computation.32 | loop fusion | flops 114688 | bytes 262144 | tf_op jit(solution)/shard_map/mul | solution.py:158
  98.1 11.7 %all-to-all-done.3.got_ref = f32[64,16,128]{2,1,0:T(8,128)S(1)} async-done(((f32[64,16,128]{2,1,0:T(8,128)}), f32[64,16,128]{2,1,0:T(8,128)S(1)}, u32[]{:S(2)}, u32[]{:S(2)}) %all-to-all-start.3) | async-done | bytes 524320 | tf_op jit(solution)/shard_map/all_to_all | solution.py:120
  109.8 0.0 copy-start.2
  109.8 0.8 copy-done.2
  110.6 3.4 %shard_map.102 = f32[16,1024]{1,0:T(8,128)} custom-call(s32[8,6]{1,0:T(8,128)} %compare_select_fusion.1.pick_ref, s32[32,2]{1,0:T(8,128)} %bitcast.76, f32[16,1024]{1,0:T(8,128)} %get-tuple-element.8.f_ref, f32[16,1024]{1,0:T(8,128)} %get-tuple-element.15.p_ref, f32[16,1024]{1,0:T(8,128)} %bitcast.80, f32[64,16,128]{2,1,0:T(8,128)} %copy-done.2, ...), custom_call_target="tpu_custom_call" | custom-call | tf_op jit(solution)/shard_map/pallas_call | solution.py:84
  (17 shorter events, 0.2 us)
Async XLA Ops:
  0.6 22.0 %copy-start.4 = (f32[16,1024]{1,0:T(8,128)S(1)}, f32[16,1024]{1,0:T(8,128)}, u32[]{:S(2)}) copy-start(f32[16,1024]{1,0:T(8,128)} %f_ref.1) | copy-start | bytes 196612
  2.4 20.5 %all-to-all-start = ((s32[32,1,128]{2,1,0:T(1,128)}), s32[32,1,128]{2,1,0:T(1,128)S(1)}, u32[]{:S(2)}, u32[]{:S(2)}) async-start(s32[32,1,128]{2,1,0:T(1,128)} %broadcast_select_fusion.1), calls=%async_computation | async-start | bytes 32768 | tf_op jit(solution)/shard_map/all_to_all | solution.py:114
  14.3 49.4 %collective-permute-start = (f32[16,128]{1,0:T(8,128)S(1)}, f32[16,128]{1,0:T(8,128)S(1)}, u32[]{:S(2)}, u32[]{:S(2)}) collective-permute-start(f32[16,128]{1,0:T(8,128)S(1)} %get-tuple-element.24), channel_id=1, source_target_pairs={{0,16},{16,32},{32,48},{48,64},{64,80},{80,96},{96,112},{112,128},... | collective-permute-start | bytes 24584 | tf_op jit(solution)/shard_map/ppermute | solution.py:22
  18.8 45.0 %collective-permute-start.1 = (f32[16,128]{1,0:T(8,128)S(1)}, f32[16,128]{1,0:T(8,128)S(1)}, u32[]{:S(2)}, u32[]{:S(2)}) collective-permute-start(f32[16,128]{1,0:T(8,128)S(1)} %get-tuple-element.25), channel_id=1, source_target_pairs={{16,0},{32,16},{48,32},{64,48},{80,64},{96,80},{112,96},{128,112},... | collective-permute-start | bytes 24584 | tf_op jit(solution)/shard_map/ppermute | solution.py:25
  22.9 13.3 %copy-start.5 = (s32[32,1,128]{2,1,0:T(1,128)}, s32[32,1,128]{2,1,0:T(1,128)S(1)}, u32[]{:S(2)}) copy-start(s32[32,1,128]{2,1,0:T(1,128)S(1)} %all-to-all-done) | copy-start | bytes 49156
  24.4 29.1 %all-to-all-start.1 = ((f32[64,16,128]{2,1,0:T(8,128)}), f32[64,16,128]{2,1,0:T(8,128)S(1)}, u32[]{:S(2)}, u32[]{:S(2)}) async-start(f32[64,16,128]{2,1,0:T(8,128)} %gather_fusion.1), calls=%async_computation.1 | async-start | bytes 1048576 | tf_op jit(solution)/shard_map/all_to_all | solution.py:120
  36.2 4.8 %copy-start.7 = (s32[3,1024]{1,0:T(4,128)S(1)}, s32[3,1024]{1,0:T(4,128)}, u32[]{:S(2)}) copy-start(s32[3,1024]{1,0:T(4,128)} %param.11) | copy-start | bytes 36868
  36.2 4.9 %copy-start.8 = (s32[8,6]{1,0:T(8,128)S(1)}, s32[8,6]{1,0:T(8,128)}, u32[]{:S(2)}) copy-start(s32[8,6]{1,0:T(8,128)} %param.10) | copy-start | bytes 580
  40.3 23.4 %copy-start.3 = (f32[16,1024]{1,0:T(8,128)S(1)}, f32[16,1024]{1,0:T(8,128)}, u32[]{:S(2)}) copy-start(f32[16,1024]{1,0:T(8,128)} %param.8) | copy-start | bytes 196612
  53.6 0.8 copy-start.1
  57.9 9.1 %copy-start.6 = (f32[16,1024]{1,0:T(8,128)S(1)}, f32[16,1024]{1,0:T(8,128)}, u32[]{:S(2)}) copy-start(f32[16,1024]{1,0:T(8,128)} %get-tuple-element.11.f_ref) | copy-start | bytes 196612
  57.9 23.2 %all-to-all-start.2 = ((f32[64,16,128]{2,1,0:T(8,128)}), f32[64,16,128]{2,1,0:T(8,128)S(1)}, u32[]{:S(2)}, u32[]{:S(2)}) async-start(f32[64,16,128]{2,1,0:T(8,128)} %get-tuple-element.13), calls=%async_computation.2 | async-start | bytes 1048576 | tf_op jit(solution)/shard_map/all_to_all | solution.py:120
  65.1 20.4 %collective-permute-start.2 = (f32[1,1024]{1,0:T(1,128)S(1)}, f32[1,1024]{1,0:T(1,128)S(1)}, u32[]{:S(2)}, u32[]{:S(2)}) collective-permute-start(f32[1,1024]{1,0:T(1,128)S(1)} %slice.48), channel_id=1, source_target_pairs={{0,1},{1,2},{2,3},{3,4},{4,5},{5,6},{6,7},{7,8},{8,9},{9,10},{10,1... | collective-permute-start | bytes 12296 | tf_op jit(solution)/shard_map/ppermute | solution.py:33
  81.1 0.8 copy-start
  85.5 24.3 %all-to-all-start.3 = ((f32[64,16,128]{2,1,0:T(8,128)}), f32[64,16,128]{2,1,0:T(8,128)S(1)}, u32[]{:S(2)}, u32[]{:S(2)}) async-start(f32[64,16,128]{2,1,0:T(8,128)} %get-tuple-element.17), calls=%async_computation.3 | async-start | bytes 1048576 | tf_op jit(solution)/shard_map/all_to_all | solution.py:120
  109.8 0.8 copy-start.2

commit v11 on v9

--- a/solution.py
+++ b/solution.py
@@ -102,9 +102,10 @@
     local_id = lax.rem(columns, tile_rows)
     remote = run_of != me
     runs = lax.broadcasted_iota(jnp.int32, (space_count, tile_rows * kept), 0)
-    flat_run = jnp.where(remote, run_of, -1).reshape(1, -1)
-    flat_id = local_id.reshape(1, -1)
-    hit = flat_run == runs
+    flat = columns.reshape(1, -1)
+    flat_run = lax.div(flat, tile_rows)
+    flat_id = lax.rem(flat, tile_rows)
+    hit = (flat_run == runs) & (flat_run != me)
     lo = jnp.min(jnp.where(hit, flat_id, tile_rows), axis=1)
     hi = jnp.max(jnp.where(hit, flat_id, -1), axis=1)
     lo = jnp.clip(lo, 0, tile_rows - 1)

time: 108 us -> 113 us (1.046)
  starting transfers between devices: 37.2 us -> 42.7 us
  local copies, waits for them, and re-layouts: 8.43 us -> 9.8 us
    all_to_all x1, waiting for transfers between devices: 8.43 us -> 1.35 us  [body(): send_ids = lax.all_to_all(request, 'space', 0, 0, tiled=True)[:, :2]]
    all_to_all x3, waiting for transfers between devices: 35.6 us -> 41.7 us  [exchange(): return lax.all_to_all(sent, 'space', 0, 0, tiled=True)]
    all_to_all x3, starting transfers between devices: 17.7 us -> 23.2 us  [exchange(): return lax.all_to_all(sent, 'space', 0, 0, tiled=True)]
  transfers between devices with their start and end apart: 7 -> 7, of which waited for: 4 -> 4; matrix products, arithmetic and copies ran while one was open for 8% -> 9% of each run, Pallas kernels for 7% -> 7%
where the time goes in v11:
time: 113 us; the launch traced here: 112 us
  waiting for transfers between devices  43.1 us (38%)
  starting transfers between devices  42.7 us (38%)
  Pallas kernels  11.1 us (10%)
  local copies, waits for them, and re-layouts  9.8 us (9%)
  other arithmetic  3.85 us (3%)
    all_to_all x3, waiting for transfers between devices, exchange(): return lax.all_to_all(sent, 'space', 0, 0, tiled=True)  41.7 us
    all_to_all x3, starting transfers between devices, exchange(): return lax.all_to_all(sent, 'space', 0, 0, tiled=True)  23.2 us
    all_to_all x1, starting transfers between devices, body(): send_ids = lax.all_to_all(request, 'space', 0, 0, tiled=True)[:, :2]  11.2 us
    pallas_call x3, Pallas kernels, substep(): pl.pallas_call(kernel, out_shape=tuple(out_shape), in_specs=[smem, smem,...  11.1 us
    ppermute x1, starting transfers between devices, with_halo(): lax.ppermute(lax.slice_in_dim(block, block.shape[dim] - width, None, axis...  4.43 us
    unnamed x17, local copies, waits for them, and re-layouts  2.56 us
    transpose x1, local copies, waits for them, and re-layouts, body(): tiles = tiles.transpose(0, 1, 3, 2).reshape(tile_rows, kept * TILE, TILE)  2.34 us
  transfers between devices with their start and end apart: 7, of which 4 were waited for; matrix products, arithmetic and copies ran while one was open for 9% of the time, Pallas kernels for 7%

profile of v11, /device:TPU:1, one launch (start us, length us, event | category | flops | bytes accessed | tf_op | source)
XLA Modules:
  0.0 112.5 jit_solution(4604834928899065011)
XLA Ops:
  0.6 0.0 copy-start.5
  0.7 0.8 reshape.174
  1.5 0.1 select_reduce_fusion
  1.6 0.7 broadcast_select_fusion.1
  2.4 11.2 %all-to-all-start = ((s32[32,1,128]{2,1,0:T(1,128)}), s32[32,1,128]{2,1,0:T(1,128)S(1)}, u32[]{:S(2)}, u32[]{:S(2)}) async-start(s32[32,1,128]{2,1,0:T(1,128)} %broadcast_select_fusion.1), calls=%async_computation | async-start | bytes 32768 | tf_op jit(solution)/shard_map/all_to_all | solution.py:115
  13.6 0.7 fusion.13
  14.3 4.4 %collective-permute-start = (f32[16,128]{1,0:T(8,128)S(1)}, f32[16,128]{1,0:T(8,128)S(1)}, u32[]{:S(2)}, u32[]{:S(2)}) collective-permute-start(f32[16,128]{1,0:T(8,128)S(1)} %get-tuple-element.26), channel_id=1, source_target_pairs={{0,16},{16,32},{32,48},{48,64},{64,80},{80,96},{96,112},{112,128},... | collective-permute-start | bytes 24584 | tf_op jit(solution)/shard_map/ppermute | solution.py:22
  18.8 1.9 %collective-permute-start.1 = (f32[16,128]{1,0:T(8,128)S(1)}, f32[16,128]{1,0:T(8,128)S(1)}, u32[]{:S(2)}, u32[]{:S(2)}) collective-permute-start(f32[16,128]{1,0:T(8,128)S(1)} %get-tuple-element.27), channel_id=1, source_target_pairs={{16,0},{32,16},{48,32},{64,48},{80,64},{96,80},{112,96},{128,112},... | collective-permute-start | bytes 24584 | tf_op jit(solution)/shard_map/ppermute | solution.py:25
  20.7 0.8 copy_bitcast_fusion
  21.5 1.3 %all-to-all-done = s32[32,1,128]{2,1,0:T(1,128)S(1)} async-done(((s32[32,1,128]{2,1,0:T(1,128)}), s32[32,1,128]{2,1,0:T(1,128)S(1)}, u32[]{:S(2)}, u32[]{:S(2)}) %all-to-all-start) | async-done | bytes 16416 | tf_op jit(solution)/shard_map/all_to_all | solution.py:115
  22.9 0.0 copy-start.4
  22.9 0.1 reshape.190
  23.0 1.4 %gather_fusion.1 = f32[64,16,128]{2,1,0:T(8,128)} fusion(f32[16,8,128]{2,0,1:T(8,128)S(1)} %copy_bitcast_fusion, s32[1024]{0:T(1024)S(1)} %pad_clamp_fusion), kind=kCustom, calls=%fused_computation.1 | custom fusion | bytes 1048832 | tf_op jit(solution)/shard_map/jit(_take)/gather | solution.py:139
  24.4 9.8 %all-to-all-start.1 = ((f32[64,16,128]{2,1,0:T(8,128)}), f32[64,16,128]{2,1,0:T(8,128)}, u32[]{:S(2)}, u32[]{:S(2)}) async-start(f32[64,16,128]{2,1,0:T(8,128)} %gather_fusion.1), calls=%async_computation.1 | async-start | bytes 1048576 | tf_op jit(solution)/shard_map/all_to_all | solution.py:121
  34.2 0.0 copy-done.5
  34.3 0.1 reshape.182
  34.4 0.0 copy-start.6
  34.4 0.0 copy-start
  34.4 0.8 gather_fusion
  35.2 0.0 copy-done.4
  35.2 0.1 reshape.181
  35.2 0.0 copy-done.6
  35.3 0.1 fusion.9
  35.4 0.9 copy-done
  36.3 2.3 %copy.33 = f32[8,6,128,128]{3,2,1,0:T(8,128)} copy(f32[8,6,128,128]{2,3,1,0:T(8,128)S(1)} %bitcast.27) | data formatting | bytes 6291456 | tf_op jit(solution)/shard_map/transpose | solution.py:123
  38.6 0.6 add_select_fusion.1.pick_ref
  39.2 13.2 %all-to-all-done.1.got_ref = f32[64,16,128]{2,1,0:T(8,128)} async-done(((f32[64,16,128]{2,1,0:T(8,128)}), f32[64,16,128]{2,1,0:T(8,128)}, u32[]{:S(2)}, u32[]{:S(2)}) %all-to-all-start.1) | async-done | bytes 524320 | tf_op jit(solution)/shard_map/all_to_all | solution.py:121
  52.5 3.8 %shard_map.90 = (f32[16,1024]{1,0:T(8,128)}, f32[16,1024]{1,0:T(8,128)}, f32[64,16,128]{2,1,0:T(8,128)}) custom-call(s32[8,6]{1,0:T(8,128)} %add_select_fusion.1.pick_ref, s32[32,2]{1,0:T(8,128)} %bitcast.29, f32[16,1024]{1,0:T(8,128)} %f_ref.1, f32[16,1024]{1,0:T(8,128)} %p_ref.1, f32[64,16,128]{2,1,0:T(8,128)} %all-to-all-done.1.got_ref, ...), custom_call_target="tpu_custom_call" | custom-call | tf_op jit(solution)/shard_map/pallas_call | solution.py:84
  56.2 0.0 copy-start.3
  56.2 5.1 %all-to-all-start.2 = ((f32[64,16,128]{2,1,0:T(8,128)}), f32[64,16,128]{2,1,0:T(8,128)S(1)}, u32[]{:S(2)}, u32[]{:S(2)}) async-start(f32[64,16,128]{2,1,0:T(8,128)} %get-tuple-element.13), calls=%async_computation.2 | async-start | bytes 1048576 | tf_op jit(solution)/shard_map/all_to_all | solution.py:121
  61.3 0.7 convert_reduce_fusion
  62.0 0.0 collective-permute-done
  62.1 0.0 collective-permute-done.1
  62.1 0.0 copy-done.3
  62.2 1.1 fusion
  63.3 1.9 %collective-permute-start.2 = (f32[1,1024]{1,0:T(1,128)S(1)}, f32[1,1024]{1,0:T(1,128)S(1)}, u32[]{:S(2)}, u32[]{:S(2)}) collective-permute-start(f32[1,1024]{1,0:T(1,128)S(1)} %slice.40), channel_id=1, source_target_pairs={{0,1},{1,2},{2,3},{3,4},{4,5},{5,6},{6,7},{7,8},{8,9},{9,10},{10,1... | collective-permute-start | bytes 12296 | tf_op jit(solution)/shard_map/ppermute | solution.py:33
  65.3 14.1 %all-to-all-done.2.got_ref = f32[64,16,128]{2,1,0:T(8,128)S(1)} async-done(((f32[64,16,128]{2,1,0:T(8,128)}), f32[64,16,128]{2,1,0:T(8,128)S(1)}, u32[]{:S(2)}, u32[]{:S(2)}) %all-to-all-start.2) | async-done | bytes 524320 | tf_op jit(solution)/shard_map/all_to_all | solution.py:121
  79.4 0.0 copy-start.2
  79.4 0.8 copy-done.2
  80.2 3.8 %shard_map.91 = (f32[16,1024]{1,0:T(8,128)}, f32[16,1024]{1,0:T(8,128)}, f32[64,16,128]{2,1,0:T(8,128)}) custom-call(s32[8,6]{1,0:T(8,128)} %add_select_fusion.1.pick_ref, s32[32,2]{1,0:T(8,128)} %bitcast.30, f32[16,1024]{1,0:T(8,128)} %get-tuple-element.11.f_ref, f32[16,1024]{1,0:T(8,128)} %get-tuple-element.12.p_ref, f32[64,16,128]{2,1,0:T(8,128)} %copy-done.2, ...), custom_call_target="tpu_custom_call" | custom-call | tf_op jit(solution)/shard_map/pallas_call | solution.py:84
  84.0 0.0 collective-permute-done.2
  84.0 8.3 %all-to-all-start.3 = ((f32[64,16,128]{2,1,0:T(8,128)}), f32[64,16,128]{2,1,0:T(8,128)S(1)}, u32[]{:S(2)}, u32[]{:S(2)}) async-start(f32[64,16,128]{2,1,0:T(8,128)} %get-tuple-element.17), calls=%async_computation.3 | async-start | bytes 1048576 | tf_op jit(solution)/shard_map/all_to_all | solution.py:121
  92.3 1.5 %multiply_multiply_fusion = f32[16,1024]{1,0:T(8,128)} fusion(f32[16,1024]{1,0:T(8,128)S(1)} %copy-done.3, f32[15,1024]{1,0:T(8,128)S(1)} %bitcast.32, f32[1,1024]{1,0:T(1,128)S(1)} %broadcast_multiply_fusion, f32[16,1024]{1,0:T(8,128)} %get-tuple-element.8.f_ref), kind=kLoop, calls=%fused_computation.15 | loop fusion | flops 114688 | bytes 262144 | tf_op jit(solution)/shard_map/mul | solution.py:152
  93.8 14.4 %all-to-all-done.3.got_ref = f32[64,16,128]{2,1,0:T(8,128)S(1)} async-done(((f32[64,16,128]{2,1,0:T(8,128)}), f32[64,16,128]{2,1,0:T(8,128)S(1)}, u32[]{:S(2)}, u32[]{:S(2)}) %all-to-all-start.3) | async-done | bytes 524320 | tf_op jit(solution)/shard_map/all_to_all | solution.py:121
  108.1 0.0 copy-start.1
  108.1 0.8 copy-done.1
  108.9 3.5 %shard_map.92 = f32[16,1024]{1,0:T(8,128)} custom-call(s32[8,6]{1,0:T(8,128)} %add_select_fusion.1.pick_ref, s32[32,2]{1,0:T(8,128)} %bitcast.31, f32[16,1024]{1,0:T(8,128)} %get-tuple-element.8.f_ref, f32[16,1024]{1,0:T(8,128)} %get-tuple-element.15.p_ref, f32[64,16,128]{2,1,0:T(8,128)} %copy-done.1, f32[8,768,128]{2,1,0:T(8,128)} %bitcast.26), custom_call_target="tpu_custom_call" | custom-call | tf_op jit(solution)/shard_map/pallas_call | solution.py:84
  (19 shorter events, 0.2 us)
Async XLA Ops:
  0.6 33.6 %copy-start.5 = (s32[8,6]{1,0:T(8,128)S(1)}, s32[8,6]{1,0:T(8,128)}, u32[]{:S(2)}) copy-start(s32[8,6]{1,0:T(8,128)} %param.10) | copy-start | bytes 580
  2.4 20.5 %all-to-all-start = ((s32[32,1,128]{2,1,0:T(1,128)}), s32[32,1,128]{2,1,0:T(1,128)S(1)}, u32[]{:S(2)}, u32[]{:S(2)}) async-start(s32[32,1,128]{2,1,0:T(1,128)} %broadcast_select_fusion.1), calls=%async_computation | async-start | bytes 32768 | tf_op jit(solution)/shard_map/all_to_all | solution.py:115
  14.3 47.7 %collective-permute-start = (f32[16,128]{1,0:T(8,128)S(1)}, f32[16,128]{1,0:T(8,128)S(1)}, u32[]{:S(2)}, u32[]{:S(2)}) collective-permute-start(f32[16,128]{1,0:T(8,128)S(1)} %get-tuple-element.26), channel_id=1, source_target_pairs={{0,16},{16,32},{32,48},{48,64},{64,80},{80,96},{96,112},{112,128},... | collective-permute-start | bytes 24584 | tf_op jit(solution)/shard_map/ppermute | solution.py:22
  18.8 43.3 %collective-permute-start.1 = (f32[16,128]{1,0:T(8,128)S(1)}, f32[16,128]{1,0:T(8,128)S(1)}, u32[]{:S(2)}, u32[]{:S(2)}) collective-permute-start(f32[16,128]{1,0:T(8,128)S(1)} %get-tuple-element.27), channel_id=1, source_target_pairs={{16,0},{32,16},{48,32},{64,48},{80,64},{96,80},{112,96},{128,112},... | collective-permute-start | bytes 24584 | tf_op jit(solution)/shard_map/ppermute | solution.py:25
  22.9 12.3 %copy-start.4 = (s32[32,1,128]{2,1,0:T(1,128)}, s32[32,1,128]{2,1,0:T(1,128)S(1)}, u32[]{:S(2)}) copy-start(s32[32,1,128]{2,1,0:T(1,128)S(1)} %all-to-all-done) | copy-start | bytes 49156
  24.4 28.0 %all-to-all-start.1 = ((f32[64,16,128]{2,1,0:T(8,128)}), f32[64,16,128]{2,1,0:T(8,128)}, u32[]{:S(2)}, u32[]{:S(2)}) async-start(f32[64,16,128]{2,1,0:T(8,128)} %gather_fusion.1), calls=%async_computation.1 | async-start | bytes 1048576 | tf_op jit(solution)/shard_map/all_to_all | solution.py:121
  34.4 0.9 copy-start.6
  34.4 1.9 %copy-start = (f32[8,6,128,128]{3,2,1,0:T(8,128)S(1)}, f32[8,6,128,128]{3,2,1,0:T(8,128)}, u32[]{:S(2)}) copy-start(f32[8,6,128,128]{3,2,1,0:T(8,128)} %param.9) | copy-start | bytes 9437188
  56.2 5.8 %copy-start.3 = (f32[16,1024]{1,0:T(8,128)S(1)}, f32[16,1024]{1,0:T(8,128)}, u32[]{:S(2)}) copy-start(f32[16,1024]{1,0:T(8,128)} %param.8) | copy-start | bytes 196612
  56.2 23.2 %all-to-all-start.2 = ((f32[64,16,128]{2,1,0:T(8,128)}), f32[64,16,128]{2,1,0:T(8,128)S(1)}, u32[]{:S(2)}, u32[]{:S(2)}) async-start(f32[64,16,128]{2,1,0:T(8,128)} %get-tuple-element.13), calls=%async_computation.2 | async-start | bytes 1048576 | tf_op jit(solution)/shard_map/all_to_all | solution.py:121
  63.3 20.6 %collective-permute-start.2 = (f32[1,1024]{1,0:T(1,128)S(1)}, f32[1,1024]{1,0:T(1,128)S(1)}, u32[]{:S(2)}, u32[]{:S(2)}) collective-permute-start(f32[1,1024]{1,0:T(1,128)S(1)} %slice.40), channel_id=1, source_target_pairs={{0,1},{1,2},{2,3},{3,4},{4,5},{5,6},{6,7},{7,8},{8,9},{9,10},{10,1... | collective-permute-start | bytes 12296 | tf_op jit(solution)/shard_map/ppermute | solution.py:33
  79.4 0.8 copy-start.2
  84.0 24.2 %all-to-all-start.3 = ((f32[64,16,128]{2,1,0:T(8,128)}), f32[64,16,128]{2,1,0:T(8,128)S(1)}, u32[]{:S(2)}, u32[]{:S(2)}) async-start(f32[64,16,128]{2,1,0:T(8,128)} %get-tuple-element.17), calls=%async_computation.3 | async-start | bytes 1048576 | tf_op jit(solution)/shard_map/all_to_all | solution.py:121
  108.1 0.8 copy-start.1

commit v12 on v9

--- a/solution.py
+++ b/solution.py
@@ -120,6 +120,7 @@
         return lax.all_to_all(sent, "space", 0, 0, tiled=True)
 
     tiles = tiles.transpose(0, 1, 3, 2).reshape(tile_rows, kept * TILE, TILE)
+    send_ids, tiles, pick = lax.optimization_barrier((send_ids, tiles, pick))
     total_sites = site_count * space_count
     first_site = me * site_count
     lookup = (neighbours - first_site + TILE) % total_sites

time: 108 us -> 108 us (level)
  waiting for transfers between devices: 44 us -> 45.1 us
    all_to_all x3, waiting for transfers between devices: 35.6 us -> 40.2 us  [exchange(): return lax.all_to_all(sent, 'space', 0, 0, tiled=True)]
    all_to_all x1, waiting for transfers between devices: 8.43 us -> 4.9 us  [body(): send_ids = lax.all_to_all(request, 'space', 0, 0, tiled=True)[:, :2]]
    unnamed x17 -> x21, local copies, waits for them, and re-layouts: 2.56 us -> 2.88 us
  transfers between devices with their start and end apart: 7 -> 7, of which waited for: 4 -> 4; matrix products, arithmetic and copies ran while one was open for 8% -> 7% of each run, Pallas kernels for 7% -> 7%
where the time goes in v12:
time: 108 us
  waiting for transfers between devices  45.1 us (42%)
  starting transfers between devices  37.3 us (35%)
  Pallas kernels  11 us (10%)
  local copies, waits for them, and re-layouts  7.89 us (7%)
  other arithmetic  4.52 us (4%)
  matrix products  1.09 us (1%)
    all_to_all x3, waiting for transfers between devices, exchange(): return lax.all_to_all(sent, 'space', 0, 0, tiled=True)  40.2 us
    all_to_all x3, starting transfers between devices, exchange(): return lax.all_to_all(sent, 'space', 0, 0, tiled=True)  17.8 us
    all_to_all x1, starting transfers between devices, body(): send_ids = lax.all_to_all(request, 'space', 0, 0, tiled=True)[:, :2]  11.2 us
    pallas_call x3, Pallas kernels, substep(): pl.pallas_call(kernel, out_shape=tuple(out_shape), in_specs=[smem, smem,...  11 us
    all_to_all x1, waiting for transfers between devices, body(): send_ids = lax.all_to_all(request, 'space', 0, 0, tiled=True)[:, :2]  4.9 us
    ppermute x1, starting transfers between devices, with_halo(): lax.ppermute(lax.slice_in_dim(block, block.shape[dim] - width, None, axis...  4.44 us
    unnamed x21, local copies, waits for them, and re-layouts  2.88 us
    transpose x1, local copies, waits for them, and re-layouts, body(): tiles = tiles.transpose(0, 1, 3, 2).reshape(tile_rows, kept * TILE, TILE)  2.33 us
  transfers between devices with their start and end apart: 7, of which 4 were waited for; matrix products, arithmetic and copies ran while one was open for 7% of the time, Pallas kernels for 7%

profile of v12, /device:TPU:1, one launch (start us, length us, event | category | flops | bytes accessed | tf_op | source)
XLA Modules:
  0.0 107.8 jit_solution(143993397617385220)
XLA Ops:
  0.6 0.7 compare_select_fusion
  1.3 0.1 eq.49
  1.4 0.1 broadcast_in_dim.62
  1.5 0.1 select_reduce_fusion
  1.6 0.7 broadcast_select_fusion.1
  2.4 11.2 %all-to-all-start = ((s32[32,1,128]{2,1,0:T(1,128)}), s32[32,1,128]{2,1,0:T(1,128)S(1)}, u32[]{:S(2)}, u32[]{:S(2)}) async-start(s32[32,1,128]{2,1,0:T(1,128)} %broadcast_select_fusion.1), calls=%async_computation | async-start | bytes 32768 | tf_op jit(solution)/shard_map/all_to_all | solution.py:114
  13.6 0.1 reshape.120
  13.7 0.0 copy-start.6
  13.7 0.0 copy-start.8
  13.7 0.0 copy-start
  13.7 0.8 gather_fusion
  14.5 0.1 reshape.119
  14.6 0.0 copy-done.6
  14.6 0.0 copy-done.8
  14.6 0.6 compare_select_fusion.1.pick_ref
  15.2 0.4 copy-done
  15.7 2.3 %copy.32 = f32[8,6,128,128]{3,2,1,0:T(8,128)} copy(f32[8,6,128,128]{2,3,1,0:T(8,128)S(1)} %bitcast.27) | data formatting | bytes 6291456 | tf_op jit(solution)/shard_map/transpose | solution.py:122
  18.0 0.0 copy-start.4
  18.0 0.0 copy-start.7
  18.0 4.9 %all-to-all-done = s32[32,1,128]{2,1,0:T(1,128)S(1)} async-done(((s32[32,1,128]{2,1,0:T(1,128)}), s32[32,1,128]{2,1,0:T(1,128)S(1)}, u32[]{:S(2)}, u32[]{:S(2)}) %all-to-all-start) | async-done | bytes 16416 | tf_op jit(solution)/shard_map/all_to_all | solution.py:114
  22.9 0.0 copy-start.5
  22.9 0.1 reshape.128
  23.0 1.4 %gather_fusion.1 = f32[64,16,128]{2,1,0:T(8,128)} fusion(f32[16,8,128]{2,0,1:T(8,128)S(1)} %copy_bitcast_fusion, s32[1024]{0:T(1024)S(1)} %pad_clamp_fusion), kind=kCustom, calls=%fused_computation.1 | custom fusion | bytes 1048832 | tf_op jit(solution)/shard_map/jit(_take)/gather | solution.py:139
  24.4 4.9 %all-to-all-start.1 = ((f32[64,16,128]{2,1,0:T(8,128)}), f32[64,16,128]{2,1,0:T(8,128)S(1)}, u32[]{:S(2)}, u32[]{:S(2)}) async-start(f32[64,16,128]{2,1,0:T(8,128)} %gather_fusion.1), calls=%async_computation.1 | async-start | bytes 1048576 | tf_op jit(solution)/shard_map/all_to_all | solution.py:120
  29.3 0.0 copy-done.4
  29.4 4.4 %collective-permute-start = (f32[16,128]{1,0:T(8,128)S(1)}, f32[16,128]{1,0:T(8,128)S(1)}, u32[]{:S(2)}, u32[]{:S(2)}) collective-permute-start(f32[16,128]{1,0:T(8,128)S(1)} %get-tuple-element.30), channel_id=1, source_target_pairs={{0,16},{16,32},{32,48},{48,64},{64,80},{80,96},{96,112},{112,128},... | collective-permute-start | bytes 24584 | tf_op jit(solution)/shard_map/ppermute | solution.py:22
  33.8 1.9 %collective-permute-start.1 = (f32[16,128]{1,0:T(8,128)S(1)}, f32[16,128]{1,0:T(8,128)S(1)}, u32[]{:S(2)}, u32[]{:S(2)}) collective-permute-start(f32[16,128]{1,0:T(8,128)S(1)} %get-tuple-element.31), channel_id=1, source_target_pairs={{16,0},{32,16},{48,32},{64,48},{80,64},{96,80},{112,96},{128,112},... | collective-permute-start | bytes 24584 | tf_op jit(solution)/shard_map/ppermute | solution.py:25
  35.7 0.0 copy-done.7
  35.8 0.1 fusion.8
  35.9 11.7 %all-to-all-done.1.got_ref = f32[64,16,128]{2,1,0:T(8,128)S(1)} async-done(((f32[64,16,128]{2,1,0:T(8,128)}), f32[64,16,128]{2,1,0:T(8,128)S(1)}, u32[]{:S(2)}, u32[]{:S(2)}) %all-to-all-start.1) | async-done | bytes 524320 | tf_op jit(solution)/shard_map/all_to_all | solution.py:120
  47.6 0.0 copy-done.5
  47.6 0.0 copy-start.3
  47.6 0.8 copy-done.3
  48.4 3.8 %shard_map.100 = (f32[16,1024]{1,0:T(8,128)}, f32[16,1024]{1,0:T(8,128)}, f32[64,16,128]{2,1,0:T(8,128)}) custom-call(s32[8,6]{1,0:T(8,128)} %compare_select_fusion.1.pick_ref, s32[32,2]{1,0:T(8,128)} %bitcast.29, f32[16,1024]{1,0:T(8,128)} %f_ref.1, f32[16,1024]{1,0:T(8,128)} %p_ref.1, f32[64,16,128]{2,1,0:T(8,128)} %copy-done.3, f32[8,768,128]{2,1,0:T(8,128)} %bitcast.24), custom_call_target="tpu_custom_call" | custom-call | tf_op jit(solution)/shard_map/pallas_call | solution.py:84
  52.1 5.0 %all-to-all-start.2 = ((f32[64,16,128]{2,1,0:T(8,128)}), f32[64,16,128]{2,1,0:T(8,128)S(1)}, u32[]{:S(2)}, u32[]{:S(2)}) async-start(f32[64,16,128]{2,1,0:T(8,128)} %get-tuple-element.19), calls=%async_computation.2 | async-start | bytes 1048576 | tf_op jit(solution)/shard_map/all_to_all | solution.py:120
  57.1 0.7 convert_reduce_fusion
  57.8 0.0 collective-permute-done
  57.9 0.0 collective-permute-done.1
  58.0 1.1 %fusion = f32[8,2,8,128]{3,2,1,0:T(8,128)S(1)} fusion(f32[8,384,128]{2,1,0:T(8,128)S(1)} %convert_reduce_fusion, f32[16,8,128]{2,0,1:T(8,128)S(1)} %copy.41, f32[16,8,128]{2,0,1:T(8,128)S(1)} %copy.40, f32[16,8,128]{2,0,1:T(8,128)S(1)} %copy.39), kind=kOutput, calls=%fused_computation.5 | convolution fusion | flops 75612160 | bytes 1835008 | tf_op jit(solution)/shard_map/tbj,bji->tbi/dot_general | solution.py:136
  59.1 1.9 %collective-permute-start.2 = (f32[1,1024]{1,0:T(1,128)S(1)}, f32[1,1024]{1,0:T(1,128)S(1)}, u32[]{:S(2)}, u32[]{:S(2)}) collective-permute-start(f32[1,1024]{1,0:T(1,128)S(1)} %slice.40), channel_id=1, source_target_pairs={{0,1},{1,2},{2,3},{3,4},{4,5},{5,6},{6,7},{7,8},{8,9},{9,10},{10,1... | collective-permute-start | bytes 12296 | tf_op jit(solution)/shard_map/ppermute | solution.py:33
  61.1 14.1 %all-to-all-done.2.got_ref = f32[64,16,128]{2,1,0:T(8,128)S(1)} async-done(((f32[64,16,128]{2,1,0:T(8,128)}), f32[64,16,128]{2,1,0:T(8,128)S(1)}, u32[]{:S(2)}, u32[]{:S(2)}) %all-to-all-start.2) | async-done | bytes 524320 | tf_op jit(solution)/shard_map/all_to_all | solution.py:120
  75.2 0.0 copy-start.2
  75.2 0.8 copy-done.2
  76.0 3.8 %shard_map.101 = (f32[16,1024]{1,0:T(8,128)}, f32[16,1024]{1,0:T(8,128)}, f32[64,16,128]{2,1,0:T(8,128)}) custom-call(s32[8,6]{1,0:T(8,128)} %compare_select_fusion.1.pick_ref, s32[32,2]{1,0:T(8,128)} %bitcast.30, f32[16,1024]{1,0:T(8,128)} %get-tuple-element.17.f_ref, f32[16,1024]{1,0:T(8,128)} %get-tuple-element.18.p_ref, f32[64,16,128]{2,1,0:T(8,128)} %copy-done.2, ...), custom_call_target="tpu_custom_call" | custom-call | tf_op jit(solution)/shard_map/pallas_call | solution.py:84
  79.7 0.0 collective-permute-done.2
  79.7 7.9 %all-to-all-start.3 = ((f32[64,16,128]{2,1,0:T(8,128)}), f32[64,16,128]{2,1,0:T(8,128)S(1)}, u32[]{:S(2)}, u32[]{:S(2)}) async-start(f32[64,16,128]{2,1,0:T(8,128)} %get-tuple-element.23), calls=%async_computation.3 | async-start | bytes 1048576 | tf_op jit(solution)/shard_map/all_to_all | solution.py:120
  87.6 1.5 %multiply_multiply_fusion = f32[16,1024]{1,0:T(8,128)} fusion(f32[16,1024]{1,0:T(8,128)S(1)} %copy-done.4, f32[15,1024]{1,0:T(8,128)S(1)} %bitcast.32, f32[1,1024]{1,0:T(1,128)S(1)} %broadcast_multiply_fusion, f32[16,1024]{1,0:T(8,128)} %get-tuple-element.11.f_ref), kind=kLoop, calls=%fused_computation.15 | loop fusion | flops 114688 | bytes 262144 | tf_op jit(solution)/shard_map/mul | solution.py:152
  89.1 14.4 %all-to-all-done.3.got_ref = f32[64,16,128]{2,1,0:T(8,128)S(1)} async-done(((f32[64,16,128]{2,1,0:T(8,128)}), f32[64,16,128]{2,1,0:T(8,128)S(1)}, u32[]{:S(2)}, u32[]{:S(2)}) %all-to-all-start.3) | async-done | bytes 524320 | tf_op jit(solution)/shard_map/all_to_all | solution.py:120
  103.5 0.0 copy-start.1
  103.5 0.8 copy-done.1
  104.3 3.5 %shard_map.102 = f32[16,1024]{1,0:T(8,128)} custom-call(s32[8,6]{1,0:T(8,128)} %compare_select_fusion.1.pick_ref, s32[32,2]{1,0:T(8,128)} %bitcast.31, f32[16,1024]{1,0:T(8,128)} %get-tuple-element.11.f_ref, f32[16,1024]{1,0:T(8,128)} %get-tuple-element.21.p_ref, f32[64,16,128]{2,1,0:T(8,128)} %copy-done.1, f32[8,768,128]{2,1,0:T(8,128)} %bitcast.26), custom_call_target="tpu_custom_call" | custom-call | tf_op jit(solution)/shard_map/pallas_call | solution.py:84
  (18 shorter events, 0.2 us)
Async XLA Ops:
  2.4 20.5 %all-to-all-start = ((s32[32,1,128]{2,1,0:T(1,128)}), s32[32,1,128]{2,1,0:T(1,128)S(1)}, u32[]{:S(2)}, u32[]{:S(2)}) async-start(s32[32,1,128]{2,1,0:T(1,128)} %broadcast_select_fusion.1), calls=%async_computation | async-start | bytes 32768 | tf_op jit(solution)/shard_map/all_to_all | solution.py:114
  13.7 0.9 copy-start.6
  13.7 0.9 copy-start.8
  13.7 1.9 %copy-start = (f32[8,6,128,128]{3,2,1,0:T(8,128)S(1)}, f32[8,6,128,128]{3,2,1,0:T(8,128)}, u32[]{:S(2)}) copy-start(f32[8,6,128,128]{3,2,1,0:T(8,128)} %param.9) | copy-start | bytes 9437188
  18.0 11.3 %copy-start.4 = (f32[16,1024]{1,0:T(8,128)S(1)}, f32[16,1024]{1,0:T(8,128)}, u32[]{:S(2)}) copy-start(f32[16,1024]{1,0:T(8,128)} %param.8) | copy-start | bytes 196612
  18.0 17.8 %copy-start.7 = (s32[3,1024]{1,0:T(4,128)S(1)}, s32[3,1024]{1,0:T(4,128)}, u32[]{:S(2)}) copy-start(s32[3,1024]{1,0:T(4,128)} %param.11) | copy-start | bytes 36868
  22.9 24.7 %copy-start.5 = (s32[32,1,128]{2,1,0:T(1,128)}, s32[32,1,128]{2,1,0:T(1,128)S(1)}, u32[]{:S(2)}) copy-start(s32[32,1,128]{2,1,0:T(1,128)S(1)} %all-to-all-done) | copy-start | bytes 49156
  24.4 23.1 %all-to-all-start.1 = ((f32[64,16,128]{2,1,0:T(8,128)}), f32[64,16,128]{2,1,0:T(8,128)S(1)}, u32[]{:S(2)}, u32[]{:S(2)}) async-start(f32[64,16,128]{2,1,0:T(8,128)} %gather_fusion.1), calls=%async_computation.1 | async-start | bytes 1048576 | tf_op jit(solution)/shard_map/all_to_all | solution.py:120
  29.4 28.5 %collective-permute-start = (f32[16,128]{1,0:T(8,128)S(1)}, f32[16,128]{1,0:T(8,128)S(1)}, u32[]{:S(2)}, u32[]{:S(2)}) collective-permute-start(f32[16,128]{1,0:T(8,128)S(1)} %get-tuple-element.30), channel_id=1, source_target_pairs={{0,16},{16,32},{32,48},{48,64},{64,80},{80,96},{96,112},{112,128},... | collective-permute-start | bytes 24584 | tf_op jit(solution)/shard_map/ppermute | solution.py:22
  33.8 24.1 %collective-permute-start.1 = (f32[16,128]{1,0:T(8,128)S(1)}, f32[16,128]{1,0:T(8,128)S(1)}, u32[]{:S(2)}, u32[]{:S(2)}) collective-permute-start(f32[16,128]{1,0:T(8,128)S(1)} %get-tuple-element.31), channel_id=1, source_target_pairs={{16,0},{32,16},{48,32},{64,48},{80,64},{96,80},{112,96},{128,112},... | collective-permute-start | bytes 24584 | tf_op jit(solution)/shard_map/ppermute | solution.py:25
  47.6 0.8 copy-start.3
  52.1 23.0 %all-to-all-start.2 = ((f32[64,16,128]{2,1,0:T(8,128)}), f32[64,16,128]{2,1,0:T(8,128)S(1)}, u32[]{:S(2)}, u32[]{:S(2)}) async-start(f32[64,16,128]{2,1,0:T(8,128)} %get-tuple-element.19), calls=%async_computation.2 | async-start | bytes 1048576 | tf_op jit(solution)/shard_map/all_to_all | solution.py:120
  59.1 20.6 %collective-permute-start.2 = (f32[1,1024]{1,0:T(1,128)S(1)}, f32[1,1024]{1,0:T(1,128)S(1)}, u32[]{:S(2)}, u32[]{:S(2)}) collective-permute-start(f32[1,1024]{1,0:T(1,128)S(1)} %slice.40), channel_id=1, source_target_pairs={{0,1},{1,2},{2,3},{3,4},{4,5},{5,6},{6,7},{7,8},{8,9},{9,10},{10,1... | collective-permute-start | bytes 12296 | tf_op jit(solution)/shard_map/ppermute | solution.py:33
  75.2 0.8 copy-start.2
  79.7 23.8 %all-to-all-start.3 = ((f32[64,16,128]{2,1,0:T(8,128)}), f32[64,16,128]{2,1,0:T(8,128)S(1)}, u32[]{:S(2)}, u32[]{:S(2)}) async-start(f32[64,16,128]{2,1,0:T(8,128)} %get-tuple-element.23), calls=%async_computation.3 | async-start | bytes 1048576 | tf_op jit(solution)/shard_map/all_to_all | solution.py:120
  103.5 0.8 copy-start.1

commit v13 on v9

--- a/solution.py
+++ b/solution.py
@@ -45,21 +45,26 @@
     return part(a_hi, b_hi) + (part(a_hi, b_lo) + part(a_lo, b_hi))
 
 
-def substep(field, moment, got, tiles, pick, send_ids, scale, advance, send):
+def substep(field, moment, got, tiles, pick, send_ids, scale, advance, send, local=None):
     slices, site_count = field.shape
-    rows, kept = tiles.shape[0], tiles.shape[1] // TILE
+    rows = tiles.shape[0]
+    kept = tiles.shape[1] // TILE + (0 if local is None else 1)
     slots = send_ids.shape[0] * send_ids.shape[1]
 
     def kernel(pick_ref, sid_ref, f_ref, p_ref, got_ref, tiles_ref, *refs):
         outs = list(refs)
+        local_ref = outs.pop(0) if local is not None else None
         p_out = outs.pop(0)
         f_out = outs.pop(0) if advance else None
         send_out = outs.pop(0) if send else None
         held = outs.pop(0) if send else None
         for r in range(rows):
             cols = slice(r * TILE, (r + 1) * TILE)
-            pieces = [f_ref[:, cols]] + [got_ref[pick_ref[r, k]] for k in range(1, kept)]
-            acc = split_dot(jnp.concatenate(pieces, axis=1), tiles_ref[r])
+            pieces = [got_ref[pick_ref[r, k]] for k in range(1, kept)]
+            if local is None:
+                acc = split_dot(jnp.concatenate([f_ref[:, cols]] + pieces, axis=1), tiles_ref[r])
+            else:
+                acc = local_ref[:, cols] + split_dot(jnp.concatenate(pieces, axis=1), tiles_ref[r])
             p_new = p_ref[:, cols] - scale * acc
             p_out[:, cols] = p_new
             if advance:
@@ -84,10 +89,10 @@
     return pl.pallas_call(
         kernel,
         out_shape=tuple(out_shape),
-        in_specs=[smem, smem, vmem, vmem, vmem, vmem],
+        in_specs=[smem, smem, vmem, vmem, vmem, vmem] + ([] if local is None else [vmem]),
         out_specs=tuple([vmem] * len(out_shape)),
         scratch_shapes=scratch,
-    )(pick, send_ids, field, moment, got, tiles)
+    )(pick, send_ids, field, moment, got, tiles, *([] if local is None else [local]))
 
 
 def body(field, momentum, solution, tiles, columns, neighbours):
@@ -119,6 +124,8 @@
     def exchange(sent):
         return lax.all_to_all(sent, "space", 0, 0, tiled=True)
 
+    own_tiles = tiles[:, 0]
+    remote_tiles = tiles[:, 1:].transpose(0, 1, 3, 2).reshape(tile_rows, (kept - 1) * TILE, TILE)
     tiles = tiles.transpose(0, 1, 3, 2).reshape(tile_rows, kept * TILE, TILE)
     total_sites = site_count * space_count
     first_site = me * site_count
@@ -143,7 +150,12 @@
     moment, field_two, sent = substep(field_one, moment, got, tiles, pick, send_ids, step_size, True, True)
     sent, arrived = lax.optimization_barrier((sent, arrived))
     got = exchange(sent)
-    (moment,) = substep(field_two, moment, got, tiles, pick, send_ids, 0.5 * step_size, False, False)
+    local = jnp.einsum(
+        "rij,trj->tri", own_tiles, field_two.reshape(slices, tile_rows, TILE), precision=lax.Precision.HIGHEST
+    ).reshape(slices, site_count)
+    (moment,) = substep(
+        field_two, moment, got, remote_tiles, pick, send_ids, 0.5 * step_size, False, False, local
+    )
 
     earlier = jnp.concatenate([parity_sign * arrived, hopped[:-1]], axis=0)
     link_factor = jnp.exp(coupling * field_two)

time: 108 us -> 107 us (level)
  waiting for transfers between devices: 44 us -> 35.7 us
  local copies, waits for them, and re-layouts: 8.43 us -> 12.4 us
  matrix products: 1.09 us -> 3.41 us
  starting transfers between devices: 37.2 us -> 38.4 us
    all_to_all x3, waiting for transfers between devices: 35.6 us -> 27.2 us  [exchange(): return lax.all_to_all(sent, 'space', 0, 0, tiled=True)]
    transpose x0 -> x2, local copies, waits for them, and re-layouts: none -> 5.07 us  [body(): tiles[:, 1:].transpose(0, 1, 3, 2)]
    unnamed x17 -> x15, local copies, waits for them, and re-layouts: 2.56 us -> 0.07 us
    dot_general x1, matrix products: 1.09 us -> 2.5 us  [body(): jnp.einsum('tbj,bji->tbi', windows, adjacency, precision=lax.Precision.HI...]
    reduce_sum x1, other arithmetic: 0.7 us -> 1.86 us  [body(): jnp.sum((offsets[:, :, None, :] == window).astype(jnp.float32), axis=1)]
    all_to_all x3, starting transfers between devices: 17.7 us -> 18.8 us  [exchange(): return lax.all_to_all(sent, 'space', 0, 0, tiled=True)]
  transfers between devices with their start and end apart: 7 -> 7, of which waited for: 4 -> 4; matrix products, arithmetic and copies ran while one was open for 8% -> 16% of each run, Pallas kernels for 7% -> 7%
where the time goes in v13:
time: 107 us; the launch traced here: 106 us
  starting transfers between devices  38.4 us (36%)
  waiting for transfers between devices  35.7 us (33%)
  local copies, waits for them, and re-layouts  12.4 us (12%)
  Pallas kernels  10.9 us (10%)
  other arithmetic  4.83 us (5%)
  matrix products  3.41 us (3%)
    all_to_all x3, waiting for transfers between devices, exchange(): return lax.all_to_all(sent, 'space', 0, 0, tiled=True)  27.2 us
    all_to_all x3, starting transfers between devices, exchange(): return lax.all_to_all(sent, 'space', 0, 0, tiled=True)  18.8 us
    all_to_all x1, starting transfers between devices, body(): send_ids = lax.all_to_all(request, 'space', 0, 0, tiled=True)[:, :2]  11.2 us
    pallas_call x3, Pallas kernels, substep(): pl.pallas_call(kernel, out_shape=tuple(out_shape), in_specs=[smem, smem,...  10.9 us
    all_to_all x1, waiting for transfers between devices, body(): send_ids = lax.all_to_all(request, 'space', 0, 0, tiled=True)[:, :2]  8.43 us
    transpose x2, local copies, waits for them, and re-layouts, body(): tiles[:, 1:].transpose(0, 1, 3, 2)  5.07 us
    ppermute x1, starting transfers between devices, with_halo(): lax.ppermute(lax.slice_in_dim(block, block.shape[dim] - width, None, axis...  4.13 us
    dot_general x1, matrix products, body(): jnp.einsum('tbj,bji->tbi', windows, adjacency, precision=lax.Precision.HI...  2.5 us
  transfers between devices with their start and end apart: 7, of which 4 were waited for; matrix products, arithmetic and copies ran while one was open for 16% of the time, Pallas kernels for 7%

profile of v13, /device:TPU:1, one launch (start us, length us, event | category | flops | bytes accessed | tf_op | source)
XLA Modules:
  0.0 106.4 jit_solution(2378188303333019307)
XLA Ops:
  0.6 0.7 compare_select_fusion
  1.3 0.1 broadcast_in_dim.62
  1.4 0.1 eq.47
  1.5 0.1 select_reduce_fusion
  1.6 0.7 broadcast_select_fusion.1
  2.4 11.2 %all-to-all-start = ((s32[32,1,128]{2,1,0:T(1,128)}), s32[32,1,128]{2,1,0:T(1,128)S(1)}, u32[]{:S(2)}, u32[]{:S(2)}) async-start(s32[32,1,128]{2,1,0:T(1,128)} %broadcast_select_fusion.1), calls=%async_computation | async-start | bytes 32768 | tf_op jit(solution)/shard_map/all_to_all | solution.py:119
  13.6 0.8 copy_bitcast_fusion.1
  14.5 8.4 %all-to-all-done = s32[32,1,128]{2,1,0:T(1,128)S(1)} async-done(((s32[32,1,128]{2,1,0:T(1,128)}), s32[32,1,128]{2,1,0:T(1,128)S(1)}, u32[]{:S(2)}, u32[]{:S(2)}) %all-to-all-start) | async-done | bytes 16416 | tf_op jit(solution)/shard_map/all_to_all | solution.py:119
  22.9 0.0 copy-start.3
  22.9 0.1 reshape.140
  23.0 1.4 %gather_fusion.1 = f32[64,16,128]{2,1,0:T(8,128)} fusion(f32[16,8,128]{2,0,1:T(8,128)S(1)} %copy_bitcast_fusion.1, s32[1024]{0:T(1024)S(1)} %pad_clamp_fusion), kind=kCustom, calls=%fused_computation.1 | custom fusion | bytes 1048832 | tf_op jit(solution)/shard_map/jit(_take)/gather | solution.py:145
  24.5 0.0 copy-start
  24.5 5.1 %all-to-all-start.1 = ((f32[64,16,128]{2,1,0:T(8,128)}), f32[64,16,128]{2,1,0:T(8,128)}, u32[]{:S(2)}, u32[]{:S(2)}) async-start(f32[64,16,128]{2,1,0:T(8,128)} %gather_fusion.1), calls=%async_computation.1 | async-start | bytes 1048576 | tf_op jit(solution)/shard_map/all_to_all | solution.py:125
  29.6 0.7 fusion.15
  30.3 2.3 %collective-permute-start.1 = (f32[16,128]{1,0:T(8,128)S(1)}, f32[16,128]{1,0:T(8,128)S(1)}, u32[]{:S(2)}, u32[]{:S(2)}) collective-permute-start(f32[16,128]{1,0:T(8,128)S(1)} %get-tuple-element.25), channel_id=1, source_target_pairs={{16,0},{32,16},{48,32},{64,48},{80,64},{96,80},{112,96},{128,112},... | collective-permute-start | bytes 24584 | tf_op jit(solution)/shard_map/ppermute | solution.py:25
  32.6 4.1 %collective-permute-start = (f32[16,128]{1,0:T(8,128)S(1)}, f32[16,128]{1,0:T(8,128)S(1)}, u32[]{:S(2)}, u32[]{:S(2)}) collective-permute-start(f32[16,128]{1,0:T(8,128)S(1)} %get-tuple-element.24), channel_id=1, source_target_pairs={{0,16},{16,32},{32,48},{48,64},{64,80},{80,96},{96,112},{112,128},... | collective-permute-start | bytes 24584 | tf_op jit(solution)/shard_map/ppermute | solution.py:22
  36.8 0.1 reshape.132
  36.8 0.8 gather_fusion
  37.6 0.0 copy-done.3
  37.6 0.1 reshape.131
  37.7 0.0 copy-done
  37.7 0.0 copy-start.4
  37.7 0.0 copy-start.5
  37.7 2.4 %copy.49 = f32[8,6,128,128]{3,2,1,0:T(8,128)} copy(f32[8,6,128,128]{2,3,1,0:T(8,128)S(1)} %bitcast.47) | data formatting | bytes 6291456 | tf_op jit(solution)/shard_map/transpose | solution.py:129
  40.1 0.0 copy-done.4
  40.1 0.1 fusion.12
  40.2 0.0 copy-done.5
  40.2 0.6 compare_select_fusion.1.pick_ref
  40.8 7.2 %all-to-all-done.1.got_ref = f32[64,16,128]{2,1,0:T(8,128)} async-done(((f32[64,16,128]{2,1,0:T(8,128)}), f32[64,16,128]{2,1,0:T(8,128)}, u32[]{:S(2)}, u32[]{:S(2)}) %all-to-all-start.1) | async-done | bytes 524320 | tf_op jit(solution)/shard_map/all_to_all | solution.py:125
  48.0 0.0 copy-start.1
  48.0 3.8 %shard_map.100 = (f32[16,1024]{1,0:T(8,128)}, f32[16,1024]{1,0:T(8,128)}, f32[64,16,128]{2,1,0:T(8,128)}) custom-call(s32[8,6]{1,0:T(8,128)} %compare_select_fusion.1.pick_ref, s32[32,2]{1,0:T(8,128)} %bitcast.50, f32[16,1024]{1,0:T(8,128)} %f_ref.1, f32[16,1024]{1,0:T(8,128)} %p_ref.1, f32[64,16,128]{2,1,0:T(8,128)} %all-to-all-done.1.got_ref, ...), custom_call_target="tpu_custom_call" | custom-call | tf_op jit(solution)/shard_map/pallas_call | solution.py:89
  51.8 5.2 %all-to-all-start.2 = ((f32[64,16,128]{2,1,0:T(8,128)}), f32[64,16,128]{2,1,0:T(8,128)}, u32[]{:S(2)}, u32[]{:S(2)}) async-start(f32[64,16,128]{2,1,0:T(8,128)} %get-tuple-element.13), calls=%async_computation.2 | async-start | bytes 1048576 | tf_op jit(solution)/shard_map/all_to_all | solution.py:125
  57.0 1.9 %convert_reduce_fusion = f32[8,384,128]{2,1,0:T(8,128)} fusion(s32[8,3,128]{2,1,0:T(4,128)S(1)} %copy.50), kind=kLoop, calls=%fused_computation.2 | loop fusion | flops 3145728 | bytes 1585152 | tf_op jit(solution)/shard_map/reduce_sum | solution.py:139
  58.8 0.0 collective-permute-done.1
  58.8 0.0 collective-permute-done
  58.8 0.0 copy-done.1
  59.0 2.5 %fusion = f32[8,2,8,128]{3,2,1,0:T(8,128)S(1)} fusion(f32[8,384,128]{2,1,0:T(8,128)} %convert_reduce_fusion, f32[16,8,128]{2,0,1:T(8,128)S(1)} %copy.61, f32[16,8,128]{2,0,1:T(8,128)S(1)} %copy.60, f32[16,8,128]{2,0,1:T(8,128)S(1)} %copy.59), kind=kOutput, calls=%fused_computation.6 | convolution fusion | flops 75612160 | bytes 1835008 | tf_op jit(solution)/shard_map/tbj,bji->tbi/dot_general | solution.py:142
  61.5 1.9 %collective-permute-start.2 = (f32[1,1024]{1,0:T(1,128)S(1)}, f32[1,1024]{1,0:T(1,128)S(1)}, u32[]{:S(2)}, u32[]{:S(2)}) collective-permute-start(f32[1,1024]{1,0:T(1,128)S(1)} %slice.48), channel_id=1, source_target_pairs={{0,1},{1,2},{2,3},{3,4},{4,5},{5,6},{6,7},{7,8},{8,9},{9,10},{10,1... | collective-permute-start | bytes 12296 | tf_op jit(solution)/shard_map/ppermute | solution.py:33
  63.5 11.5 %all-to-all-done.2.got_ref = f32[64,16,128]{2,1,0:T(8,128)} async-done(((f32[64,16,128]{2,1,0:T(8,128)}), f32[64,16,128]{2,1,0:T(8,128)}, u32[]{:S(2)}, u32[]{:S(2)}) %all-to-all-start.2) | async-done | bytes 524320 | tf_op jit(solution)/shard_map/all_to_all | solution.py:125
  74.9 3.8 %shard_map.101 = (f32[16,1024]{1,0:T(8,128)}, f32[16,1024]{1,0:T(8,128)}, f32[64,16,128]{2,1,0:T(8,128)}) custom-call(s32[8,6]{1,0:T(8,128)} %compare_select_fusion.1.pick_ref, s32[32,2]{1,0:T(8,128)} %bitcast.51, f32[16,1024]{1,0:T(8,128)} %get-tuple-element.11.f_ref, f32[16,1024]{1,0:T(8,128)} %get-tuple-element.12.p_ref, ...), custom_call_target="tpu_custom_call" | custom-call | tf_op jit(solution)/shard_map/pallas_call | solution.py:89
  78.7 0.0 collective-permute-done.2
  78.7 8.5 %all-to-all-start.3 = ((f32[64,16,128]{2,1,0:T(8,128)}), f32[64,16,128]{2,1,0:T(8,128)}, u32[]{:S(2)}, u32[]{:S(2)}) async-start(f32[64,16,128]{2,1,0:T(8,128)} %get-tuple-element.17), calls=%async_computation.3 | async-start | bytes 1048576 | tf_op jit(solution)/shard_map/all_to_all | solution.py:125
  87.2 1.8 %slice_bitcast_fusion = f32[8,5,128,128]{2,3,1,0:T(8,128)} fusion(f32[8,6,128,128]{3,2,1,0:T(8,128)S(1)} %copy-done), kind=kLoop, calls=%fused_computation.4 | loop fusion | bytes 5242880 | tf_op jit(solution)/shard_map/transpose | solution.py:128
  89.1 0.0 copy-start.2
  89.1 3.2 %copy.55 = f32[8,5,128,128]{3,2,1,0:T(8,128)} copy(f32[8,5,128,128]{2,3,1,0:T(8,128)} %slice_bitcast_fusion) | data formatting | bytes 5242880 | tf_op jit(solution)/shard_map/transpose | solution.py:128
  92.3 0.0 copy-done.2
  92.3 0.9 convolution_bitcast_fusion
  93.2 0.6 copy.76
  93.9 0.7 multiply_multiply_fusion
  94.5 8.5 %all-to-all-done.3.got_ref = f32[64,16,128]{2,1,0:T(8,128)} async-done(((f32[64,16,128]{2,1,0:T(8,128)}), f32[64,16,128]{2,1,0:T(8,128)}, u32[]{:S(2)}, u32[]{:S(2)}) %all-to-all-start.3) | async-done | bytes 524320 | tf_op jit(solution)/shard_map/all_to_all | solution.py:125
  103.1 3.3 %shard_map.102 = f32[16,1024]{1,0:T(8,128)} custom-call(s32[8,6]{1,0:T(8,128)} %compare_select_fusion.1.pick_ref, s32[32,2]{1,0:T(8,128)} %bitcast.52, f32[16,1024]{1,0:T(8,128)} %get-tuple-element.8.f_ref, f32[16,1024]{1,0:T(8,128)} %get-tuple-element.15.p_ref, f32[64,16,128]{2,1,0:T(8,128)} %all-to-all-done.3.got_ref, f32[8,640,128]{2,1,0:T(8,128)} %bitcast.48, ...), custom_call_target="tpu_custom_call" | custom-call | tf_op jit(solution)/shard_map/pallas_call | solution.py:89
  (16 shorter events, 0.2 us)
Async XLA Ops:
  2.4 20.5 %all-to-all-start = ((s32[32,1,128]{2,1,0:T(1,128)}), s32[32,1,128]{2,1,0:T(1,128)S(1)}, u32[]{:S(2)}, u32[]{:S(2)}) async-start(s32[32,1,128]{2,1,0:T(1,128)} %broadcast_select_fusion.1), calls=%async_computation | async-start | bytes 32768 | tf_op jit(solution)/shard_map/all_to_all | solution.py:119
  22.9 14.7 %copy-start.3 = (s32[32,1,128]{2,1,0:T(1,128)}, s32[32,1,128]{2,1,0:T(1,128)S(1)}, u32[]{:S(2)}) copy-start(s32[32,1,128]{2,1,0:T(1,128)S(1)} %all-to-all-done) | copy-start | bytes 49156
  24.5 13.3 %copy-start = (f32[8,6,128,128]{3,2,1,0:T(8,128)S(1)}, f32[8,6,128,128]{3,2,1,0:T(8,128)}, u32[]{:S(2)}) copy-start(f32[8,6,128,128]{3,2,1,0:T(8,128)} %param.9) | copy-start | bytes 9437188
  24.5 23.5 %all-to-all-start.1 = ((f32[64,16,128]{2,1,0:T(8,128)}), f32[64,16,128]{2,1,0:T(8,128)}, u32[]{:S(2)}, u32[]{:S(2)}) async-start(f32[64,16,128]{2,1,0:T(8,128)} %gather_fusion.1), calls=%async_computation.1 | async-start | bytes 1048576 | tf_op jit(solution)/shard_map/all_to_all | solution.py:125
  30.3 28.6 %collective-permute-start.1 = (f32[16,128]{1,0:T(8,128)S(1)}, f32[16,128]{1,0:T(8,128)S(1)}, u32[]{:S(2)}, u32[]{:S(2)}) collective-permute-start(f32[16,128]{1,0:T(8,128)S(1)} %get-tuple-element.25), channel_id=1, source_target_pairs={{16,0},{32,16},{48,32},{64,48},{80,64},{96,80},{112,96},{128,112},... | collective-permute-start | bytes 24584 | tf_op jit(solution)/shard_map/ppermute | solution.py:25
  32.6 26.2 %collective-permute-start = (f32[16,128]{1,0:T(8,128)S(1)}, f32[16,128]{1,0:T(8,128)S(1)}, u32[]{:S(2)}, u32[]{:S(2)}) collective-permute-start(f32[16,128]{1,0:T(8,128)S(1)} %get-tuple-element.24), channel_id=1, source_target_pairs={{0,16},{16,32},{32,48},{48,64},{64,80},{80,96},{96,112},{112,128},... | collective-permute-start | bytes 24584 | tf_op jit(solution)/shard_map/ppermute | solution.py:22
  37.7 2.4 %copy-start.4 = (s32[3,1024]{1,0:T(4,128)S(1)}, s32[3,1024]{1,0:T(4,128)}, u32[]{:S(2)}) copy-start(s32[3,1024]{1,0:T(4,128)} %param.11) | copy-start | bytes 36868
  37.7 2.5 %copy-start.5 = (s32[8,6]{1,0:T(8,128)S(1)}, s32[8,6]{1,0:T(8,128)}, u32[]{:S(2)}) copy-start(s32[8,6]{1,0:T(8,128)} %param.10) | copy-start | bytes 580
  48.0 10.9 %copy-start.1 = (f32[16,1024]{1,0:T(8,128)S(1)}, f32[16,1024]{1,0:T(8,128)}, u32[]{:S(2)}) copy-start(f32[16,1024]{1,0:T(8,128)} %param.8) | copy-start | bytes 196612
  51.8 23.1 %all-to-all-start.2 = ((f32[64,16,128]{2,1,0:T(8,128)}), f32[64,16,128]{2,1,0:T(8,128)}, u32[]{:S(2)}, u32[]{:S(2)}) async-start(f32[64,16,128]{2,1,0:T(8,128)} %get-tuple-element.13), calls=%async_computation.2 | async-start | bytes 1048576 | tf_op jit(solution)/shard_map/all_to_all | solution.py:125
  61.5 17.2 %collective-permute-start.2 = (f32[1,1024]{1,0:T(1,128)S(1)}, f32[1,1024]{1,0:T(1,128)S(1)}, u32[]{:S(2)}, u32[]{:S(2)}) collective-permute-start(f32[1,1024]{1,0:T(1,128)S(1)} %slice.48), channel_id=1, source_target_pairs={{0,1},{1,2},{2,3},{3,4},{4,5},{5,6},{6,7},{7,8},{8,9},{9,10},{10,1... | collective-permute-start | bytes 12296 | tf_op jit(solution)/shard_map/ppermute | solution.py:33
  78.7 24.4 %all-to-all-start.3 = ((f32[64,16,128]{2,1,0:T(8,128)}), f32[64,16,128]{2,1,0:T(8,128)}, u32[]{:S(2)}, u32[]{:S(2)}) async-start(f32[64,16,128]{2,1,0:T(8,128)} %get-tuple-element.17), calls=%async_computation.3 | async-start | bytes 1048576 | tf_op jit(solution)/shard_map/all_to_all | solution.py:125
  89.1 3.3 %copy-start.2 = (f32[16,1024]{1,0:T(8,128)S(1)}, f32[16,1024]{1,0:T(8,128)}, u32[]{:S(2)}) copy-start(f32[16,1024]{1,0:T(8,128)} %get-tuple-element.8.f_ref) | copy-start | bytes 196612

commit v14 on v13

--- a/solution.py
+++ b/solution.py
@@ -147,7 +147,12 @@
     moment, field_one, sent = substep(field, momentum, got, tiles, pick, send_ids, 0.5 * step_size, True, True)
     arrived = from_behind(hopped[-1:], "tm", 1)
     got = exchange(sent)
-    moment, field_two, sent = substep(field_one, moment, got, tiles, pick, send_ids, step_size, True, True)
+    local = jnp.einsum(
+        "rij,trj->tri", own_tiles, field_one.reshape(slices, tile_rows, TILE), precision=lax.Precision.HIGHEST
+    ).reshape(slices, site_count)
+    moment, field_two, sent = substep(
+        field_one, moment, got, remote_tiles, pick, send_ids, step_size, True, True, local
+    )
     sent, arrived = lax.optimization_barrier((sent, arrived))
     got = exchange(sent)
     local = jnp.einsum(

time: 107 us -> 116 us (1.084)
  starting transfers between devices: 38.4 us -> 44.7 us
  matrix products: 3.41 us -> 5.16 us
    all_to_all x1, waiting for transfers between devices: 8.43 us -> 0.01 us  [body(): send_ids = lax.all_to_all(request, 'space', 0, 0, tiled=True)[:, :2]]
    all_to_all x3, waiting for transfers between devices: 27.2 us -> 35 us  [exchange(): return lax.all_to_all(sent, 'space', 0, 0, tiled=True)]
    all_to_all x3, starting transfers between devices: 18.8 us -> 25.1 us  [exchange(): return lax.all_to_all(sent, 'space', 0, 0, tiled=True)]
  transfers between devices with their start and end apart: 7 -> 7, of which waited for: 4 -> 3; matrix products, arithmetic and copies ran while one was open for 16% -> 19% of each run, Pallas kernels for 7% -> 6%
where the time goes in v14:
time: 116 us; the launch traced here: 115 us
  starting transfers between devices  44.7 us (39%)
  waiting for transfers between devices  35 us (30%)
  local copies, waits for them, and re-layouts  13 us (11%)
  Pallas kernels  10.5 us (9%)
  other arithmetic  5.83 us (5%)
  matrix products  5.16 us (4%)
    all_to_all x3, waiting for transfers between devices, exchange(): return lax.all_to_all(sent, 'space', 0, 0, tiled=True)  35 us
    all_to_all x3, starting transfers between devices, exchange(): return lax.all_to_all(sent, 'space', 0, 0, tiled=True)  25.1 us
    all_to_all x1, starting transfers between devices, body(): send_ids = lax.all_to_all(request, 'space', 0, 0, tiled=True)[:, :2]  11.2 us
    pallas_call x3, Pallas kernels, substep(): pl.pallas_call(kernel, out_shape=tuple(out_shape), in_specs=[smem, smem,...  10.5 us
    transpose x2, local copies, waits for them, and re-layouts, body(): tiles[:, 1:].transpose(0, 1, 3, 2)  5.07 us
    ppermute x1, starting transfers between devices, with_halo(): lax.ppermute(lax.slice_in_dim(block, block.shape[dim] - width, None, axis...  4.32 us
    dot_general x1, matrix products, body(): jnp.einsum('tbj,bji->tbi', windows, adjacency, precision=lax.Precision.HI...  2.5 us
    transpose x1, local copies, waits for them, and re-layouts, body(): tiles = tiles.transpose(0, 1, 3, 2).reshape(tile_rows, kept * TILE, TILE)  2.36 us
  transfers between devices with their start and end apart: 7, of which 3 were waited for; matrix products, arithmetic and copies ran while one was open for 19% of the time, Pallas kernels for 6%

profile of v14, /device:TPU:1, one launch (start us, length us, event | category | flops | bytes accessed | tf_op | source)
XLA Modules:
  0.0 115.1 jit_solution(17611881210759162442)
XLA Ops:
  0.6 0.0 copy-start
  0.7 0.8 compare_select_fusion
  1.5 0.1 broadcast_in_dim.62
  1.6 0.1 eq.47
  1.7 0.1 select_reduce_fusion
  1.8 0.7 broadcast_select_fusion.1
  2.5 11.2 %all-to-all-start = ((s32[32,1,128]{2,1,0:T(1,128)}), s32[32,1,128]{2,1,0:T(1,128)S(1)}, u32[]{:S(2)}, u32[]{:S(2)}) async-start(s32[32,1,128]{2,1,0:T(1,128)} %broadcast_select_fusion.1), calls=%async_computation | async-start | bytes 32768 | tf_op jit(solution)/shard_map/all_to_all | solution.py:119
  13.8 0.7 fusion.19
  14.5 2.1 %collective-permute-start.1 = (f32[16,128]{1,0:T(8,128)S(1)}, f32[16,128]{1,0:T(8,128)S(1)}, u32[]{:S(2)}, u32[]{:S(2)}) collective-permute-start(f32[16,128]{1,0:T(8,128)S(1)} %get-tuple-element.25), channel_id=1, source_target_pairs={{16,0},{32,16},{48,32},{64,48},{80,64},{96,80},{112,96},{128,112},... | collective-permute-start | bytes 24584 | tf_op jit(solution)/shard_map/ppermute | solution.py:25
  16.6 4.3 %collective-permute-start = (f32[16,128]{1,0:T(8,128)S(1)}, f32[16,128]{1,0:T(8,128)S(1)}, u32[]{:S(2)}, u32[]{:S(2)}) collective-permute-start(f32[16,128]{1,0:T(8,128)S(1)} %get-tuple-element.24), channel_id=1, source_target_pairs={{0,16},{16,32},{32,48},{48,64},{64,80},{80,96},{96,112},{112,128},... | collective-permute-start | bytes 24584 | tf_op jit(solution)/shard_map/ppermute | solution.py:22
  21.0 0.1 reshape.140
  21.0 0.8 copy_bitcast_fusion.2
  21.9 0.8 gather_fusion
  22.7 0.1 reshape.139
  22.8 0.0 copy-done
  22.8 0.0 copy-start.4
  22.8 0.0 copy-start.5
  22.8 2.4 %copy.57 = f32[8,6,128,128]{3,2,1,0:T(8,128)} copy(f32[8,6,128,128]{2,3,1,0:T(8,128)S(1)} %bitcast.62) | data formatting | bytes 6291456 | tf_op jit(solution)/shard_map/transpose | solution.py:129
  25.1 0.0 all-to-all-done
  25.1 0.0 copy-start.2
  25.1 0.1 reshape.148
  25.3 1.4 %gather_fusion.1 = f32[64,16,128]{2,1,0:T(8,128)} fusion(f32[16,8,128]{2,0,1:T(8,128)S(1)} %copy_bitcast_fusion.2, s32[1024]{0:T(1024)S(1)} %pad_clamp_fusion), kind=kCustom, calls=%fused_computation.1 | custom fusion | bytes 1048832 | tf_op jit(solution)/shard_map/jit(_take)/gather | solution.py:145
  26.7 10.9 %all-to-all-start.1 = ((f32[64,16,128]{2,1,0:T(8,128)}), f32[64,16,128]{2,1,0:T(8,128)}, u32[]{:S(2)}, u32[]{:S(2)}) async-start(f32[64,16,128]{2,1,0:T(8,128)} %gather_fusion.1), calls=%async_computation.1 | async-start | bytes 1048576 | tf_op jit(solution)/shard_map/all_to_all | solution.py:125
  37.6 0.0 copy-done.4
  37.6 0.1 fusion.16
  37.7 0.0 copy-done.5
  37.7 0.6 compare_select_fusion.1.pick_ref
  38.3 1.8 %slice_bitcast_fusion = f32[8,5,128,128]{2,3,1,0:T(8,128)} fusion(f32[8,6,128,128]{3,2,1,0:T(8,128)S(1)} %copy-done), kind=kLoop, calls=%fused_computation.4 | loop fusion | bytes 5242880 | tf_op jit(solution)/shard_map/transpose | solution.py:128
  40.1 0.0 copy-done.2
  40.1 15.7 %all-to-all-done.1.got_ref = f32[64,16,128]{2,1,0:T(8,128)} async-done(((f32[64,16,128]{2,1,0:T(8,128)}), f32[64,16,128]{2,1,0:T(8,128)}, u32[]{:S(2)}, u32[]{:S(2)}) %all-to-all-start.1) | async-done | bytes 524320 | tf_op jit(solution)/shard_map/all_to_all | solution.py:125
  55.8 3.8 %shard_map.100 = (f32[16,1024]{1,0:T(8,128)}, f32[16,1024]{1,0:T(8,128)}, f32[64,16,128]{2,1,0:T(8,128)}) custom-call(s32[8,6]{1,0:T(8,128)} %compare_select_fusion.1.pick_ref, s32[32,2]{1,0:T(8,128)} %bitcast.65, f32[16,1024]{1,0:T(8,128)} %f_ref.1, f32[16,1024]{1,0:T(8,128)} %p_ref.1, f32[64,16,128]{2,1,0:T(8,128)} %all-to-all-done.1.got_ref, ...), custom_call_target="tpu_custom_call" | custom-call | tf_op jit(solution)/shard_map/pallas_call | solution.py:89
  59.6 5.2 %all-to-all-start.2 = ((f32[64,16,128]{2,1,0:T(8,128)}), f32[64,16,128]{2,1,0:T(8,128)}, u32[]{:S(2)}, u32[]{:S(2)}) async-start(f32[64,16,128]{2,1,0:T(8,128)} %get-tuple-element.13), calls=%async_computation.2 | async-start | bytes 1048576 | tf_op jit(solution)/shard_map/all_to_all | solution.py:125
  64.7 0.0 copy-start.1
  64.8 1.9 %convert_reduce_fusion = f32[8,384,128]{2,1,0:T(8,128)} fusion(s32[8,3,128]{2,1,0:T(4,128)S(1)} %copy.62), kind=kLoop, calls=%fused_computation.2 | loop fusion | flops 3145728 | bytes 1585152 | tf_op jit(solution)/shard_map/reduce_sum | solution.py:139
  66.6 0.0 copy-start.3
  66.6 3.2 %copy.58 = f32[8,5,128,128]{3,2,1,0:T(8,128)} copy(f32[8,5,128,128]{2,3,1,0:T(8,128)} %slice_bitcast_fusion) | data formatting | bytes 5242880 | tf_op jit(solution)/shard_map/transpose | solution.py:128
  69.9 0.0 collective-permute-done.1
  69.9 0.0 collective-permute-done
  69.9 0.0 copy-done.1
  70.0 2.5 %fusion = f32[8,2,8,128]{3,2,1,0:T(8,128)S(1)} fusion(f32[8,384,128]{2,1,0:T(8,128)} %convert_reduce_fusion, f32[16,8,128]{2,0,1:T(8,128)S(1)} %copy.72, f32[16,8,128]{2,0,1:T(8,128)S(1)} %copy.71, f32[16,8,128]{2,0,1:T(8,128)S(1)} %copy.70), kind=kOutput, calls=%fused_computation.6 | convolution fusion | flops 75612160 | bytes 1835008 | tf_op jit(solution)/shard_map/tbj,bji->tbi/dot_general | solution.py:142
  72.6 1.9 %collective-permute-start.2 = (f32[1,1024]{1,0:T(1,128)S(1)}, f32[1,1024]{1,0:T(1,128)S(1)}, u32[]{:S(2)}, u32[]{:S(2)}) collective-permute-start(f32[1,1024]{1,0:T(1,128)S(1)} %slice.48), channel_id=1, source_target_pairs={{0,1},{1,2},{2,3},{3,4},{4,5},{5,6},{6,7},{7,8},{8,9},{9,10},{10,1... | collective-permute-start | bytes 12296 | tf_op jit(solution)/shard_map/ppermute | solution.py:33
  74.5 0.0 copy-done.3
  74.5 0.9 convolution_bitcast_fusion.1
  75.4 0.6 copy.94
  76.1 6.9 %all-to-all-done.2.got_ref = f32[64,16,128]{2,1,0:T(8,128)} async-done(((f32[64,16,128]{2,1,0:T(8,128)}), f32[64,16,128]{2,1,0:T(8,128)}, u32[]{:S(2)}, u32[]{:S(2)}) %all-to-all-start.2) | async-done | bytes 524320 | tf_op jit(solution)/shard_map/all_to_all | solution.py:125
  83.0 3.5 %shard_map.101 = (f32[16,1024]{1,0:T(8,128)}, f32[16,1024]{1,0:T(8,128)}, f32[64,16,128]{2,1,0:T(8,128)}) custom-call(s32[8,6]{1,0:T(8,128)} %compare_select_fusion.1.pick_ref, s32[32,2]{1,0:T(8,128)} %bitcast.66, f32[16,1024]{1,0:T(8,128)} %get-tuple-element.11.f_ref, f32[16,1024]{1,0:T(8,128)} %get-tuple-element.12.p_ref, ...), custom_call_target="tpu_custom_call" | custom-call | tf_op jit(solution)/shard_map/pallas_call | solution.py:89
  86.5 0.0 collective-permute-done.2
  86.5 9.0 %all-to-all-start.3 = ((f32[64,16,128]{2,1,0:T(8,128)}), f32[64,16,128]{2,1,0:T(8,128)}, u32[]{:S(2)}, u32[]{:S(2)}) async-start(f32[64,16,128]{2,1,0:T(8,128)} %get-tuple-element.17), calls=%async_computation.3 | async-start | bytes 1048576 | tf_op jit(solution)/shard_map/all_to_all | solution.py:125
  95.5 1.8 %convolution_bitcast_fusion = f32[8,2,8,128]{3,2,1,0:T(8,128)S(1)} fusion(f32[8,6,128,128]{3,2,1,0:T(8,128)S(1)} %copy-done, f32[16,1024]{1,0:T(8,128)} %get-tuple-element.8.f_ref), kind=kOutput, calls=%fused_computation.7 | convolution fusion | flops 25165824 | bytes 655360 | tf_op jit(solution)/shard_map/rij,trj->tri/dot_general | solution.py:158
  97.3 0.6 copy.93
  97.9 1.5 %multiply_multiply_fusion = f32[16,1024]{1,0:T(8,128)} fusion(f32[16,1024]{1,0:T(8,128)S(1)} %copy-done.1, f32[15,1024]{1,0:T(8,128)S(1)} %bitcast.68, f32[1,1024]{1,0:T(1,128)S(1)} %broadcast_multiply_fusion, f32[16,1024]{1,0:T(8,128)} %get-tuple-element.8.f_ref), kind=kLoop, calls=%fused_computation.28 | loop fusion | flops 114688 | bytes 262144 | tf_op jit(solution)/shard_map/mul | solution.py:168
  99.4 12.4 %all-to-all-done.3.got_ref = f32[64,16,128]{2,1,0:T(8,128)} async-done(((f32[64,16,128]{2,1,0:T(8,128)}), f32[64,16,128]{2,1,0:T(8,128)}, u32[]{:S(2)}, u32[]{:S(2)}) %all-to-all-start.3) | async-done | bytes 524320 | tf_op jit(solution)/shard_map/all_to_all | solution.py:125
  111.9 3.3 %shard_map.102 = f32[16,1024]{1,0:T(8,128)} custom-call(s32[8,6]{1,0:T(8,128)} %compare_select_fusion.1.pick_ref, s32[32,2]{1,0:T(8,128)} %bitcast.67, f32[16,1024]{1,0:T(8,128)} %get-tuple-element.8.f_ref, f32[16,1024]{1,0:T(8,128)} %get-tuple-element.15.p_ref, f32[64,16,128]{2,1,0:T(8,128)} %all-to-all-done.3.got_ref, f32[8,640,128]{2,1,0:T(8,128)} %bitcast.61, ...), custom_call_target="tpu_custom_call" | custom-call | tf_op jit(solution)/shard_map/pallas_call | solution.py:89
  (16 shorter events, 0.2 us)
Async XLA Ops:
  0.6 22.1 %copy-start = (f32[8,6,128,128]{3,2,1,0:T(8,128)S(1)}, f32[8,6,128,128]{3,2,1,0:T(8,128)}, u32[]{:S(2)}) copy-start(f32[8,6,128,128]{3,2,1,0:T(8,128)} %param.9) | copy-start | bytes 9437188
  2.5 22.6 %all-to-all-start = ((s32[32,1,128]{2,1,0:T(1,128)}), s32[32,1,128]{2,1,0:T(1,128)S(1)}, u32[]{:S(2)}, u32[]{:S(2)}) async-start(s32[32,1,128]{2,1,0:T(1,128)} %broadcast_select_fusion.1), calls=%async_computation | async-start | bytes 32768 | tf_op jit(solution)/shard_map/all_to_all | solution.py:119
  14.5 55.4 %collective-permute-start.1 = (f32[16,128]{1,0:T(8,128)S(1)}, f32[16,128]{1,0:T(8,128)S(1)}, u32[]{:S(2)}, u32[]{:S(2)}) collective-permute-start(f32[16,128]{1,0:T(8,128)S(1)} %get-tuple-element.25), channel_id=1, source_target_pairs={{16,0},{32,16},{48,32},{64,48},{80,64},{96,80},{112,96},{128,112},... | collective-permute-start | bytes 24584 | tf_op jit(solution)/shard_map/ppermute | solution.py:25
  16.6 53.2 %collective-permute-start = (f32[16,128]{1,0:T(8,128)S(1)}, f32[16,128]{1,0:T(8,128)S(1)}, u32[]{:S(2)}, u32[]{:S(2)}) collective-permute-start(f32[16,128]{1,0:T(8,128)S(1)} %get-tuple-element.24), channel_id=1, source_target_pairs={{0,16},{16,32},{32,48},{48,64},{64,80},{80,96},{96,112},{112,128},... | collective-permute-start | bytes 24584 | tf_op jit(solution)/shard_map/ppermute | solution.py:22
  22.8 14.8 %copy-start.4 = (s32[3,1024]{1,0:T(4,128)S(1)}, s32[3,1024]{1,0:T(4,128)}, u32[]{:S(2)}) copy-start(s32[3,1024]{1,0:T(4,128)} %param.11) | copy-start | bytes 36868
  22.8 15.0 %copy-start.5 = (s32[8,6]{1,0:T(8,128)S(1)}, s32[8,6]{1,0:T(8,128)}, u32[]{:S(2)}) copy-start(s32[8,6]{1,0:T(8,128)} %param.10) | copy-start | bytes 580
  25.1 15.0 %copy-start.2 = (s32[32,1,128]{2,1,0:T(1,128)}, s32[32,1,128]{2,1,0:T(1,128)S(1)}, u32[]{:S(2)}) copy-start(s32[32,1,128]{2,1,0:T(1,128)S(1)} %all-to-all-done) | copy-start | bytes 49156
  26.7 29.1 %all-to-all-start.1 = ((f32[64,16,128]{2,1,0:T(8,128)}), f32[64,16,128]{2,1,0:T(8,128)}, u32[]{:S(2)}, u32[]{:S(2)}) async-start(f32[64,16,128]{2,1,0:T(8,128)} %gather_fusion.1), calls=%async_computation.1 | async-start | bytes 1048576 | tf_op jit(solution)/shard_map/all_to_all | solution.py:125
  59.6 23.4 %all-to-all-start.2 = ((f32[64,16,128]{2,1,0:T(8,128)}), f32[64,16,128]{2,1,0:T(8,128)}, u32[]{:S(2)}, u32[]{:S(2)}) async-start(f32[64,16,128]{2,1,0:T(8,128)} %get-tuple-element.13), calls=%async_computation.2 | async-start | bytes 1048576 | tf_op jit(solution)/shard_map/all_to_all | solution.py:125
  64.7 5.1 %copy-start.1 = (f32[16,1024]{1,0:T(8,128)S(1)}, f32[16,1024]{1,0:T(8,128)}, u32[]{:S(2)}) copy-start(f32[16,1024]{1,0:T(8,128)} %param.8) | copy-start | bytes 196612
  66.6 7.9 %copy-start.3 = (f32[16,1024]{1,0:T(8,128)S(1)}, f32[16,1024]{1,0:T(8,128)}, u32[]{:S(2)}) copy-start(f32[16,1024]{1,0:T(8,128)} %get-tuple-element.11.f_ref) | copy-start | bytes 196612
  72.6 13.9 %collective-permute-start.2 = (f32[1,1024]{1,0:T(1,128)S(1)}, f32[1,1024]{1,0:T(1,128)S(1)}, u32[]{:S(2)}, u32[]{:S(2)}) collective-permute-start(f32[1,1024]{1,0:T(1,128)S(1)} %slice.48), channel_id=1, source_target_pairs={{0,1},{1,2},{2,3},{3,4},{4,5},{5,6},{6,7},{7,8},{8,9},{9,10},{10,1... | collective-permute-start | bytes 12296 | tf_op jit(solution)/shard_map/ppermute | solution.py:33
  86.5 25.4 %all-to-all-start.3 = ((f32[64,16,128]{2,1,0:T(8,128)}), f32[64,16,128]{2,1,0:T(8,128)}, u32[]{:S(2)}, u32[]{:S(2)}) async-start(f32[64,16,128]{2,1,0:T(8,128)} %get-tuple-element.17), calls=%async_computation.3 | async-start | bytes 1048576 | tf_op jit(solution)/shard_map/all_to_all | solution.py:125

commit v15 on v14

--- a/solution.py
+++ b/solution.py
@@ -47,8 +47,8 @@
 
 def substep(field, moment, got, tiles, pick, send_ids, scale, advance, send, local=None):
     slices, site_count = field.shape
-    rows = tiles.shape[0]
-    kept = tiles.shape[1] // TILE + (0 if local is None else 1)
+    rows, kept = tiles.shape[0], pick.shape[1]
+    offset = tiles.shape[1] - (kept - 1) * TILE
     slots = send_ids.shape[0] * send_ids.shape[1]
 
     def kernel(pick_ref, sid_ref, f_ref, p_ref, got_ref, tiles_ref, *refs):
@@ -64,7 +64,7 @@
             if local is None:
                 acc = split_dot(jnp.concatenate([f_ref[:, cols]] + pieces, axis=1), tiles_ref[r])
             else:
-                acc = local_ref[:, cols] + split_dot(jnp.concatenate(pieces, axis=1), tiles_ref[r])
+                acc = local_ref[:, cols] + split_dot(jnp.concatenate(pieces, axis=1), tiles_ref[r, offset:, :])
             p_new = p_ref[:, cols] - scale * acc
             p_out[:, cols] = p_new
             if advance:
@@ -151,7 +151,7 @@
         "rij,trj->tri", own_tiles, field_one.reshape(slices, tile_rows, TILE), precision=lax.Precision.HIGHEST
     ).reshape(slices, site_count)
     moment, field_two, sent = substep(
-        field_one, moment, got, remote_tiles, pick, send_ids, step_size, True, True, local
+        field_one, moment, got, tiles, pick, send_ids, step_size, True, True, local
     )
     sent, arrived = lax.optimization_barrier((sent, arrived))
     got = exchange(sent)

time: 116 us -> 107 us (0.922)
  starting transfers between devices: 44.7 us -> 38.3 us
    all_to_all x3, waiting for transfers between devices: 35 us -> 25.7 us  [exchange(): return lax.all_to_all(sent, 'space', 0, 0, tiled=True)]
    all_to_all x1, waiting for transfers between devices: 0.01 us -> 8.43 us  [body(): send_ids = lax.all_to_all(request, 'space', 0, 0, tiled=True)[:, :2]]
    all_to_all x3, starting transfers between devices: 25.1 us -> 18.8 us  [exchange(): return lax.all_to_all(sent, 'space', 0, 0, tiled=True)]
  transfers between devices with their start and end apart: 7 -> 7, of which waited for: 3 -> 4; matrix products, arithmetic and copies ran while one was open for 19% -> 18% of each run, Pallas kernels for 6% -> 7%
where the time goes in v15:
time: 107 us; the launch traced here: 106 us
  starting transfers between devices  38.3 us (36%)
  waiting for transfers between devices  34.1 us (32%)
  local copies, waits for them, and re-layouts  13 us (12%)
  Pallas kernels  10.8 us (10%)
  other arithmetic  4.82 us (5%)
  matrix products  4.32 us (4%)
    all_to_all x3, waiting for transfers between devices, exchange(): return lax.all_to_all(sent, 'space', 0, 0, tiled=True)  25.7 us
    all_to_all x3, starting transfers between devices, exchange(): return lax.all_to_all(sent, 'space', 0, 0, tiled=True)  18.8 us
    all_to_all x1, starting transfers between devices, body(): send_ids = lax.all_to_all(request, 'space', 0, 0, tiled=True)[:, :2]  11.2 us
    pallas_call x3, Pallas kernels, substep(): pl.pallas_call(kernel, out_shape=tuple(out_shape), in_specs=[smem, smem,...  10.8 us
    all_to_all x1, waiting for transfers between devices, body(): send_ids = lax.all_to_all(request, 'space', 0, 0, tiled=True)[:, :2]  8.43 us
    transpose x2, local copies, waits for them, and re-layouts, body(): tiles[:, 1:].transpose(0, 1, 3, 2)  5.07 us
    ppermute x1, starting transfers between devices, with_halo(): lax.ppermute(lax.slice_in_dim(block, block.shape[dim] - width, None, axis...  4.13 us
    dot_general x1, matrix products, body(): jnp.einsum('tbj,bji->tbi', windows, adjacency, precision=lax.Precision.HI...  2.5 us
  transfers between devices with their start and end apart: 7, of which 4 were waited for; matrix products, arithmetic and copies ran while one was open for 18% of the time, Pallas kernels for 7%

profile of v15, /device:TPU:1, one launch (start us, length us, event | category | flops | bytes accessed | tf_op | source)
XLA Modules:
  0.0 106.3 jit_solution(2315701346543861349)
XLA Ops:
  0.6 0.7 compare_select_fusion
  1.3 0.1 broadcast_in_dim.62
  1.4 0.1 eq.47
  1.5 0.1 select_reduce_fusion
  1.6 0.7 broadcast_select_fusion.1
  2.4 11.2 %all-to-all-start = ((s32[32,1,128]{2,1,0:T(1,128)}), s32[32,1,128]{2,1,0:T(1,128)S(1)}, u32[]{:S(2)}, u32[]{:S(2)}) async-start(s32[32,1,128]{2,1,0:T(1,128)} %broadcast_select_fusion.1), calls=%async_computation | async-start | bytes 32768 | tf_op jit(solution)/shard_map/all_to_all | solution.py:119
  13.6 0.8 copy_bitcast_fusion.2
  14.5 8.4 %all-to-all-done = s32[32,1,128]{2,1,0:T(1,128)S(1)} async-done(((s32[32,1,128]{2,1,0:T(1,128)}), s32[32,1,128]{2,1,0:T(1,128)S(1)}, u32[]{:S(2)}, u32[]{:S(2)}) %all-to-all-start) | async-done | bytes 16416 | tf_op jit(solution)/shard_map/all_to_all | solution.py:119
  22.9 0.0 copy-start.3
  22.9 0.1 reshape.148
  23.0 0.0 copy-start
  23.0 1.4 %gather_fusion.1 = f32[64,16,128]{2,1,0:T(8,128)} fusion(f32[16,8,128]{2,0,1:T(8,128)S(1)} %copy_bitcast_fusion.2, s32[1024]{0:T(1024)S(1)} %pad_clamp_fusion), kind=kCustom, calls=%fused_computation.1 | custom fusion | bytes 1048832 | tf_op jit(solution)/shard_map/jit(_take)/gather | solution.py:145
  24.5 4.8 %all-to-all-start.1 = ((f32[64,16,128]{2,1,0:T(8,128)}), f32[64,16,128]{2,1,0:T(8,128)}, u32[]{:S(2)}, u32[]{:S(2)}) async-start(f32[64,16,128]{2,1,0:T(8,128)} %gather_fusion.1), calls=%async_computation.1 | async-start | bytes 1048576 | tf_op jit(solution)/shard_map/all_to_all | solution.py:125
  29.3 0.7 fusion.19
  30.0 2.3 %collective-permute-start.1 = (f32[16,128]{1,0:T(8,128)S(1)}, f32[16,128]{1,0:T(8,128)S(1)}, u32[]{:S(2)}, u32[]{:S(2)}) collective-permute-start(f32[16,128]{1,0:T(8,128)S(1)} %get-tuple-element.25), channel_id=1, source_target_pairs={{16,0},{32,16},{48,32},{64,48},{80,64},{96,80},{112,96},{128,112},... | collective-permute-start | bytes 24584 | tf_op jit(solution)/shard_map/ppermute | solution.py:25
  32.4 4.1 %collective-permute-start = (f32[16,128]{1,0:T(8,128)S(1)}, f32[16,128]{1,0:T(8,128)S(1)}, u32[]{:S(2)}, u32[]{:S(2)}) collective-permute-start(f32[16,128]{1,0:T(8,128)S(1)} %get-tuple-element.24), channel_id=1, source_target_pairs={{0,16},{16,32},{32,48},{48,64},{64,80},{80,96},{96,112},{112,128},... | collective-permute-start | bytes 24584 | tf_op jit(solution)/shard_map/ppermute | solution.py:22
  36.5 0.1 reshape.140
  36.6 0.8 gather_fusion
  37.4 0.0 copy-done.3
  37.4 0.1 reshape.139
  37.4 0.0 copy-done
  37.4 0.0 copy-start.5
  37.5 0.0 copy-start.6
  37.5 2.4 %copy.57 = f32[8,6,128,128]{3,2,1,0:T(8,128)} copy(f32[8,6,128,128]{2,3,1,0:T(8,128)S(1)} %bitcast.62) | data formatting | bytes 6291456 | tf_op jit(solution)/shard_map/transpose | solution.py:129
  39.8 0.0 copy-done.5
  39.8 0.1 fusion.16
  39.9 0.0 copy-done.6
  39.9 0.6 compare_select_fusion.1.pick_ref
  40.5 7.2 %all-to-all-done.1.got_ref = f32[64,16,128]{2,1,0:T(8,128)} async-done(((f32[64,16,128]{2,1,0:T(8,128)}), f32[64,16,128]{2,1,0:T(8,128)}, u32[]{:S(2)}, u32[]{:S(2)}) %all-to-all-start.1) | async-done | bytes 524320 | tf_op jit(solution)/shard_map/all_to_all | solution.py:125
  47.7 0.0 copy-start.1
  47.7 3.8 %shard_map.100 = (f32[16,1024]{1,0:T(8,128)}, f32[16,1024]{1,0:T(8,128)}, f32[64,16,128]{2,1,0:T(8,128)}) custom-call(s32[8,6]{1,0:T(8,128)} %compare_select_fusion.1.pick_ref, s32[32,2]{1,0:T(8,128)} %bitcast.65, f32[16,1024]{1,0:T(8,128)} %f_ref.1, f32[16,1024]{1,0:T(8,128)} %p_ref.1, f32[64,16,128]{2,1,0:T(8,128)} %all-to-all-done.1.got_ref, ...), custom_call_target="tpu_custom_call" | custom-call | tf_op jit(solution)/shard_map/pallas_call | solution.py:89
  51.5 0.0 copy-start.4
  51.5 5.3 %all-to-all-start.2 = ((f32[64,16,128]{2,1,0:T(8,128)}), f32[64,16,128]{2,1,0:T(8,128)}, u32[]{:S(2)}, u32[]{:S(2)}) async-start(f32[64,16,128]{2,1,0:T(8,128)} %get-tuple-element.13), calls=%async_computation.2 | async-start | bytes 1048576 | tf_op jit(solution)/shard_map/all_to_all | solution.py:125
  56.9 1.9 %convert_reduce_fusion = f32[8,384,128]{2,1,0:T(8,128)} fusion(s32[8,3,128]{2,1,0:T(4,128)S(1)} %copy.61), kind=kLoop, calls=%fused_computation.2 | loop fusion | flops 3145728 | bytes 1585152 | tf_op jit(solution)/shard_map/reduce_sum | solution.py:139
  58.7 0.0 collective-permute-done.1
  58.7 0.0 collective-permute-done
  58.7 0.0 copy-done.1
  58.9 2.5 %fusion = f32[8,2,8,128]{3,2,1,0:T(8,128)S(1)} fusion(f32[8,384,128]{2,1,0:T(8,128)} %convert_reduce_fusion, f32[16,8,128]{2,0,1:T(8,128)S(1)} %copy.72, f32[16,8,128]{2,0,1:T(8,128)S(1)} %copy.71, f32[16,8,128]{2,0,1:T(8,128)S(1)} %copy.70), kind=kOutput, calls=%fused_computation.6 | convolution fusion | flops 75612160 | bytes 1835008 | tf_op jit(solution)/shard_map/tbj,bji->tbi/dot_general | solution.py:142
  61.4 1.9 %collective-permute-start.2 = (f32[1,1024]{1,0:T(1,128)S(1)}, f32[1,1024]{1,0:T(1,128)S(1)}, u32[]{:S(2)}, u32[]{:S(2)}) collective-permute-start(f32[1,1024]{1,0:T(1,128)S(1)} %slice.48), channel_id=1, source_target_pairs={{0,1},{1,2},{2,3},{3,4},{4,5},{5,6},{6,7},{7,8},{8,9},{9,10},{10,1... | collective-permute-start | bytes 12296 | tf_op jit(solution)/shard_map/ppermute | solution.py:33
  63.3 0.0 copy-done.4
  63.3 0.9 convolution_bitcast_fusion.1
  64.3 0.6 copy.94
  64.9 9.9 %all-to-all-done.2.got_ref = f32[64,16,128]{2,1,0:T(8,128)} async-done(((f32[64,16,128]{2,1,0:T(8,128)}), f32[64,16,128]{2,1,0:T(8,128)}, u32[]{:S(2)}, u32[]{:S(2)}) %all-to-all-start.2) | async-done | bytes 524320 | tf_op jit(solution)/shard_map/all_to_all | solution.py:125
  74.8 3.7 %shard_map.101 = (f32[16,1024]{1,0:T(8,128)}, f32[16,1024]{1,0:T(8,128)}, f32[64,16,128]{2,1,0:T(8,128)}) custom-call(s32[8,6]{1,0:T(8,128)} %compare_select_fusion.1.pick_ref, s32[32,2]{1,0:T(8,128)} %bitcast.66, f32[16,1024]{1,0:T(8,128)} %get-tuple-element.11.f_ref, f32[16,1024]{1,0:T(8,128)} %get-tuple-element.12.p_ref, ...), custom_call_target="tpu_custom_call" | custom-call | tf_op jit(solution)/shard_map/pallas_call | solution.py:89
  78.5 0.0 collective-permute-done.2
  78.5 8.6 %all-to-all-start.3 = ((f32[64,16,128]{2,1,0:T(8,128)}), f32[64,16,128]{2,1,0:T(8,128)}, u32[]{:S(2)}, u32[]{:S(2)}) async-start(f32[64,16,128]{2,1,0:T(8,128)} %get-tuple-element.17), calls=%async_computation.3 | async-start | bytes 1048576 | tf_op jit(solution)/shard_map/all_to_all | solution.py:125
  87.1 1.8 %slice_bitcast_fusion = f32[8,5,128,128]{2,3,1,0:T(8,128)} fusion(f32[8,6,128,128]{3,2,1,0:T(8,128)S(1)} %copy-done), kind=kLoop, calls=%fused_computation.4 | loop fusion | bytes 5242880 | tf_op jit(solution)/shard_map/transpose | solution.py:128
  88.9 0.0 copy-start.2
  88.9 3.3 %copy.66 = f32[8,5,128,128]{3,2,1,0:T(8,128)} copy(f32[8,5,128,128]{2,3,1,0:T(8,128)} %slice_bitcast_fusion) | data formatting | bytes 5242880 | tf_op jit(solution)/shard_map/transpose | solution.py:128
  92.2 0.0 copy-done.2
  92.2 0.9 convolution_bitcast_fusion
  93.1 0.6 copy.93
  93.7 0.7 multiply_multiply_fusion
  94.4 8.6 %all-to-all-done.3.got_ref = f32[64,16,128]{2,1,0:T(8,128)} async-done(((f32[64,16,128]{2,1,0:T(8,128)}), f32[64,16,128]{2,1,0:T(8,128)}, u32[]{:S(2)}, u32[]{:S(2)}) %all-to-all-start.3) | async-done | bytes 524320 | tf_op jit(solution)/shard_map/all_to_all | solution.py:125
  103.0 3.3 %shard_map.102 = f32[16,1024]{1,0:T(8,128)} custom-call(s32[8,6]{1,0:T(8,128)} %compare_select_fusion.1.pick_ref, s32[32,2]{1,0:T(8,128)} %bitcast.67, f32[16,1024]{1,0:T(8,128)} %get-tuple-element.8.f_ref, f32[16,1024]{1,0:T(8,128)} %get-tuple-element.15.p_ref, f32[64,16,128]{2,1,0:T(8,128)} %all-to-all-done.3.got_ref, f32[8,640,128]{2,1,0:T(8,128)} %bitcast.63, ...), custom_call_target="tpu_custom_call" | custom-call | tf_op jit(solution)/shard_map/pallas_call | solution.py:89
  (16 shorter events, 0.2 us)
Async XLA Ops:
  2.4 20.5 %all-to-all-start = ((s32[32,1,128]{2,1,0:T(1,128)}), s32[32,1,128]{2,1,0:T(1,128)S(1)}, u32[]{:S(2)}, u32[]{:S(2)}) async-start(s32[32,1,128]{2,1,0:T(1,128)} %broadcast_select_fusion.1), calls=%async_computation | async-start | bytes 32768 | tf_op jit(solution)/shard_map/all_to_all | solution.py:119
  22.9 14.5 %copy-start.3 = (s32[32,1,128]{2,1,0:T(1,128)}, s32[32,1,128]{2,1,0:T(1,128)S(1)}, u32[]{:S(2)}) copy-start(s32[32,1,128]{2,1,0:T(1,128)S(1)} %all-to-all-done) | copy-start | bytes 49156
  23.0 14.4 %copy-start = (f32[8,6,128,128]{3,2,1,0:T(8,128)S(1)}, f32[8,6,128,128]{3,2,1,0:T(8,128)}, u32[]{:S(2)}) copy-start(f32[8,6,128,128]{3,2,1,0:T(8,128)} %param.9) | copy-start | bytes 9437188
  24.5 23.3 %all-to-all-start.1 = ((f32[64,16,128]{2,1,0:T(8,128)}), f32[64,16,128]{2,1,0:T(8,128)}, u32[]{:S(2)}, u32[]{:S(2)}) async-start(f32[64,16,128]{2,1,0:T(8,128)} %gather_fusion.1), calls=%async_computation.1 | async-start | bytes 1048576 | tf_op jit(solution)/shard_map/all_to_all | solution.py:125
  30.0 28.7 %collective-permute-start.1 = (f32[16,128]{1,0:T(8,128)S(1)}, f32[16,128]{1,0:T(8,128)S(1)}, u32[]{:S(2)}, u32[]{:S(2)}) collective-permute-start(f32[16,128]{1,0:T(8,128)S(1)} %get-tuple-element.25), channel_id=1, source_target_pairs={{16,0},{32,16},{48,32},{64,48},{80,64},{96,80},{112,96},{128,112},... | collective-permute-start | bytes 24584 | tf_op jit(solution)/shard_map/ppermute | solution.py:25
  32.4 26.4 %collective-permute-start = (f32[16,128]{1,0:T(8,128)S(1)}, f32[16,128]{1,0:T(8,128)S(1)}, u32[]{:S(2)}, u32[]{:S(2)}) collective-permute-start(f32[16,128]{1,0:T(8,128)S(1)} %get-tuple-element.24), channel_id=1, source_target_pairs={{0,16},{16,32},{32,48},{48,64},{64,80},{80,96},{96,112},{112,128},... | collective-permute-start | bytes 24584 | tf_op jit(solution)/shard_map/ppermute | solution.py:22
  37.4 2.4 %copy-start.5 = (s32[3,1024]{1,0:T(4,128)S(1)}, s32[3,1024]{1,0:T(4,128)}, u32[]{:S(2)}) copy-start(s32[3,1024]{1,0:T(4,128)} %param.11) | copy-start | bytes 36868
  37.5 2.5 %copy-start.6 = (s32[8,6]{1,0:T(8,128)S(1)}, s32[8,6]{1,0:T(8,128)}, u32[]{:S(2)}) copy-start(s32[8,6]{1,0:T(8,128)} %param.10) | copy-start | bytes 580
  47.7 11.0 %copy-start.1 = (f32[16,1024]{1,0:T(8,128)S(1)}, f32[16,1024]{1,0:T(8,128)}, u32[]{:S(2)}) copy-start(f32[16,1024]{1,0:T(8,128)} %param.8) | copy-start | bytes 196612
  51.5 11.8 %copy-start.4 = (f32[16,1024]{1,0:T(8,128)S(1)}, f32[16,1024]{1,0:T(8,128)}, u32[]{:S(2)}) copy-start(f32[16,1024]{1,0:T(8,128)} %get-tuple-element.11.f_ref) | copy-start | bytes 196612
  51.5 23.3 %all-to-all-start.2 = ((f32[64,16,128]{2,1,0:T(8,128)}), f32[64,16,128]{2,1,0:T(8,128)}, u32[]{:S(2)}, u32[]{:S(2)}) async-start(f32[64,16,128]{2,1,0:T(8,128)} %get-tuple-element.13), calls=%async_computation.2 | async-start | bytes 1048576 | tf_op jit(solution)/shard_map/all_to_all | solution.py:125
  61.4 17.1 %collective-permute-start.2 = (f32[1,1024]{1,0:T(1,128)S(1)}, f32[1,1024]{1,0:T(1,128)S(1)}, u32[]{:S(2)}, u32[]{:S(2)}) collective-permute-start(f32[1,1024]{1,0:T(1,128)S(1)} %slice.48), channel_id=1, source_target_pairs={{0,1},{1,2},{2,3},{3,4},{4,5},{5,6},{6,7},{7,8},{8,9},{9,10},{10,1... | collective-permute-start | bytes 12296 | tf_op jit(solution)/shard_map/ppermute | solution.py:33
  78.5 24.5 %all-to-all-start.3 = ((f32[64,16,128]{2,1,0:T(8,128)}), f32[64,16,128]{2,1,0:T(8,128)}, u32[]{:S(2)}, u32[]{:S(2)}) async-start(f32[64,16,128]{2,1,0:T(8,128)} %get-tuple-element.17), calls=%async_computation.3 | async-start | bytes 1048576 | tf_op jit(solution)/shard_map/all_to_all | solution.py:125
  88.9 3.3 %copy-start.2 = (f32[16,1024]{1,0:T(8,128)S(1)}, f32[16,1024]{1,0:T(8,128)}, u32[]{:S(2)}) copy-start(f32[16,1024]{1,0:T(8,128)} %get-tuple-element.8.f_ref) | copy-start | bytes 196612

commit v16 on v15

--- a/solution.py
+++ b/solution.py
@@ -144,7 +144,13 @@
     own = field.reshape(slices, tile_rows, TILE)
     first = jnp.take(own, send_ids.reshape(-1), axis=1, mode="clip").transpose(1, 0, 2)
     got = exchange(first)
-    moment, field_one, sent = substep(field, momentum, got, tiles, pick, send_ids, 0.5 * step_size, True, True)
+    held_field, _ = lax.optimization_barrier((field, send_ids))
+    local = jnp.einsum(
+        "rij,trj->tri", own_tiles, held_field.reshape(slices, tile_rows, TILE), precision=lax.Precision.HIGHEST
+    ).reshape(slices, site_count)
+    moment, field_one, sent = substep(
+        field, momentum, got, tiles, pick, send_ids, 0.5 * step_size, True, True, local
+    )
     arrived = from_behind(hopped[-1:], "tm", 1)
     got = exchange(sent)
     local = jnp.einsum(

time: 107 us -> 112 us (1.047)
  starting transfers between devices: 38.3 us -> 43.5 us
  waiting for transfers between devices: 34.1 us -> 32.6 us
    all_to_all x1, waiting for transfers between devices: 8.43 us -> 1.16 us  [body(): send_ids = lax.all_to_all(request, 'space', 0, 0, tiled=True)[:, :2]]
    all_to_all x3, waiting for transfers between devices: 25.7 us -> 31.4 us  [exchange(): return lax.all_to_all(sent, 'space', 0, 0, tiled=True)]
    all_to_all x3, starting transfers between devices: 18.8 us -> 23.9 us  [exchange(): return lax.all_to_all(sent, 'space', 0, 0, tiled=True)]
  transfers between devices with their start and end apart: 7 -> 7, of which waited for: 4 -> 4; matrix products, arithmetic and copies ran while one was open for 18% -> 20% of each run, Pallas kernels for 7% -> 7%
where the time goes in v16:
time: 112 us; the launch traced here: 111 us
  starting transfers between devices  43.5 us (39%)
  waiting for transfers between devices  32.6 us (29%)
  local copies, waits for them, and re-layouts  13.7 us (12%)
  Pallas kernels  10.7 us (10%)
  matrix products  5.22 us (5%)
  other arithmetic  4.83 us (4%)
    all_to_all x3, waiting for transfers between devices, exchange(): return lax.all_to_all(sent, 'space', 0, 0, tiled=True)  31.4 us
    all_to_all x3, starting transfers between devices, exchange(): return lax.all_to_all(sent, 'space', 0, 0, tiled=True)  23.9 us
    all_to_all x1, starting transfers between devices, body(): send_ids = lax.all_to_all(request, 'space', 0, 0, tiled=True)[:, :2]  11.2 us
    pallas_call x3, Pallas kernels, substep(): pl.pallas_call(kernel, out_shape=tuple(out_shape), in_specs=[smem, smem,...  10.7 us
    transpose x2, local copies, waits for them, and re-layouts, body(): tiles[:, 1:].transpose(0, 1, 3, 2)  5.08 us
    ppermute x1, starting transfers between devices, with_halo(): lax.ppermute(lax.slice_in_dim(block, block.shape[dim] - width, None, axis...  4.32 us
    dot_general x1, matrix products, body(): jnp.einsum('tbj,bji->tbi', windows, adjacency, precision=lax.Precision.HI...  2.5 us
    transpose x1, local copies, waits for them, and re-layouts, body(): tiles = tiles.transpose(0, 1, 3, 2).reshape(tile_rows, kept * TILE, TILE)  2.35 us
  transfers between devices with their start and end apart: 7, of which 4 were waited for; matrix products, arithmetic and copies ran while one was open for 20% of the time, Pallas kernels for 7%

profile of v16, /device:TPU:1, one launch (start us, length us, event | category | flops | bytes accessed | tf_op | source)
XLA Modules:
  0.0 111.4 jit_solution(1644825081571642520)
XLA Ops:
  0.6 0.7 compare_select_fusion
  1.3 0.1 broadcast_in_dim.62
  1.4 0.1 eq.47
  1.5 0.1 select_reduce_fusion
  1.6 0.7 broadcast_select_fusion.1
  2.4 11.2 %all-to-all-start = ((s32[32,1,128]{2,1,0:T(1,128)}), s32[32,1,128]{2,1,0:T(1,128)S(1)}, u32[]{:S(2)}, u32[]{:S(2)}) async-start(s32[32,1,128]{2,1,0:T(1,128)} %broadcast_select_fusion.1), calls=%async_computation | async-start | bytes 32768 | tf_op jit(solution)/shard_map/all_to_all | solution.py:119
  13.6 0.7 fusion.23
  14.3 2.1 %collective-permute-start.1 = (f32[16,128]{1,0:T(8,128)S(1)}, f32[16,128]{1,0:T(8,128)S(1)}, u32[]{:S(2)}, u32[]{:S(2)}) collective-permute-start(f32[16,128]{1,0:T(8,128)S(1)} %get-tuple-element.27), channel_id=1, source_target_pairs={{16,0},{32,16},{48,32},{64,48},{80,64},{96,80},{112,96},{128,112},... | collective-permute-start | bytes 24584 | tf_op jit(solution)/shard_map/ppermute | solution.py:25
  16.5 4.3 %collective-permute-start = (f32[16,128]{1,0:T(8,128)S(1)}, f32[16,128]{1,0:T(8,128)S(1)}, u32[]{:S(2)}, u32[]{:S(2)}) collective-permute-start(f32[16,128]{1,0:T(8,128)S(1)} %get-tuple-element.26), channel_id=1, source_target_pairs={{0,16},{16,32},{32,48},{48,64},{64,80},{80,96},{96,112},{112,128},... | collective-permute-start | bytes 24584 | tf_op jit(solution)/shard_map/ppermute | solution.py:22
  20.8 0.8 copy_bitcast_fusion.3
  21.6 0.1 reshape.148
  21.7 1.2 %all-to-all-done = s32[32,1,128]{2,1,0:T(1,128)S(1)} async-done(((s32[32,1,128]{2,1,0:T(1,128)}), s32[32,1,128]{2,1,0:T(1,128)S(1)}, u32[]{:S(2)}, u32[]{:S(2)}) %all-to-all-start) | async-done | bytes 16416 | tf_op jit(solution)/shard_map/all_to_all | solution.py:119
  22.9 0.0 copy-start.4
  22.9 0.1 reshape.156
  23.0 0.0 copy-start
  23.0 1.4 %gather_fusion.1 = f32[64,16,128]{2,1,0:T(8,128)} fusion(f32[16,8,128]{2,0,1:T(8,128)S(1)} %copy_bitcast_fusion.3, s32[1024]{0:T(1024)S(1)} %pad_clamp_fusion), kind=kCustom, calls=%fused_computation.1 | custom fusion | bytes 1048832 | tf_op jit(solution)/shard_map/jit(_take)/gather | solution.py:145
  24.5 9.7 %all-to-all-start.1 = ((f32[64,16,128]{2,1,0:T(8,128)}), f32[64,16,128]{2,1,0:T(8,128)}, u32[]{:S(2)}, u32[]{:S(2)}) async-start(f32[64,16,128]{2,1,0:T(8,128)} %gather_fusion.1), calls=%async_computation.1 | async-start | bytes 1048576 | tf_op jit(solution)/shard_map/all_to_all | solution.py:125
  34.2 0.8 gather_fusion
  35.0 0.0 copy-done.4
  35.0 0.1 reshape.147
  35.1 0.0 copy-done
  35.1 0.0 copy-start.6
  35.1 0.0 copy-start.7
  35.1 0.0 copy-start.2
  35.1 2.3 %copy.65 = f32[8,6,128,128]{3,2,1,0:T(8,128)} copy(f32[8,6,128,128]{2,3,1,0:T(8,128)S(1)} %bitcast.77) | data formatting | bytes 6291456 | tf_op jit(solution)/shard_map/transpose | solution.py:129
  37.4 0.0 copy-done.6
  37.5 0.1 fusion.20
  37.6 0.0 copy-done.7
  37.6 0.6 compare_select_fusion.1.pick_ref
  38.2 0.0 copy-done.2
  38.2 0.9 convolution_bitcast_fusion.2
  39.1 0.7 copy.112
  39.7 12.7 %all-to-all-done.1.got_ref = f32[64,16,128]{2,1,0:T(8,128)} async-done(((f32[64,16,128]{2,1,0:T(8,128)}), f32[64,16,128]{2,1,0:T(8,128)}, u32[]{:S(2)}, u32[]{:S(2)}) %all-to-all-start.1) | async-done | bytes 524320 | tf_op jit(solution)/shard_map/all_to_all | solution.py:125
  52.4 0.0 copy-start.1
  52.4 3.7 %shard_map.100 = (f32[16,1024]{1,0:T(8,128)}, f32[16,1024]{1,0:T(8,128)}, f32[64,16,128]{2,1,0:T(8,128)}) custom-call(s32[8,6]{1,0:T(8,128)} %compare_select_fusion.1.pick_ref, s32[32,2]{1,0:T(8,128)} %bitcast.80, f32[16,1024]{1,0:T(8,128)} %f_ref.1, f32[16,1024]{1,0:T(8,128)} %p_ref.1, f32[64,16,128]{2,1,0:T(8,128)} %all-to-all-done.1.got_ref, ...), custom_call_target="tpu_custom_call" | custom-call | tf_op jit(solution)/shard_map/pallas_call | solution.py:89
  56.1 0.0 copy-start.5
  56.1 5.3 %all-to-all-start.2 = ((f32[64,16,128]{2,1,0:T(8,128)}), f32[64,16,128]{2,1,0:T(8,128)}, u32[]{:S(2)}, u32[]{:S(2)}) async-start(f32[64,16,128]{2,1,0:T(8,128)} %get-tuple-element.15), calls=%async_computation.2 | async-start | bytes 1048576 | tf_op jit(solution)/shard_map/all_to_all | solution.py:125
  61.4 1.9 %convert_reduce_fusion = f32[8,384,128]{2,1,0:T(8,128)} fusion(s32[8,3,128]{2,1,0:T(4,128)S(1)} %copy.71), kind=kLoop, calls=%fused_computation.2 | loop fusion | flops 3145728 | bytes 1585152 | tf_op jit(solution)/shard_map/reduce_sum | solution.py:139
  63.3 0.0 collective-permute-done.1
  63.3 0.0 collective-permute-done
  63.3 0.0 copy-done.1
  63.5 2.5 %fusion = f32[8,2,8,128]{3,2,1,0:T(8,128)S(1)} fusion(f32[8,384,128]{2,1,0:T(8,128)} %convert_reduce_fusion, f32[16,8,128]{2,0,1:T(8,128)S(1)} %copy.82, f32[16,8,128]{2,0,1:T(8,128)S(1)} %copy.81, f32[16,8,128]{2,0,1:T(8,128)S(1)} %copy.80), kind=kOutput, calls=%fused_computation.6 | convolution fusion | flops 75612160 | bytes 1835008 | tf_op jit(solution)/shard_map/tbj,bji->tbi/dot_general | solution.py:142
  66.0 1.9 %collective-permute-start.2 = (f32[1,1024]{1,0:T(1,128)S(1)}, f32[1,1024]{1,0:T(1,128)S(1)}, u32[]{:S(2)}, u32[]{:S(2)}) collective-permute-start(f32[1,1024]{1,0:T(1,128)S(1)} %slice.48), channel_id=1, source_target_pairs={{0,1},{1,2},{2,3},{3,4},{4,5},{5,6},{6,7},{7,8},{8,9},{9,10},{10,1... | collective-permute-start | bytes 12296 | tf_op jit(solution)/shard_map/ppermute | solution.py:33
  67.9 0.0 copy-done.5
  67.9 0.9 convolution_bitcast_fusion.1
  68.8 0.7 copy.111
  69.5 10.2 %all-to-all-done.2.got_ref = f32[64,16,128]{2,1,0:T(8,128)} async-done(((f32[64,16,128]{2,1,0:T(8,128)}), f32[64,16,128]{2,1,0:T(8,128)}, u32[]{:S(2)}, u32[]{:S(2)}) %all-to-all-start.2) | async-done | bytes 524320 | tf_op jit(solution)/shard_map/all_to_all | solution.py:125
  79.7 3.7 %shard_map.101 = (f32[16,1024]{1,0:T(8,128)}, f32[16,1024]{1,0:T(8,128)}, f32[64,16,128]{2,1,0:T(8,128)}) custom-call(s32[8,6]{1,0:T(8,128)} %compare_select_fusion.1.pick_ref, s32[32,2]{1,0:T(8,128)} %bitcast.81, f32[16,1024]{1,0:T(8,128)} %get-tuple-element.13.f_ref, f32[16,1024]{1,0:T(8,128)} %get-tuple-element.14.p_ref, ...), custom_call_target="tpu_custom_call" | custom-call | tf_op jit(solution)/shard_map/pallas_call | solution.py:89
  83.4 0.0 collective-permute-done.2
  83.4 8.8 %all-to-all-start.3 = ((f32[64,16,128]{2,1,0:T(8,128)}), f32[64,16,128]{2,1,0:T(8,128)}, u32[]{:S(2)}, u32[]{:S(2)}) async-start(f32[64,16,128]{2,1,0:T(8,128)} %get-tuple-element.19), calls=%async_computation.3 | async-start | bytes 1048576 | tf_op jit(solution)/shard_map/all_to_all | solution.py:125
  92.2 1.8 %slice_bitcast_fusion = f32[8,5,128,128]{2,3,1,0:T(8,128)} fusion(f32[8,6,128,128]{3,2,1,0:T(8,128)S(1)} %copy-done), kind=kLoop, calls=%fused_computation.4 | loop fusion | bytes 5242880 | tf_op jit(solution)/shard_map/transpose | solution.py:128
  94.0 0.0 copy-start.3
  94.0 3.3 %copy.76 = f32[8,5,128,128]{3,2,1,0:T(8,128)} copy(f32[8,5,128,128]{2,3,1,0:T(8,128)} %slice_bitcast_fusion) | data formatting | bytes 5242880 | tf_op jit(solution)/shard_map/transpose | solution.py:128
  97.3 0.0 copy-done.3
  97.3 0.9 convolution_bitcast_fusion
  98.2 0.6 copy.110
  98.8 0.7 multiply_multiply_fusion
  99.5 8.6 %all-to-all-done.3.got_ref = f32[64,16,128]{2,1,0:T(8,128)} async-done(((f32[64,16,128]{2,1,0:T(8,128)}), f32[64,16,128]{2,1,0:T(8,128)}, u32[]{:S(2)}, u32[]{:S(2)}) %all-to-all-start.3) | async-done | bytes 524320 | tf_op jit(solution)/shard_map/all_to_all | solution.py:125
  108.1 3.3 %shard_map.102 = f32[16,1024]{1,0:T(8,128)} custom-call(s32[8,6]{1,0:T(8,128)} %compare_select_fusion.1.pick_ref, s32[32,2]{1,0:T(8,128)} %bitcast.82, f32[16,1024]{1,0:T(8,128)} %get-tuple-element.9.f_ref, f32[16,1024]{1,0:T(8,128)} %get-tuple-element.17.p_ref, f32[64,16,128]{2,1,0:T(8,128)} %all-to-all-done.3.got_ref, f32[8,640,128]{2,1,0:T(8,128)} %bitcast.78, ...), custom_call_target="tpu_custom_call" | custom-call | tf_op jit(solution)/shard_map/pallas_call | solution.py:89
  (16 shorter events, 0.2 us)
Async XLA Ops:
  2.4 20.5 %all-to-all-start = ((s32[32,1,128]{2,1,0:T(1,128)}), s32[32,1,128]{2,1,0:T(1,128)S(1)}, u32[]{:S(2)}, u32[]{:S(2)}) async-start(s32[32,1,128]{2,1,0:T(1,128)} %broadcast_select_fusion.1), calls=%async_computation | async-start | bytes 32768 | tf_op jit(solution)/shard_map/all_to_all | solution.py:119
  14.3 49.0 %collective-permute-start.1 = (f32[16,128]{1,0:T(8,128)S(1)}, f32[16,128]{1,0:T(8,128)S(1)}, u32[]{:S(2)}, u32[]{:S(2)}) collective-permute-start(f32[16,128]{1,0:T(8,128)S(1)} %get-tuple-element.27), channel_id=1, source_target_pairs={{16,0},{32,16},{48,32},{64,48},{80,64},{96,80},{112,96},{128,112},... | collective-permute-start | bytes 24584 | tf_op jit(solution)/shard_map/ppermute | solution.py:25
  16.5 46.8 %collective-permute-start = (f32[16,128]{1,0:T(8,128)S(1)}, f32[16,128]{1,0:T(8,128)S(1)}, u32[]{:S(2)}, u32[]{:S(2)}) collective-permute-start(f32[16,128]{1,0:T(8,128)S(1)} %get-tuple-element.26), channel_id=1, source_target_pairs={{0,16},{16,32},{32,48},{48,64},{64,80},{80,96},{96,112},{112,128},... | collective-permute-start | bytes 24584 | tf_op jit(solution)/shard_map/ppermute | solution.py:22
  22.9 12.1 %copy-start.4 = (s32[32,1,128]{2,1,0:T(1,128)}, s32[32,1,128]{2,1,0:T(1,128)S(1)}, u32[]{:S(2)}) copy-start(s32[32,1,128]{2,1,0:T(1,128)S(1)} %all-to-all-done) | copy-start | bytes 49156
  23.0 12.1 %copy-start = (f32[8,6,128,128]{3,2,1,0:T(8,128)S(1)}, f32[8,6,128,128]{3,2,1,0:T(8,128)}, u32[]{:S(2)}) copy-start(f32[8,6,128,128]{3,2,1,0:T(8,128)} %param.9) | copy-start | bytes 9437188
  24.5 28.0 %all-to-all-start.1 = ((f32[64,16,128]{2,1,0:T(8,128)}), f32[64,16,128]{2,1,0:T(8,128)}, u32[]{:S(2)}, u32[]{:S(2)}) async-start(f32[64,16,128]{2,1,0:T(8,128)} %gather_fusion.1), calls=%async_computation.1 | async-start | bytes 1048576 | tf_op jit(solution)/shard_map/all_to_all | solution.py:125
  35.1 2.4 %copy-start.6 = (s32[3,1024]{1,0:T(4,128)S(1)}, s32[3,1024]{1,0:T(4,128)}, u32[]{:S(2)}) copy-start(s32[3,1024]{1,0:T(4,128)} %param.11) | copy-start | bytes 36868
  35.1 2.5 %copy-start.7 = (s32[8,6]{1,0:T(8,128)S(1)}, s32[8,6]{1,0:T(8,128)}, u32[]{:S(2)}) copy-start(s32[8,6]{1,0:T(8,128)} %param.10) | copy-start | bytes 580
  35.1 3.1 %copy-start.2 = (f32[16,1024]{1,0:T(8,128)S(1)}, f32[16,1024]{1,0:T(8,128)}, u32[]{:S(2)}) copy-start(f32[16,1024]{1,0:T(8,128)} %f_ref.1) | copy-start | bytes 196612
  52.4 10.9 %copy-start.1 = (f32[16,1024]{1,0:T(8,128)S(1)}, f32[16,1024]{1,0:T(8,128)}, u32[]{:S(2)}) copy-start(f32[16,1024]{1,0:T(8,128)} %param.8) | copy-start | bytes 196612
  56.1 11.8 %copy-start.5 = (f32[16,1024]{1,0:T(8,128)S(1)}, f32[16,1024]{1,0:T(8,128)}, u32[]{:S(2)}) copy-start(f32[16,1024]{1,0:T(8,128)} %get-tuple-element.13.f_ref) | copy-start | bytes 196612
  56.1 23.5 %all-to-all-start.2 = ((f32[64,16,128]{2,1,0:T(8,128)}), f32[64,16,128]{2,1,0:T(8,128)}, u32[]{:S(2)}, u32[]{:S(2)}) async-start(f32[64,16,128]{2,1,0:T(8,128)} %get-tuple-element.15), calls=%async_computation.2 | async-start | bytes 1048576 | tf_op jit(solution)/shard_map/all_to_all | solution.py:125
  66.0 17.4 %collective-permute-start.2 = (f32[1,1024]{1,0:T(1,128)S(1)}, f32[1,1024]{1,0:T(1,128)S(1)}, u32[]{:S(2)}, u32[]{:S(2)}) collective-permute-start(f32[1,1024]{1,0:T(1,128)S(1)} %slice.48), channel_id=1, source_target_pairs={{0,1},{1,2},{2,3},{3,4},{4,5},{5,6},{6,7},{7,8},{8,9},{9,10},{10,1... | collective-permute-start | bytes 12296 | tf_op jit(solution)/shard_map/ppermute | solution.py:33
  83.4 24.7 %all-to-all-start.3 = ((f32[64,16,128]{2,1,0:T(8,128)}), f32[64,16,128]{2,1,0:T(8,128)}, u32[]{:S(2)}, u32[]{:S(2)}) async-start(f32[64,16,128]{2,1,0:T(8,128)} %get-tuple-element.19), calls=%async_computation.3 | async-start | bytes 1048576 | tf_op jit(solution)/shard_map/all_to_all | solution.py:125
  94.0 3.3 %copy-start.3 = (f32[16,1024]{1,0:T(8,128)S(1)}, f32[16,1024]{1,0:T(8,128)}, u32[]{:S(2)}) copy-start(f32[16,1024]{1,0:T(8,128)} %get-tuple-element.9.f_ref) | copy-start | bytes 196612

commit v17 on v13

--- a/solution.py
+++ b/solution.py
@@ -131,7 +131,12 @@
     first_site = me * site_count
     lookup = (neighbours - first_site + TILE) % total_sites
     parity_sign = jnp.where(lax.axis_index("tm") == 0, -1.0, 1.0).astype(jnp.float32)
-    widened = with_halo(solution, (("space", 1),), TILE)
+    own = field.reshape(slices, tile_rows, TILE)
+    first = jnp.take(own, send_ids.reshape(-1), axis=1, mode="clip").transpose(1, 0, 2)
+    got = exchange(first)
+    moment, field_one, sent = substep(field, momentum, got, tiles, pick, send_ids, 0.5 * step_size, True, True)
+    sent, held_solution = lax.optimization_barrier((sent, solution))
+    widened = with_halo(held_solution, (("space", 1),), TILE)
     blocks = site_count // TILE
     starts = (jnp.arange(blocks, dtype=jnp.int32) * TILE)[:, None, None]
     offsets = lookup.reshape(3, blocks, TILE).transpose(1, 0, 2) - starts
@@ -141,10 +146,6 @@
     windows = jnp.concatenate([parts[:, :-2], parts[:, 1:-1], parts[:, 2:]], axis=2)
     beside = jnp.einsum("tbj,bji->tbi", windows, adjacency, precision=lax.Precision.HIGHEST)
     hopped = solution + hop_kappa * beside.reshape(slices, site_count)
-    own = field.reshape(slices, tile_rows, TILE)
-    first = jnp.take(own, send_ids.reshape(-1), axis=1, mode="clip").transpose(1, 0, 2)
-    got = exchange(first)
-    moment, field_one, sent = substep(field, momentum, got, tiles, pick, send_ids, 0.5 * step_size, True, True)
     arrived = from_behind(hopped[-1:], "tm", 1)
     got = exchange(sent)
     moment, field_two, sent = substep(field_one, moment, got, tiles, pick, send_ids, step_size, True, True)

time: 107 us -> 115 us (1.075)
  starting transfers between devices: 38.4 us -> 42.8 us
  waiting for transfers between devices: 35.7 us -> 39.5 us
    ppermute x1, waiting for transfers between devices: 0.01 us -> 6.24 us  [with_halo(): lax.ppermute(lax.slice_in_dim(block, 0, width, axis=dim), axis, backward)]
    all_to_all x3, starting transfers between devices: 18.8 us -> 23.2 us  [exchange(): return lax.all_to_all(sent, 'space', 0, 0, tiled=True)]
    all_to_all x3, waiting for transfers between devices: 27.2 us -> 23.2 us  [exchange(): return lax.all_to_all(sent, 'space', 0, 0, tiled=True)]
    ppermute x1, waiting for transfers between devices: 0.01 us -> 1.64 us  [from_behind(): return lax.ppermute(value, axis, pairs)]
  transfers between devices with their start and end apart: 7 -> 7, of which waited for: 4 -> 5; matrix products, arithmetic and copies ran while one was open for 16% -> 15% of each run, Pallas kernels for 7% -> 3%
where the time goes in v17:
time: 115 us; the launch traced here: 114 us
  starting transfers between devices  42.8 us (37%)
  waiting for transfers between devices  39.5 us (34%)
  local copies, waits for them, and re-layouts  11.7 us (10%)
  Pallas kernels  10.8 us (9%)
  other arithmetic  4.83 us (4%)
  matrix products  3.41 us (3%)
    all_to_all x3, starting transfers between devices, exchange(): return lax.all_to_all(sent, 'space', 0, 0, tiled=True)  23.2 us
    all_to_all x3, waiting for transfers between devices, exchange(): return lax.all_to_all(sent, 'space', 0, 0, tiled=True)  23.2 us
    all_to_all x1, starting transfers between devices, body(): send_ids = lax.all_to_all(request, 'space', 0, 0, tiled=True)[:, :2]  11.2 us
    pallas_call x3, Pallas kernels, substep(): pl.pallas_call(kernel, out_shape=tuple(out_shape), in_specs=[smem, smem,...  10.8 us
    all_to_all x1, waiting for transfers between devices, body(): send_ids = lax.all_to_all(request, 'space', 0, 0, tiled=True)[:, :2]  8.43 us
    ppermute x1, waiting for transfers between devices, with_halo(): lax.ppermute(lax.slice_in_dim(block, 0, width, axis=dim), axis, backward)  6.24 us
    transpose x2, local copies, waits for them, and re-layouts, body(): tiles[:, 1:].transpose(0, 1, 3, 2)  5.07 us
    ppermute x1, starting transfers between devices, with_halo(): lax.ppermute(lax.slice_in_dim(block, block.shape[dim] - width, None, axis...  4.13 us
  transfers between devices with their start and end apart: 7, of which 5 were waited for; matrix products, arithmetic and copies ran while one was open for 15% of the time, Pallas kernels for 3%

profile of v17, /device:TPU:1, one launch (start us, length us, event | category | flops | bytes accessed | tf_op | source)
XLA Modules:
  0.0 113.9 jit_solution(7896076113739807672)
XLA Ops:
  0.6 0.7 compare_select_fusion
  1.3 0.1 broadcast_in_dim.62
  1.4 0.1 eq.47
  1.5 0.1 select_reduce_fusion
  1.6 0.7 broadcast_select_fusion.1
  2.4 11.2 %all-to-all-start = ((s32[32,1,128]{2,1,0:T(1,128)}), s32[32,1,128]{2,1,0:T(1,128)S(1)}, u32[]{:S(2)}, u32[]{:S(2)}) async-start(s32[32,1,128]{2,1,0:T(1,128)} %broadcast_select_fusion.1), calls=%async_computation | async-start | bytes 32768 | tf_op jit(solution)/shard_map/all_to_all | solution.py:119
  13.6 0.8 copy_bitcast_fusion.1
  14.5 8.4 %all-to-all-done = s32[32,1,128]{2,1,0:T(1,128)S(1)} async-done(((s32[32,1,128]{2,1,0:T(1,128)}), s32[32,1,128]{2,1,0:T(1,128)S(1)}, u32[]{:S(2)}, u32[]{:S(2)}) %all-to-all-start) | async-done | bytes 16416 | tf_op jit(solution)/shard_map/all_to_all | solution.py:119
  22.9 0.0 copy-start.3
  22.9 0.1 reshape.140
  23.0 1.4 %gather_fusion.1 = f32[64,16,128]{2,1,0:T(8,128)} fusion(f32[16,8,128]{2,0,1:T(8,128)S(1)} %copy_bitcast_fusion.1, s32[1024]{0:T(1024)S(1)} %pad_clamp_fusion), kind=kCustom, calls=%fused_computation.1 | custom fusion | bytes 1048832 | tf_op jit(solution)/shard_map/jit(_take)/gather | solution.py:135
  24.5 0.0 copy-start
  24.5 5.1 %all-to-all-start.1 = ((f32[64,16,128]{2,1,0:T(8,128)}), f32[64,16,128]{2,1,0:T(8,128)}, u32[]{:S(2)}, u32[]{:S(2)}) async-start(f32[64,16,128]{2,1,0:T(8,128)} %gather_fusion.1), calls=%async_computation.1 | async-start | bytes 1048576 | tf_op jit(solution)/shard_map/all_to_all | solution.py:125
  29.6 0.1 reshape.132
  29.7 0.8 gather_fusion
  30.4 0.0 copy-done.3
  30.4 0.1 reshape.131
  30.5 0.0 copy-done
  30.5 0.0 copy-start.4
  30.5 0.0 copy-start.5
  30.5 2.4 %copy.49 = f32[8,6,128,128]{3,2,1,0:T(8,128)} copy(f32[8,6,128,128]{2,3,1,0:T(8,128)S(1)} %bitcast.47) | data formatting | bytes 6291456 | tf_op jit(solution)/shard_map/transpose | solution.py:129
  32.9 0.0 copy-start.1
  32.9 0.0 copy-done.4
  32.9 0.1 fusion.12
  33.0 0.0 copy-done.5
  33.0 0.6 compare_select_fusion.1.pick_ref
  33.6 14.3 %all-to-all-done.1.got_ref = f32[64,16,128]{2,1,0:T(8,128)} async-done(((f32[64,16,128]{2,1,0:T(8,128)}), f32[64,16,128]{2,1,0:T(8,128)}, u32[]{:S(2)}, u32[]{:S(2)}) %all-to-all-start.1) | async-done | bytes 524320 | tf_op jit(solution)/shard_map/all_to_all | solution.py:125
  47.9 3.8 %shard_map.100 = (f32[16,1024]{1,0:T(8,128)}, f32[16,1024]{1,0:T(8,128)}, f32[64,16,128]{2,1,0:T(8,128)}) custom-call(s32[8,6]{1,0:T(8,128)} %compare_select_fusion.1.pick_ref, s32[32,2]{1,0:T(8,128)} %bitcast.50, f32[16,1024]{1,0:T(8,128)} %f_ref.1, f32[16,1024]{1,0:T(8,128)} %p_ref.1, f32[64,16,128]{2,1,0:T(8,128)} %all-to-all-done.1.got_ref, ...), custom_call_target="tpu_custom_call" | custom-call | tf_op jit(solution)/shard_map/pallas_call | solution.py:89
  51.7 5.2 %all-to-all-start.2 = ((f32[64,16,128]{2,1,0:T(8,128)}), f32[64,16,128]{2,1,0:T(8,128)}, u32[]{:S(2)}, u32[]{:S(2)}) async-start(f32[64,16,128]{2,1,0:T(8,128)} %get-tuple-element.16), calls=%async_computation.2 | async-start | bytes 1048576 | tf_op jit(solution)/shard_map/all_to_all | solution.py:125
  56.9 0.0 copy-done.1
  56.9 2.3 %collective-permute-start.1 = (f32[16,128]{1,0:T(8,128)S(1)}, f32[16,128]{1,0:T(8,128)S(1)}, u32[]{:S(2)}, u32[]{:S(2)}) collective-permute-start(f32[16,128]{1,0:T(8,128)S(1)} %get-tuple-element.29), channel_id=1, source_target_pairs={{16,0},{32,16},{48,32},{64,48},{80,64},{96,80},{112,96},{128,112},... | collective-permute-start | bytes 24584 | tf_op jit(solution)/shard_map/ppermute | solution.py:25
  59.2 4.1 %collective-permute-start = (f32[16,128]{1,0:T(8,128)S(1)}, f32[16,128]{1,0:T(8,128)S(1)}, u32[]{:S(2)}, u32[]{:S(2)}) collective-permute-start(f32[16,128]{1,0:T(8,128)S(1)} %get-tuple-element.28), channel_id=1, source_target_pairs={{0,16},{16,32},{32,48},{48,64},{64,80},{80,96},{96,112},{112,128},... | collective-permute-start | bytes 24584 | tf_op jit(solution)/shard_map/ppermute | solution.py:22
  63.4 1.9 %convert_reduce_fusion = f32[8,384,128]{2,1,0:T(8,128)} fusion(s32[8,3,128]{2,1,0:T(4,128)S(1)} %copy.50), kind=kLoop, calls=%fused_computation.2 | loop fusion | flops 3145728 | bytes 1585152 | tf_op jit(solution)/shard_map/reduce_sum | solution.py:144
  65.2 6.2 %collective-permute-done.1 = f32[16,128]{1,0:T(8,128)S(1)} collective-permute-done((f32[16,128]{1,0:T(8,128)S(1)}, f32[16,128]{1,0:T(8,128)S(1)}, u32[]{:S(2)}, u32[]{:S(2)}) %collective-permute-start.1) | collective-permute-done | bytes 8224 | tf_op jit(solution)/shard_map/ppermute | solution.py:25
  71.5 0.0 collective-permute-done
  71.6 2.5 %fusion = f32[8,2,8,128]{3,2,1,0:T(8,128)S(1)} fusion(f32[8,384,128]{2,1,0:T(8,128)} %convert_reduce_fusion, f32[16,8,128]{2,0,1:T(8,128)S(1)} %copy.61, f32[16,8,128]{2,0,1:T(8,128)S(1)} %copy.60, f32[16,8,128]{2,0,1:T(8,128)S(1)} %copy.59), kind=kOutput, calls=%fused_computation.6 | convolution fusion | flops 75612160 | bytes 1835008 | tf_op jit(solution)/shard_map/tbj,bji->tbi/dot_general | solution.py:147
  74.1 1.9 %collective-permute-start.2 = (f32[1,1024]{1,0:T(1,128)S(1)}, f32[1,1024]{1,0:T(1,128)S(1)}, u32[]{:S(2)}, u32[]{:S(2)}) collective-permute-start(f32[1,1024]{1,0:T(1,128)S(1)} %slice.48), channel_id=1, source_target_pairs={{0,1},{1,2},{2,3},{3,4},{4,5},{5,6},{6,7},{7,8},{8,9},{9,10},{10,1... | collective-permute-start | bytes 12296 | tf_op jit(solution)/shard_map/ppermute | solution.py:33
  76.1 0.0 all-to-all-done.2.got_ref
  76.1 3.8 %shard_map.101 = (f32[16,1024]{1,0:T(8,128)}, f32[16,1024]{1,0:T(8,128)}, f32[64,16,128]{2,1,0:T(8,128)}) custom-call(s32[8,6]{1,0:T(8,128)} %compare_select_fusion.1.pick_ref, s32[32,2]{1,0:T(8,128)} %bitcast.51, f32[16,1024]{1,0:T(8,128)} %get-tuple-element.13.f_ref, f32[16,1024]{1,0:T(8,128)} %get-tuple-element.14.p_ref, ...), custom_call_target="tpu_custom_call" | custom-call | tf_op jit(solution)/shard_map/pallas_call | solution.py:89
  79.9 1.6 %collective-permute-done.2 = f32[1,1024]{1,0:T(1,128)S(1)} collective-permute-done((f32[1,1024]{1,0:T(1,128)S(1)}, f32[1,1024]{1,0:T(1,128)S(1)}, u32[]{:S(2)}, u32[]{:S(2)}) %collective-permute-start.2) | collective-permute-done | bytes 4128 | tf_op jit(solution)/shard_map/ppermute | solution.py:33
  81.5 13.0 %all-to-all-start.3 = ((f32[64,16,128]{2,1,0:T(8,128)}), f32[64,16,128]{2,1,0:T(8,128)}, u32[]{:S(2)}, u32[]{:S(2)}) async-start(f32[64,16,128]{2,1,0:T(8,128)} %get-tuple-element.21), calls=%async_computation.3 | async-start | bytes 1048576 | tf_op jit(solution)/shard_map/all_to_all | solution.py:125
  94.5 1.8 %slice_bitcast_fusion = f32[8,5,128,128]{2,3,1,0:T(8,128)} fusion(f32[8,6,128,128]{3,2,1,0:T(8,128)S(1)} %copy-done), kind=kLoop, calls=%fused_computation.4 | loop fusion | bytes 5242880 | tf_op jit(solution)/shard_map/transpose | solution.py:128
  96.3 0.0 copy-start.2
  96.3 3.2 %copy.55 = f32[8,5,128,128]{3,2,1,0:T(8,128)} copy(f32[8,5,128,128]{2,3,1,0:T(8,128)} %slice_bitcast_fusion) | data formatting | bytes 5242880 | tf_op jit(solution)/shard_map/transpose | solution.py:128
  99.5 0.0 copy-done.2
  99.5 0.9 convolution_bitcast_fusion
  100.5 0.6 copy.76
  101.1 0.7 multiply_multiply_fusion
  101.8 8.9 %all-to-all-done.3.got_ref = f32[64,16,128]{2,1,0:T(8,128)} async-done(((f32[64,16,128]{2,1,0:T(8,128)}), f32[64,16,128]{2,1,0:T(8,128)}, u32[]{:S(2)}, u32[]{:S(2)}) %all-to-all-start.3) | async-done | bytes 524320 | tf_op jit(solution)/shard_map/all_to_all | solution.py:125
  110.7 3.3 %shard_map.102 = f32[16,1024]{1,0:T(8,128)} custom-call(s32[8,6]{1,0:T(8,128)} %compare_select_fusion.1.pick_ref, s32[32,2]{1,0:T(8,128)} %bitcast.52, f32[16,1024]{1,0:T(8,128)} %get-tuple-element.10.f_ref, f32[16,1024]{1,0:T(8,128)} %get-tuple-element.18.p_ref, f32[64,16,128]{2,1,0:T(8,128)} %all-to-all-done.3.got_ref, f32[8,640,128]{2,1,0:T(8,128)} %bitcast.48, ...), custom_call_target="tpu_custom_call" | custom-call | tf_op jit(solution)/shard_map/pallas_call | solution.py:89
  (17 shorter events, 0.2 us)
Async XLA Ops:
  2.4 20.5 %all-to-all-start = ((s32[32,1,128]{2,1,0:T(1,128)}), s32[32,1,128]{2,1,0:T(1,128)S(1)}, u32[]{:S(2)}, u32[]{:S(2)}) async-start(s32[32,1,128]{2,1,0:T(1,128)} %broadcast_select_fusion.1), calls=%async_computation | async-start | bytes 32768 | tf_op jit(solution)/shard_map/all_to_all | solution.py:119
  22.9 7.6 %copy-start.3 = (s32[32,1,128]{2,1,0:T(1,128)}, s32[32,1,128]{2,1,0:T(1,128)S(1)}, u32[]{:S(2)}) copy-start(s32[32,1,128]{2,1,0:T(1,128)S(1)} %all-to-all-done) | copy-start | bytes 49156
  24.5 6.1 %copy-start = (f32[8,6,128,128]{3,2,1,0:T(8,128)S(1)}, f32[8,6,128,128]{3,2,1,0:T(8,128)}, u32[]{:S(2)}) copy-start(f32[8,6,128,128]{3,2,1,0:T(8,128)} %param.9) | copy-start | bytes 9437188
  24.5 23.5 %all-to-all-start.1 = ((f32[64,16,128]{2,1,0:T(8,128)}), f32[64,16,128]{2,1,0:T(8,128)}, u32[]{:S(2)}, u32[]{:S(2)}) async-start(f32[64,16,128]{2,1,0:T(8,128)} %gather_fusion.1), calls=%async_computation.1 | async-start | bytes 1048576 | tf_op jit(solution)/shard_map/all_to_all | solution.py:125
  30.5 2.4 %copy-start.4 = (s32[3,1024]{1,0:T(4,128)S(1)}, s32[3,1024]{1,0:T(4,128)}, u32[]{:S(2)}) copy-start(s32[3,1024]{1,0:T(4,128)} %param.11) | copy-start | bytes 36868
  30.5 2.5 %copy-start.5 = (s32[8,6]{1,0:T(8,128)S(1)}, s32[8,6]{1,0:T(8,128)}, u32[]{:S(2)}) copy-start(s32[8,6]{1,0:T(8,128)} %param.10) | copy-start | bytes 580
  32.9 24.0 %copy-start.1 = (f32[16,1024]{1,0:T(8,128)S(1)}, f32[16,1024]{1,0:T(8,128)}, u32[]{:S(2)}) copy-start(f32[16,1024]{1,0:T(8,128)} %param.8) | copy-start | bytes 196612
  51.7 24.4 %all-to-all-start.2 = ((f32[64,16,128]{2,1,0:T(8,128)}), f32[64,16,128]{2,1,0:T(8,128)}, u32[]{:S(2)}, u32[]{:S(2)}) async-start(f32[64,16,128]{2,1,0:T(8,128)} %get-tuple-element.16), calls=%async_computation.2 | async-start | bytes 1048576 | tf_op jit(solution)/shard_map/all_to_all | solution.py:125
  56.9 14.6 %collective-permute-start.1 = (f32[16,128]{1,0:T(8,128)S(1)}, f32[16,128]{1,0:T(8,128)S(1)}, u32[]{:S(2)}, u32[]{:S(2)}) collective-permute-start(f32[16,128]{1,0:T(8,128)S(1)} %get-tuple-element.29), channel_id=1, source_target_pairs={{16,0},{32,16},{48,32},{64,48},{80,64},{96,80},{112,96},{128,112},... | collective-permute-start | bytes 24584 | tf_op jit(solution)/shard_map/ppermute | solution.py:25
  59.2 12.2 %collective-permute-start = (f32[16,128]{1,0:T(8,128)S(1)}, f32[16,128]{1,0:T(8,128)S(1)}, u32[]{:S(2)}, u32[]{:S(2)}) collective-permute-start(f32[16,128]{1,0:T(8,128)S(1)} %get-tuple-element.28), channel_id=1, source_target_pairs={{0,16},{16,32},{32,48},{48,64},{64,80},{80,96},{96,112},{112,128},... | collective-permute-start | bytes 24584 | tf_op jit(solution)/shard_map/ppermute | solution.py:22
  74.1 7.4 %collective-permute-start.2 = (f32[1,1024]{1,0:T(1,128)S(1)}, f32[1,1024]{1,0:T(1,128)S(1)}, u32[]{:S(2)}, u32[]{:S(2)}) collective-permute-start(f32[1,1024]{1,0:T(1,128)S(1)} %slice.48), channel_id=1, source_target_pairs={{0,1},{1,2},{2,3},{3,4},{4,5},{5,6},{6,7},{7,8},{8,9},{9,10},{10,1... | collective-permute-start | bytes 12296 | tf_op jit(solution)/shard_map/ppermute | solution.py:33
  81.5 29.2 %all-to-all-start.3 = ((f32[64,16,128]{2,1,0:T(8,128)}), f32[64,16,128]{2,1,0:T(8,128)}, u32[]{:S(2)}, u32[]{:S(2)}) async-start(f32[64,16,128]{2,1,0:T(8,128)} %get-tuple-element.21), calls=%async_computation.3 | async-start | bytes 1048576 | tf_op jit(solution)/shard_map/all_to_all | solution.py:125
  96.3 3.3 %copy-start.2 = (f32[16,1024]{1,0:T(8,128)S(1)}, f32[16,1024]{1,0:T(8,128)}, u32[]{:S(2)}) copy-start(f32[16,1024]{1,0:T(8,128)} %get-tuple-element.10.f_ref) | copy-start | bytes 196612

commit v18 on v13

--- a/solution.py
+++ b/solution.py
@@ -39,10 +39,9 @@
     b_hi = b.astype(jnp.bfloat16)
     b_lo = (b - b_hi.astype(jnp.float32)).astype(jnp.bfloat16)
 
-    def part(x, y):
-        return jnp.dot(x, y, preferred_element_type=jnp.float32)
-
-    return part(a_hi, b_hi) + (part(a_hi, b_lo) + part(a_lo, b_hi))
+    left = jnp.concatenate([a_hi, a_hi, a_lo], axis=1)
+    right = jnp.concatenate([b_hi, b_lo, b_hi], axis=0)
+    return jnp.dot(left, right, preferred_element_type=jnp.float32)
 
 
 def substep(field, moment, got, tiles, pick, send_ids, scale, advance, send, local=None):

time: 107 us -> 107 us (level)
  no operation moved by 1% of the time
where the time goes in v18:
time: 107 us; the launch traced here: 106 us
  starting transfers between devices  38.4 us (36%)
  waiting for transfers between devices  35.7 us (33%)
  local copies, waits for them, and re-layouts  12.4 us (12%)
  Pallas kernels  10.8 us (10%)
  other arithmetic  4.83 us (5%)
  matrix products  3.41 us (3%)
    all_to_all x3, waiting for transfers between devices, exchange(): return lax.all_to_all(sent, 'space', 0, 0, tiled=True)  27.2 us
    all_to_all x3, starting transfers between devices, exchange(): return lax.all_to_all(sent, 'space', 0, 0, tiled=True)  18.8 us
    all_to_all x1, starting transfers between devices, body(): send_ids = lax.all_to_all(request, 'space', 0, 0, tiled=True)[:, :2]  11.2 us
    pallas_call x3, Pallas kernels, substep(): pl.pallas_call(kernel, out_shape=tuple(out_shape), in_specs=[smem, smem,...  10.8 us
    all_to_all x1, waiting for transfers between devices, body(): send_ids = lax.all_to_all(request, 'space', 0, 0, tiled=True)[:, :2]  8.43 us
    transpose x2, local copies, waits for them, and re-layouts, body(): tiles[:, 1:].transpose(0, 1, 3, 2)  5.07 us
    ppermute x1, starting transfers between devices, with_halo(): lax.ppermute(lax.slice_in_dim(block, block.shape[dim] - width, None, axis...  4.13 us
    dot_general x1, matrix products, body(): jnp.einsum('tbj,bji->tbi', windows, adjacency, precision=lax.Precision.HI...  2.5 us
  transfers between devices with their start and end apart: 7, of which 4 were waited for; matrix products, arithmetic and copies ran while one was open for 16% of the time, Pallas kernels for 7%

profile of v18, /device:TPU:1, one launch (start us, length us, event | category | flops | bytes accessed | tf_op | source)
XLA Modules:
  0.0 106.3 jit_solution(10652091106166425077)
XLA Ops:
  0.6 0.7 compare_select_fusion
  1.3 0.1 broadcast_in_dim.62
  1.4 0.1 eq.47
  1.5 0.1 select_reduce_fusion
  1.6 0.7 broadcast_select_fusion.1
  2.4 11.2 %all-to-all-start = ((s32[32,1,128]{2,1,0:T(1,128)}), s32[32,1,128]{2,1,0:T(1,128)S(1)}, u32[]{:S(2)}, u32[]{:S(2)}) async-start(s32[32,1,128]{2,1,0:T(1,128)} %broadcast_select_fusion.1), calls=%async_computation | async-start | bytes 32768 | tf_op jit(solution)/shard_map/all_to_all | solution.py:118
  13.6 0.8 copy_bitcast_fusion.1
  14.5 8.4 %all-to-all-done = s32[32,1,128]{2,1,0:T(1,128)S(1)} async-done(((s32[32,1,128]{2,1,0:T(1,128)}), s32[32,1,128]{2,1,0:T(1,128)S(1)}, u32[]{:S(2)}, u32[]{:S(2)}) %all-to-all-start) | async-done | bytes 16416 | tf_op jit(solution)/shard_map/all_to_all | solution.py:118
  22.9 0.0 copy-start.3
  22.9 0.1 reshape.140
  23.0 1.4 %gather_fusion.1 = f32[64,16,128]{2,1,0:T(8,128)} fusion(f32[16,8,128]{2,0,1:T(8,128)S(1)} %copy_bitcast_fusion.1, s32[1024]{0:T(1024)S(1)} %pad_clamp_fusion), kind=kCustom, calls=%fused_computation.1 | custom fusion | bytes 1048832 | tf_op jit(solution)/shard_map/jit(_take)/gather | solution.py:144
  24.5 0.0 copy-start
  24.5 5.1 %all-to-all-start.1 = ((f32[64,16,128]{2,1,0:T(8,128)}), f32[64,16,128]{2,1,0:T(8,128)}, u32[]{:S(2)}, u32[]{:S(2)}) async-start(f32[64,16,128]{2,1,0:T(8,128)} %gather_fusion.1), calls=%async_computation.1 | async-start | bytes 1048576 | tf_op jit(solution)/shard_map/all_to_all | solution.py:124
  29.6 0.7 fusion.15
  30.3 2.3 %collective-permute-start.1 = (f32[16,128]{1,0:T(8,128)S(1)}, f32[16,128]{1,0:T(8,128)S(1)}, u32[]{:S(2)}, u32[]{:S(2)}) collective-permute-start(f32[16,128]{1,0:T(8,128)S(1)} %get-tuple-element.25), channel_id=1, source_target_pairs={{16,0},{32,16},{48,32},{64,48},{80,64},{96,80},{112,96},{128,112},... | collective-permute-start | bytes 24584 | tf_op jit(solution)/shard_map/ppermute | solution.py:25
  32.6 4.1 %collective-permute-start = (f32[16,128]{1,0:T(8,128)S(1)}, f32[16,128]{1,0:T(8,128)S(1)}, u32[]{:S(2)}, u32[]{:S(2)}) collective-permute-start(f32[16,128]{1,0:T(8,128)S(1)} %get-tuple-element.24), channel_id=1, source_target_pairs={{0,16},{16,32},{32,48},{48,64},{64,80},{80,96},{96,112},{112,128},... | collective-permute-start | bytes 24584 | tf_op jit(solution)/shard_map/ppermute | solution.py:22
  36.8 0.1 reshape.132
  36.8 0.8 gather_fusion
  37.6 0.0 copy-done.3
  37.6 0.1 reshape.131
  37.7 0.0 copy-done
  37.7 0.0 copy-start.4
  37.7 0.0 copy-start.5
  37.7 2.4 %copy.49 = f32[8,6,128,128]{3,2,1,0:T(8,128)} copy(f32[8,6,128,128]{2,3,1,0:T(8,128)S(1)} %bitcast.47) | data formatting | bytes 6291456 | tf_op jit(solution)/shard_map/transpose | solution.py:128
  40.1 0.0 copy-done.4
  40.1 0.1 fusion.12
  40.2 0.0 copy-done.5
  40.2 0.6 compare_select_fusion.1.pick_ref
  40.8 7.2 %all-to-all-done.1.got_ref = f32[64,16,128]{2,1,0:T(8,128)} async-done(((f32[64,16,128]{2,1,0:T(8,128)}), f32[64,16,128]{2,1,0:T(8,128)}, u32[]{:S(2)}, u32[]{:S(2)}) %all-to-all-start.1) | async-done | bytes 524320 | tf_op jit(solution)/shard_map/all_to_all | solution.py:124
  48.0 0.0 copy-start.1
  48.0 3.8 %shard_map.100 = (f32[16,1024]{1,0:T(8,128)}, f32[16,1024]{1,0:T(8,128)}, f32[64,16,128]{2,1,0:T(8,128)}) custom-call(s32[8,6]{1,0:T(8,128)} %compare_select_fusion.1.pick_ref, s32[32,2]{1,0:T(8,128)} %bitcast.50, f32[16,1024]{1,0:T(8,128)} %f_ref.1, f32[16,1024]{1,0:T(8,128)} %p_ref.1, f32[64,16,128]{2,1,0:T(8,128)} %all-to-all-done.1.got_ref, ...), custom_call_target="tpu_custom_call" | custom-call | tf_op jit(solution)/shard_map/pallas_call | solution.py:88
  51.8 5.2 %all-to-all-start.2 = ((f32[64,16,128]{2,1,0:T(8,128)}), f32[64,16,128]{2,1,0:T(8,128)}, u32[]{:S(2)}, u32[]{:S(2)}) async-start(f32[64,16,128]{2,1,0:T(8,128)} %get-tuple-element.13), calls=%async_computation.2 | async-start | bytes 1048576 | tf_op jit(solution)/shard_map/all_to_all | solution.py:124
  57.0 1.9 %convert_reduce_fusion = f32[8,384,128]{2,1,0:T(8,128)} fusion(s32[8,3,128]{2,1,0:T(4,128)S(1)} %copy.50), kind=kLoop, calls=%fused_computation.2 | loop fusion | flops 3145728 | bytes 1585152 | tf_op jit(solution)/shard_map/reduce_sum | solution.py:138
  58.8 0.0 collective-permute-done.1
  58.8 0.0 collective-permute-done
  58.8 0.0 copy-done.1
  59.0 2.5 %fusion = f32[8,2,8,128]{3,2,1,0:T(8,128)S(1)} fusion(f32[8,384,128]{2,1,0:T(8,128)} %convert_reduce_fusion, f32[16,8,128]{2,0,1:T(8,128)S(1)} %copy.61, f32[16,8,128]{2,0,1:T(8,128)S(1)} %copy.60, f32[16,8,128]{2,0,1:T(8,128)S(1)} %copy.59), kind=kOutput, calls=%fused_computation.6 | convolution fusion | flops 75612160 | bytes 1835008 | tf_op jit(solution)/shard_map/tbj,bji->tbi/dot_general | solution.py:141
  61.5 1.9 %collective-permute-start.2 = (f32[1,1024]{1,0:T(1,128)S(1)}, f32[1,1024]{1,0:T(1,128)S(1)}, u32[]{:S(2)}, u32[]{:S(2)}) collective-permute-start(f32[1,1024]{1,0:T(1,128)S(1)} %slice.48), channel_id=1, source_target_pairs={{0,1},{1,2},{2,3},{3,4},{4,5},{5,6},{6,7},{7,8},{8,9},{9,10},{10,1... | collective-permute-start | bytes 12296 | tf_op jit(solution)/shard_map/ppermute | solution.py:33
  63.5 11.5 %all-to-all-done.2.got_ref = f32[64,16,128]{2,1,0:T(8,128)} async-done(((f32[64,16,128]{2,1,0:T(8,128)}), f32[64,16,128]{2,1,0:T(8,128)}, u32[]{:S(2)}, u32[]{:S(2)}) %all-to-all-start.2) | async-done | bytes 524320 | tf_op jit(solution)/shard_map/all_to_all | solution.py:124
  74.9 3.8 %shard_map.101 = (f32[16,1024]{1,0:T(8,128)}, f32[16,1024]{1,0:T(8,128)}, f32[64,16,128]{2,1,0:T(8,128)}) custom-call(s32[8,6]{1,0:T(8,128)} %compare_select_fusion.1.pick_ref, s32[32,2]{1,0:T(8,128)} %bitcast.51, f32[16,1024]{1,0:T(8,128)} %get-tuple-element.11.f_ref, f32[16,1024]{1,0:T(8,128)} %get-tuple-element.12.p_ref, ...), custom_call_target="tpu_custom_call" | custom-call | tf_op jit(solution)/shard_map/pallas_call | solution.py:88
  78.7 0.0 collective-permute-done.2
  78.7 8.5 %all-to-all-start.3 = ((f32[64,16,128]{2,1,0:T(8,128)}), f32[64,16,128]{2,1,0:T(8,128)}, u32[]{:S(2)}, u32[]{:S(2)}) async-start(f32[64,16,128]{2,1,0:T(8,128)} %get-tuple-element.17), calls=%async_computation.3 | async-start | bytes 1048576 | tf_op jit(solution)/shard_map/all_to_all | solution.py:124
  87.2 1.8 %slice_bitcast_fusion = f32[8,5,128,128]{2,3,1,0:T(8,128)} fusion(f32[8,6,128,128]{3,2,1,0:T(8,128)S(1)} %copy-done), kind=kLoop, calls=%fused_computation.4 | loop fusion | bytes 5242880 | tf_op jit(solution)/shard_map/transpose | solution.py:127
  89.1 0.0 copy-start.2
  89.1 3.2 %copy.55 = f32[8,5,128,128]{3,2,1,0:T(8,128)} copy(f32[8,5,128,128]{2,3,1,0:T(8,128)} %slice_bitcast_fusion) | data formatting | bytes 5242880 | tf_op jit(solution)/shard_map/transpose | solution.py:127
  92.3 0.0 copy-done.2
  92.3 0.9 convolution_bitcast_fusion
  93.2 0.6 copy.76
  93.9 0.7 multiply_multiply_fusion
  94.5 8.5 %all-to-all-done.3.got_ref = f32[64,16,128]{2,1,0:T(8,128)} async-done(((f32[64,16,128]{2,1,0:T(8,128)}), f32[64,16,128]{2,1,0:T(8,128)}, u32[]{:S(2)}, u32[]{:S(2)}) %all-to-all-start.3) | async-done | bytes 524320 | tf_op jit(solution)/shard_map/all_to_all | solution.py:124
  103.1 3.2 %shard_map.102 = f32[16,1024]{1,0:T(8,128)} custom-call(s32[8,6]{1,0:T(8,128)} %compare_select_fusion.1.pick_ref, s32[32,2]{1,0:T(8,128)} %bitcast.52, f32[16,1024]{1,0:T(8,128)} %get-tuple-element.8.f_ref, f32[16,1024]{1,0:T(8,128)} %get-tuple-element.15.p_ref, f32[64,16,128]{2,1,0:T(8,128)} %all-to-all-done.3.got_ref, f32[8,640,128]{2,1,0:T(8,128)} %bitcast.48, ...), custom_call_target="tpu_custom_call" | custom-call | tf_op jit(solution)/shard_map/pallas_call | solution.py:88
  (16 shorter events, 0.2 us)
Async XLA Ops:
  2.4 20.5 %all-to-all-start = ((s32[32,1,128]{2,1,0:T(1,128)}), s32[32,1,128]{2,1,0:T(1,128)S(1)}, u32[]{:S(2)}, u32[]{:S(2)}) async-start(s32[32,1,128]{2,1,0:T(1,128)} %broadcast_select_fusion.1), calls=%async_computation | async-start | bytes 32768 | tf_op jit(solution)/shard_map/all_to_all | solution.py:118
  22.9 14.7 %copy-start.3 = (s32[32,1,128]{2,1,0:T(1,128)}, s32[32,1,128]{2,1,0:T(1,128)S(1)}, u32[]{:S(2)}) copy-start(s32[32,1,128]{2,1,0:T(1,128)S(1)} %all-to-all-done) | copy-start | bytes 49156
  24.5 13.3 %copy-start = (f32[8,6,128,128]{3,2,1,0:T(8,128)S(1)}, f32[8,6,128,128]{3,2,1,0:T(8,128)}, u32[]{:S(2)}) copy-start(f32[8,6,128,128]{3,2,1,0:T(8,128)} %param.9) | copy-start | bytes 9437188
  24.5 23.5 %all-to-all-start.1 = ((f32[64,16,128]{2,1,0:T(8,128)}), f32[64,16,128]{2,1,0:T(8,128)}, u32[]{:S(2)}, u32[]{:S(2)}) async-start(f32[64,16,128]{2,1,0:T(8,128)} %gather_fusion.1), calls=%async_computation.1 | async-start | bytes 1048576 | tf_op jit(solution)/shard_map/all_to_all | solution.py:124
  30.3 28.5 %collective-permute-start.1 = (f32[16,128]{1,0:T(8,128)S(1)}, f32[16,128]{1,0:T(8,128)S(1)}, u32[]{:S(2)}, u32[]{:S(2)}) collective-permute-start(f32[16,128]{1,0:T(8,128)S(1)} %get-tuple-element.25), channel_id=1, source_target_pairs={{16,0},{32,16},{48,32},{64,48},{80,64},{96,80},{112,96},{128,112},... | collective-permute-start | bytes 24584 | tf_op jit(solution)/shard_map/ppermute | solution.py:25
  32.6 26.2 %collective-permute-start = (f32[16,128]{1,0:T(8,128)S(1)}, f32[16,128]{1,0:T(8,128)S(1)}, u32[]{:S(2)}, u32[]{:S(2)}) collective-permute-start(f32[16,128]{1,0:T(8,128)S(1)} %get-tuple-element.24), channel_id=1, source_target_pairs={{0,16},{16,32},{32,48},{48,64},{64,80},{80,96},{96,112},{112,128},... | collective-permute-start | bytes 24584 | tf_op jit(solution)/shard_map/ppermute | solution.py:22
  37.7 2.4 %copy-start.4 = (s32[3,1024]{1,0:T(4,128)S(1)}, s32[3,1024]{1,0:T(4,128)}, u32[]{:S(2)}) copy-start(s32[3,1024]{1,0:T(4,128)} %param.11) | copy-start | bytes 36868
  37.7 2.5 %copy-start.5 = (s32[8,6]{1,0:T(8,128)S(1)}, s32[8,6]{1,0:T(8,128)}, u32[]{:S(2)}) copy-start(s32[8,6]{1,0:T(8,128)} %param.10) | copy-start | bytes 580
  48.0 10.9 %copy-start.1 = (f32[16,1024]{1,0:T(8,128)S(1)}, f32[16,1024]{1,0:T(8,128)}, u32[]{:S(2)}) copy-start(f32[16,1024]{1,0:T(8,128)} %param.8) | copy-start | bytes 196612
  51.8 23.1 %all-to-all-start.2 = ((f32[64,16,128]{2,1,0:T(8,128)}), f32[64,16,128]{2,1,0:T(8,128)}, u32[]{:S(2)}, u32[]{:S(2)}) async-start(f32[64,16,128]{2,1,0:T(8,128)} %get-tuple-element.13), calls=%async_computation.2 | async-start | bytes 1048576 | tf_op jit(solution)/shard_map/all_to_all | solution.py:124
  61.5 17.2 %collective-permute-start.2 = (f32[1,1024]{1,0:T(1,128)S(1)}, f32[1,1024]{1,0:T(1,128)S(1)}, u32[]{:S(2)}, u32[]{:S(2)}) collective-permute-start(f32[1,1024]{1,0:T(1,128)S(1)} %slice.48), channel_id=1, source_target_pairs={{0,1},{1,2},{2,3},{3,4},{4,5},{5,6},{6,7},{7,8},{8,9},{9,10},{10,1... | collective-permute-start | bytes 12296 | tf_op jit(solution)/shard_map/ppermute | solution.py:33
  78.7 24.4 %all-to-all-start.3 = ((f32[64,16,128]{2,1,0:T(8,128)}), f32[64,16,128]{2,1,0:T(8,128)}, u32[]{:S(2)}, u32[]{:S(2)}) async-start(f32[64,16,128]{2,1,0:T(8,128)} %get-tuple-element.17), calls=%async_computation.3 | async-start | bytes 1048576 | tf_op jit(solution)/shard_map/all_to_all | solution.py:124
  89.1 3.3 %copy-start.2 = (f32[16,1024]{1,0:T(8,128)S(1)}, f32[16,1024]{1,0:T(8,128)}, u32[]{:S(2)}) copy-start(f32[16,1024]{1,0:T(8,128)} %get-tuple-element.8.f_ref) | copy-start | bytes 196612
